TPU v7x, 256 devices: a whole 4x4x8 slice. The times are simulated.
256 devices in a mesh: dp: 32 (over y, z), tensor: 8 (over x, core).
Axes of the slice: x: 4, y: 4, z: 8, core: 2. Of those that a mesh axis runs over, the one named last changes fastest.
Arguments:
- hidden_in: bfloat16 [1024, 8192], P('dp'), may hold values from -40 to 40
- norm_gain: bfloat16 [8192], P('dp'), may hold values from 0.25 to 2.5
- query_weight: bfloat16 [8192, 8192], P('dp', 'tensor'), may hold values from -0.0625 to 0.0625
- key_weight: bfloat16 [8192, 1024], P('dp', 'tensor'), may hold values from -0.0625 to 0.0625
- value_weight: bfloat16 [8192, 1024], P('dp', 'tensor'), may hold values from -0.0625 to 0.0625
- output_weight: bfloat16 [8192, 8192], P('tensor', 'dp'), may hold values from -0.25 to 0.25
- key_value_cache: bfloat16 [1024, 256, 2, 8, 128], P('dp', None, None, 'tensor'), may hold values from -150 to 150, as said below
- cache_lengths: int32 [1024], replicated, may hold values from 2 to 256, as said below
- parent_beam: int32 [1024], replicated, may hold values from 0 to 1023, as said below
- beam_alive: int32 [1024], replicated, may hold values 0 or 1
Outputs:
- attention_out: bfloat16 [1024, 8192], P(None, 'dp')
Inputs may be any that keep to these rules, and one draw needn't show every extreme that they name: `parent_beam`: among the beams of one device, at most 2 have parents that lie on any one device (beam i lies on device i // 32); on every device some device holds exactly 2 of their parents. `cache_lengths`: some beam holds exactly 256 tokens. `key_value_cache`: slots at or past a beam's length hold arbitrary values.
All inputs are finite; a program needn't handle non-finite values.
Results may differ from a plain program's by a relative error of at most 0.012.
Values may be sent and summed in bfloat16 or wider, within the bound.
No kernel may reach another device: no remote copies, remote signals or barrier semaphores. Data moves between devices by JAX's collectives and lax.ppermute only.
A program may use at most 128 MiB of HBM per device.

v0:
```python
import math

import jax
import jax.numpy as jnp
from jax import lax
from jax.sharding import PartitionSpec as P

HEAD_DIM = 128


def rotate(vectors, position):
    half_width = vectors.shape[-1] // 2
    pair_index = jnp.arange(half_width).astype(jnp.float32)
    frequency = jnp.exp(pair_index * (-2.0 * math.log(1000000.0) / vectors.shape[-1]))
    angles = position.astype(jnp.float32)[:, None] * frequency[None, :]
    cosine = jnp.cos(angles)[:, None, :]
    sine_part = jnp.sin(angles)[:, None, :]
    first_half = vectors[..., :half_width]
    second = vectors[..., half_width:]
    return jnp.concatenate(
        [first_half * cosine - second * sine_part, second * cosine + first_half * sine_part],
        axis=-1,
    )


def attend(queries, key_rows, value_rows, key_new, value_new, length_row):
    row_count, head_total, head_width = queries.shape
    groups = key_rows.shape[2]
    length = key_rows.shape[1]
    grouped = queries.reshape(row_count, groups, head_total // groups, head_width)
    score_scale = 1.0 / math.sqrt(head_width)
    cached = (
        jnp.einsum("rkgd,rlkd->rkgl", grouped, key_rows, preferred_element_type=jnp.float32)
        * score_scale
    )
    latest = (
        jnp.einsum("rkgd,rkd->rkg", grouped, key_new, preferred_element_type=jnp.float32)
        * score_scale
    )
    is_valid = (jnp.arange(length, dtype=jnp.int32)[None, :] < length_row[:, None])[
        :, None, None, :
    ]
    cached = jnp.where(is_valid, cached, -jnp.inf)
    highest = jnp.maximum(jnp.max(cached, axis=-1), latest)
    cached_exp = jnp.exp(cached - highest[..., None])
    latest_exp = jnp.exp(latest - highest)
    denominator = jnp.sum(cached_exp, axis=-1) + latest_exp
    cached_weight = (cached_exp / denominator[..., None]).astype(jnp.bfloat16)
    latest_weight = (latest_exp / denominator).astype(jnp.bfloat16)
    mixture = jnp.einsum(
        "rkgl,rlkd->rkgd", cached_weight, value_rows, preferred_element_type=jnp.float32
    )
    mixture = (
        mixture
        + latest_weight.astype(jnp.float32)[..., None]
        * value_new.astype(jnp.float32)[:, :, None, :]
    )
    return mixture.reshape(row_count, head_total * head_width).astype(jnp.bfloat16)


def arrival_ranks(sources):
    ordinal = jnp.arange(sources.shape[-1], dtype=jnp.int32)
    earlier = (sources[..., None, :] == sources[..., :, None]) & (
        ordinal[None, :] < ordinal[:, None]
    )
    return jnp.sum(earlier.astype(jnp.int32), axis=-1)


def body(
    hidden_in,
    norm_gain,
    query_weight,
    key_weight,
    value_weight,
    output_weight,
    key_value_cache,
    cache_lengths,
    parent_beam,
    beam_alive,
):
    device_count = lax.axis_size("dp")
    device_rank = lax.axis_index("dp")
    local_beams = hidden_in.shape[0]
    capacity = max(2, (2 * local_beams + device_count - 1) // device_count)
    hidden_float = hidden_in.astype(jnp.float32)
    inverse = lax.rsqrt(jnp.mean(hidden_float * hidden_float, axis=1) + 1e-06)
    blocked = lax.all_to_all(hidden_in, "dp", split_axis=1, concat_axis=0, tiled=True)
    scaled = (blocked.astype(jnp.float32) * norm_gain.astype(jnp.float32)[None, :]).astype(
        jnp.bfloat16
    )
    query_width = query_weight.shape[1]
    key_width = key_weight.shape[1]
    summed = (
        lax.psum_scatter(
            jnp.concatenate(
                [
                    jnp.dot(scaled, query_weight, preferred_element_type=jnp.float32),
                    jnp.dot(scaled, key_weight, preferred_element_type=jnp.float32),
                    jnp.dot(scaled, value_weight, preferred_element_type=jnp.float32),
                ],
                axis=1,
            ),
            "dp",
            scatter_dimension=0,
            tiled=True,
        )
        * inverse[:, None]
    )
    first_beam = device_rank * local_beams
    my_parent = lax.dynamic_slice_in_dim(parent_beam, first_beam, local_beams)
    my_alive = lax.dynamic_slice_in_dim(beam_alive, first_beam, local_beams)
    position = jnp.take(cache_lengths, my_parent)
    head_count = query_width // HEAD_DIM
    group_count = key_width // HEAD_DIM
    queries = rotate(
        summed[:, :query_width].reshape(local_beams, head_count, HEAD_DIM), position
    ).astype(jnp.bfloat16)
    key_new = rotate(
        summed[:, query_width : query_width + key_width].reshape(
            local_beams, group_count, HEAD_DIM
        ),
        position,
    ).astype(jnp.bfloat16)
    value_new = (
        summed[:, query_width + key_width :]
        .reshape(local_beams, group_count, HEAD_DIM)
        .astype(jnp.bfloat16)
    )
    source = my_parent // local_beams
    target = source * capacity + arrival_ranks(source)
    slot_total = device_count * capacity
    all_parents = parent_beam.reshape(device_count, local_beams)
    all_sources = all_parents // local_beams
    destination = jnp.broadcast_to(
        jnp.arange(device_count, dtype=jnp.int32)[:, None], (device_count, local_beams)
    )
    placed = jnp.where(
        all_sources == device_rank, destination * capacity + arrival_ranks(all_sources), slot_total
    )
    outgoing = (
        jnp.zeros((slot_total,), jnp.int32)
        .at[placed.reshape(-1)]
        .set((all_parents % local_beams).reshape(-1), mode="drop")
    )
    packed = jnp.take(key_value_cache, outgoing, axis=0)
    arrived = lax.all_to_all(
        packed.reshape((device_count, capacity) + key_value_cache.shape[1:]),
        "dp",
        split_axis=0,
        concat_axis=0,
        tiled=True,
    )
    inherited = jnp.take(arrived.reshape((slot_total,) + key_value_cache.shape[1:]), target, axis=0)
    attention = attend(
        queries, inherited[:, :, 0], inherited[:, :, 1], key_new, value_new, position
    )
    attention = jnp.where(my_alive[:, None] > 0, attention, jnp.zeros_like(attention))
    partial_sum = jnp.dot(
        lax.all_gather(attention, "dp", axis=0, tiled=True),
        output_weight,
        preferred_element_type=jnp.float32,
    )
    return lax.psum(partial_sum, "tensor").astype(jnp.bfloat16)


def solution(mesh):
    placed = (
        P("dp", None),
        P("dp"),
        P("dp", "tensor"),
        P("dp", "tensor"),
        P("dp", "tensor"),
        P("tensor", "dp"),
        P("dp", None, None, "tensor", None),
        P(),
        P(),
        P(),
    )
    return jax.shard_map(body, mesh=mesh, in_specs=placed, out_specs=P(None, "dp"), check_vma=False)
```

profile of v0, /device:TPU:1, one launch (start us, length us, event | category | flops | bytes accessed | tf_op | source)
XLA Modules:
  0.0 546.8 jit_solution(13126944515399061592)
XLA Ops:
  6.5 0.0 copy-start
  6.5 2.0 copy.55
  8.5 12.0 %all-to-all-start = ((bf16[32,32,256]{2,0,1:T(8,128)(2,1)}), bf16[32,32,256]{2,0,1:T(8,128)(2,1)S(1)}, u32[]{:S(2)}, u32[]{:S(2)}) async-start(bf16[32,32,256]{2,0,1:T(8,128)(2,1)} %bitcast.55), calls=%async_computation | async-start | bytes 1048576 | tf_op jit(solution)/shard_map/all_to_all | solution.py:87
  20.6 0.8 reshape.348
  21.3 0.8 convert_reduce_fusion
  22.1 0.1 broadcast_add_fusion
  22.2 0.1 add.98
  22.3 0.7 add_select_fusion.1
  23.0 4.3 scatter_custom_fusion
  27.3 20.8 %gather_fusion.1 = bf16[64,256,2,128]{3,2,1,0:T(2,128)(2,1)} fusion(bf16[32,256,2,128]{3,2,1,0:T(2,128)(2,1)} %bitcast.57, s32[1024]{0:T(1024)S(1)} %pad_clamp_fusion.1), kind=kCustom, calls=%fused_computation.1 | custom fusion | bytes 16777472 | tf_op jit(solution)/shard_map/jit(_take)/gather | solution.py:145
  48.2 8.9 %copy.41 = bf16[64,256,2,128]{3,1,2,0:T(8,128)(2,1)} copy(bf16[64,256,2,128]{3,2,1,0:T(2,128)(2,1)} %gather_fusion.1) | data formatting | bytes 16777216 | tf_op jit(solution)/shard_map/jit(_take)/gather | solution.py:145
  57.1 0.1 broadcast_in_dim.106
  57.2 7.5 %broadcast_select_fusion = bf16[32,2,256,2,1,128]{5,2,3,1,4,0:T(8,128)(2,1)} fusion(bf16[32,2,256,2,1,128]{5,2,3,1,4,0:T(8,128)(2,1)} %bitcast.56, pred[32,2]{1,0:T(8,128)(4,1)S(1)} %broadcast_in_dim.106), kind=kLoop, calls=%fused_computation.4 | loop fusion | flops 4194304 | bytes 16777280 | tf_op jit(solution)/shard_map/jit(_take)/select_n | solution.py:145
  64.7 0.0 copy-start.7
  64.7 0.0 copy-start.4
  64.7 0.0 copy-start.5
  64.7 0.0 all-to-all-done
  64.7 9.4 %all-to-all-start.1 = ((bf16[32,2,256,2,1,128]{5,2,3,1,4,0:T(8,128)(2,1)}), bf16[32,2,256,2,1,128]{5,2,3,1,4,0:T(8,128)(2,1)}, u32[]{:S(2)}, u32[]{:S(2)}) async-start(bf16[32,2,256,2,1,128]{5,2,3,1,4,0:T(8,128)(2,1)} %broadcast_select_fusion), calls=%async_computation.1 | async-start | bytes 16777216 | tf_op jit(solution)/shard_map/all_to_all | solution.py:146
  74.1 0.0 reduce-scatter.4.cloned.1.call-start
  74.2 0.0 copy-done.7
  74.2 0.1 fusion.6
  74.3 0.0 copy-done.4
  74.3 0.3 fusion.38
  74.6 0.0 copy-done.5
  74.6 0.3 fusion.37
  74.9 0.0 copy-done
  74.9 0.8 fusion.36
  75.7 2.8 pad_maximum_fusion
  78.5 5.9 %copy.45 = f32[1024,1280]{1,0:T(8,128)} copy(f32[1024,1280]{0,1:T(8,128)} %pad_maximum_fusion) | data formatting | bytes 10485760
  84.4 0.0 copy-start.2
  84.4 0.0 copy-start.3
  84.4 0.0 reduce-scatter.4.cloned.1.call-update
  84.4 0.2 all-gather.2.cloned.1.call-start
  84.6 0.8 compare_select_fusion.6
  85.4 0.0 copy-done.2
  85.4 0.7 gather_fusion
  86.1 0.8 dynamic-slice_compare_fusion
  86.9 0.2 convert_reduce_fusion.1
  87.1 0.0 copy-done.3
  87.1 0.2 multiply_reduce_fusion
  87.3 0.1 iota_compare_fusion
  87.4 0.1 multiply_cosine_fusion.1
  87.6 306.3 %reduce-scatter.4.cloned.1.call-done = f32[32,1280]{1,0:T(8,128)} async-done(((f32[1024,1280]{1,0:T(8,128)}), f32[32,1280]{1,0:T(8,128)}) %reduce-scatter.4.cloned.1.call-update) | async-done | bytes 163856 | tf_op jit(solution)/shard_map/reduce_scatter | solution.py:94
  393.8 1.0 broadcast_multiply_fusion
  394.9 0.1 fusion.25
  395.0 0.1 maximum_bitcast_fusion
  395.1 0.1 subtract_convert_fusion
  395.2 0.2 fusion.19
  395.4 0.0 all-to-all-done.1
  395.5 6.4 %gather_fusion.2 = bf16[32,256,2,128]{3,1,2,0:T(8,128)(2,1)} fusion(bf16[64,256,2,128]{3,1,2,0:T(8,128)(2,1)} %bitcast.4, s32[1024]{0:T(1024)S(1)} %pad_clamp_fusion), kind=kCustom, calls=%fused_computation.2 | custom fusion | bytes 8388736 | tf_op jit(solution)/shard_map/jit(_take)/gather | solution.py:153
  401.9 2.7 bitcast_select_fusion
  404.6 0.0 copy-start.6
  404.6 0.8 fusion.35
  405.3 0.2 fusion.7
  405.6 0.0 copy-start.1
  405.6 0.5 fusion.5
  406.0 0.7 bitcast_select_fusion.1
  406.8 0.0 all-gather.2.cloned.1.call-update
  406.8 76.0 %all-gather.2.cloned.1.call-done = bf16[1024,1024]{1,0:T(8,128)(2,1)} async-done(((bf16[32,1024]{1,0:T(8,128)(2,1)}), bf16[1024,1024]{1,0:T(8,128)(2,1)}) %all-gather.2.cloned.1.call-update) | async-done | bytes 2097168 | tf_op jit(solution)/shard_map/all_gather | solution.py:159
  482.8 0.0 copy-done.6
  482.8 2.3 fusion.39
  485.1 54.9 %all-reduce.1 = bf16[1024,256]{1,0:T(8,128)(2,1)} all-reduce(f32[1024,256]{1,0:T(8,128)S(1)} %fusion.39), channel_id=1, replica_groups=mesh['dp'=32,'tensor'=8] {'tensor'}, use_global_device_ids=true, to_apply=%region_7.8 | all-reduce | flops 262144 | bytes 1572864 | tf_op jit(solution)/shard_map/psum | solution.py:163
  540.0 0.0 copy-done.1
  (19 shorter events, 0.2 us)
Async XLA Ops:
  6.5 68.4 %copy-start = (bf16[256,1024]{1,0:T(8,128)(2,1)S(1)}, bf16[256,1024]{1,0:T(8,128)(2,1)}, u32[]{:S(2)}) copy-start(bf16[256,1024]{1,0:T(8,128)(2,1)} %param.12) | copy-start | bytes 1572868
  8.5 56.2 %all-to-all-start = ((bf16[32,32,256]{2,0,1:T(8,128)(2,1)}), bf16[32,32,256]{2,0,1:T(8,128)(2,1)S(1)}, u32[]{:S(2)}, u32[]{:S(2)}) async-start(bf16[32,32,256]{2,0,1:T(8,128)(2,1)} %bitcast.55), calls=%async_computation | async-start | bytes 1048576 | tf_op jit(solution)/shard_map/all_to_all | solution.py:87
  64.7 9.5 %copy-start.7 = (bf16[256]{0:T(256)(128)(2,1)S(1)}, bf16[256]{0:T(256)(128)(2,1)}, u32[]{:S(2)}) copy-start(bf16[256]{0:T(256)(128)(2,1)} %param.11) | copy-start | bytes 1540
  64.7 9.6 %copy-start.4 = (bf16[256,128]{1,0:T(8,128)(2,1)S(1)}, bf16[256,128]{1,0:T(8,128)(2,1)}, u32[]{:S(2)}) copy-start(bf16[256,128]{1,0:T(8,128)(2,1)} %param.14) | copy-start | bytes 196612
  64.7 9.9 %copy-start.5 = (bf16[256,128]{1,0:T(8,128)(2,1)S(1)}, bf16[256,128]{1,0:T(8,128)(2,1)}, u32[]{:S(2)}) copy-start(bf16[256,128]{1,0:T(8,128)(2,1)} %param.13) | copy-start | bytes 196612
  64.7 330.8 %all-to-all-start.1 = ((bf16[32,2,256,2,1,128]{5,2,3,1,4,0:T(8,128)(2,1)}), bf16[32,2,256,2,1,128]{5,2,3,1,4,0:T(8,128)(2,1)}, u32[]{:S(2)}, u32[]{:S(2)}) async-start(bf16[32,2,256,2,1,128]{5,2,3,1,4,0:T(8,128)(2,1)} %broadcast_select_fusion), calls=%async_computation.1 | async-start | bytes 16777216 | tf_op jit(solution)/shard_map/all_to_all | solution.py:146
  74.1 319.7 %reduce-scatter.4.cloned.1.call-start = ((), (), s32[]{:S(2)}) async-start(), calls=%async_computation.4 | async-start | bytes 5406720 | tf_op jit(solution)/shard_map/reduce_scatter | solution.py:94
  84.4 1.0 copy-start.2
  84.4 2.7 copy-start.3
  84.4 398.4 %all-gather.2.cloned.1.call-start = ((), (), s32[]{:S(2)}) async-start(), calls=%async_computation.3 | async-start | bytes 2162688 | tf_op jit(solution)/shard_map/all_gather | solution.py:159
  404.6 78.2 %copy-start.6 = (bf16[1024,256]{1,0:T(8,128)(2,1)S(1)}, bf16[1024,256]{1,0:T(8,128)(2,1)}, u32[]{:S(2)}) copy-start(bf16[1024,256]{1,0:T(8,128)(2,1)} %param.15) | copy-start | bytes 1572868
  405.6 134.4 %copy-start.1 = (bf16[256,1024]{1,0:T(8,128)(2,1)S(1)}, bf16[256,1024]{1,0:T(8,128)(2,1)}, u32[]{:S(2)}) copy-start(bf16[256,1024]{1,0:T(8,128)(2,1)} %param.12) | copy-start | bytes 1572868
Sparse Core Ops, SparseCore 0:
  84.5 309.2 reduce-scatter.3
  406.9 75.8 all-gather.1
where the time goes:
time: 548 us; the launch traced here: 547 us
  waiting for transfers between devices  382 us (70%)
  blocking collectives  54.9 us (10%)
  local copies, waits for them, and re-layouts  50 us (9%)
  starting transfers between devices  21.7 us (4%)
  other arithmetic  19.1 us (3%)
  between operations  13.7 us (2%)
    reduce_scatter x1, waiting for transfers between devices, body(): lax.psum_scatter(jnp.concatenate([jnp.dot(scaled, query_weight, preferred...  306 us
    all_gather x1, waiting for transfers between devices, body(): lax.all_gather(attention, 'dp', axis=0, tiled=True)  76 us
    psum x1, blocking collectives, body(): return lax.psum(partial_sum, 'tensor').astype(jnp.bfloat16)  54.9 us
    gather x2, local copies, waits for them, and re-layouts, body(): packed = jnp.take(key_value_cache, outgoing, axis=0)  29.7 us
    all_to_all x1, starting transfers between devices, body(): lax.all_to_all(hidden_in, 'dp', split_axis=1, concat_axis=0, tiled=True)  12 us
  transfers between devices with their start and end apart: 4, of which 2 were waited for; matrix products, arithmetic and copies ran while one was open for 11% of the time, Pallas kernels for 0%

commit v1 on v0

v1 whole, which is shorter than its diff:
```python
import functools
import math

import jax
import jax.numpy as jnp
from jax import lax
from jax.experimental import pallas as pl
from jax.experimental.pallas import tpu as pltpu
from jax.sharding import PartitionSpec as P

HEAD_DIM = 128
SLOTS_PER_STEP = 8


def rotate(vectors, position):
    half_width = vectors.shape[-1] // 2
    pair_index = jnp.arange(half_width).astype(jnp.float32)
    frequency = jnp.exp(pair_index * (-2.0 * math.log(1000000.0) / vectors.shape[-1]))
    angles = position.astype(jnp.float32)[:, None] * frequency[None, :]
    cosine = jnp.cos(angles)[:, None, :]
    sine_part = jnp.sin(angles)[:, None, :]
    first_half = vectors[..., :half_width]
    second = vectors[..., half_width:]
    return jnp.concatenate(
        [first_half * cosine - second * sine_part, second * cosine + first_half * sine_part],
        axis=-1,
    )


def arrival_ranks(sources):
    ordinal = jnp.arange(sources.shape[-1], dtype=jnp.int32)
    earlier = (sources[..., None, :] == sources[..., :, None]) & (
        ordinal[None, :] < ordinal[:, None]
    )
    return jnp.sum(earlier.astype(jnp.int32), axis=-1)


def attend_kernel(parent_ref, length_ref, packed_ref, *refs):
    cache_refs = refs[:-1]
    out_ref = refs[-1]
    group = len(cache_refs)
    step = pl.program_id(0)
    head_width = packed_ref.shape[-1]
    head_total = packed_ref.shape[1] - 2
    score_scale = 1.0 / math.sqrt(head_width)
    for g in range(group):
        length = length_ref[step * group + g]
        row = packed_ref[g].astype(jnp.float32)
        queries = row[:head_total].astype(jnp.bfloat16)
        key_new = row[head_total : head_total + 1]
        value_new = row[head_total + 1 : head_total + 2]
        block = cache_refs[g][0]
        keys = block[:, :head_width]
        values = block[:, head_width:]
        cached = (
            lax.dot_general(
                queries, keys, (((1,), (1,)), ((), ())), preferred_element_type=jnp.float32
            )
            * score_scale
        )
        latest = (
            jnp.sum(row[:head_total] * key_new, axis=-1, keepdims=True) * score_scale
        )
        slot = lax.broadcasted_iota(jnp.int32, cached.shape, 1)
        cached = jnp.where(slot < length, cached, -jnp.inf)
        highest = jnp.maximum(jnp.max(cached, axis=-1, keepdims=True), latest)
        cached_exp = jnp.exp(cached - highest)
        latest_exp = jnp.exp(latest - highest)
        denominator = jnp.sum(cached_exp, axis=-1, keepdims=True) + latest_exp
        cached_weight = (cached_exp / denominator).astype(jnp.bfloat16)
        latest_weight = (latest_exp / denominator).astype(jnp.bfloat16)
        mixture = jnp.dot(cached_weight, values, preferred_element_type=jnp.float32)
        mixture = mixture + latest_weight.astype(jnp.float32) * value_new
        out_ref[g] = mixture.astype(out_ref.dtype)


def attend_slots(packed, cache_rows, parents, lengths):
    slot_total, rows, head_width = packed.shape
    head_total = rows - 2
    group = SLOTS_PER_STEP
    cache_len, row_width = cache_rows.shape[1], cache_rows.shape[2]

    def cache_map(g):
        return lambda i, parent_ref, length_ref: (parent_ref[i * group + g], 0, 0)

    grid_spec = pltpu.PrefetchScalarGridSpec(
        num_scalar_prefetch=2,
        grid=(slot_total // group,),
        in_specs=[pl.BlockSpec((group, rows, head_width), lambda i, p, l: (i, 0, 0))]
        + [pl.BlockSpec((1, cache_len, row_width), cache_map(g)) for g in range(group)],
        out_specs=pl.BlockSpec((group, head_total, head_width), lambda i, p, l: (i, 0, 0)),
    )
    return pl.pallas_call(
        attend_kernel,
        grid_spec=grid_spec,
        out_shape=jax.ShapeDtypeStruct((slot_total, head_total, head_width), jnp.bfloat16),
    )(parents, lengths, packed, *([cache_rows] * group))


def body(
    hidden_in,
    norm_gain,
    query_weight,
    key_weight,
    value_weight,
    output_weight,
    key_value_cache,
    cache_lengths,
    parent_beam,
    beam_alive,
):
    device_count = lax.axis_size("dp")
    device_rank = lax.axis_index("dp")
    tensor_count = lax.axis_size("tensor")
    local_beams = hidden_in.shape[0]
    capacity = max(2, (2 * local_beams + device_count - 1) // device_count)
    slot_total = device_count * capacity

    hidden_float = hidden_in.astype(jnp.float32)
    inverse = lax.rsqrt(jnp.mean(hidden_float * hidden_float, axis=1) + 1e-06)
    blocked = lax.all_to_all(hidden_in, "dp", split_axis=1, concat_axis=0, tiled=True)
    scaled = (blocked.astype(jnp.float32) * norm_gain.astype(jnp.float32)[None, :]).astype(
        jnp.bfloat16
    )
    query_width = query_weight.shape[1]
    key_width = key_weight.shape[1]
    proj_width = query_width + 2 * key_width
    partial = jnp.concatenate(
        [
            jnp.dot(scaled, query_weight, preferred_element_type=jnp.float32),
            jnp.dot(scaled, key_weight, preferred_element_type=jnp.float32),
            jnp.dot(scaled, value_weight, preferred_element_type=jnp.float32),
        ],
        axis=1,
    )
    arrived = lax.all_to_all(
        partial.reshape(device_count, local_beams, proj_width), "dp", 0, 0, tiled=True
    )
    summed = jnp.sum(arrived, axis=0) * inverse[:, None]

    first_beam = device_rank * local_beams
    my_parent = lax.dynamic_slice_in_dim(parent_beam, first_beam, local_beams)
    my_alive = lax.dynamic_slice_in_dim(beam_alive, first_beam, local_beams)
    position = jnp.take(cache_lengths, my_parent)
    head_count = query_width // HEAD_DIM
    group_count = key_width // HEAD_DIM
    queries = rotate(
        summed[:, :query_width].reshape(local_beams, head_count, HEAD_DIM), position
    ).astype(jnp.bfloat16)
    key_new = rotate(
        summed[:, query_width : query_width + key_width].reshape(
            local_beams, group_count, HEAD_DIM
        ),
        position,
    ).astype(jnp.bfloat16)
    value_new = (
        summed[:, query_width + key_width :]
        .reshape(local_beams, group_count, HEAD_DIM)
        .astype(jnp.bfloat16)
    )
    packed = jnp.concatenate([queries, key_new, value_new], axis=1)
    rows = packed.shape[1]

    source = my_parent // local_beams
    target = source * capacity + arrival_ranks(source)
    slot_of = jnp.arange(slot_total, dtype=jnp.int32)
    match = target[None, :] == slot_of[:, None]
    filled = jnp.any(match, axis=1)
    sender = jnp.argmax(match, axis=1)
    outgoing = jnp.where(
        filled[:, None, None], jnp.take(packed, sender, axis=0), jnp.zeros_like(packed[:1])
    )
    incoming = lax.all_to_all(
        outgoing.reshape(device_count, capacity, rows, HEAD_DIM), "dp", 0, 0, tiled=True
    ).reshape(slot_total, rows, HEAD_DIM)

    all_parents = parent_beam.reshape(device_count, local_beams)
    all_sources = all_parents // local_beams
    destination = jnp.broadcast_to(
        jnp.arange(device_count, dtype=jnp.int32)[:, None], (device_count, local_beams)
    )
    placed = jnp.where(
        all_sources == device_rank, destination * capacity + arrival_ranks(all_sources), slot_total
    )
    local_parent = (
        jnp.zeros((slot_total,), jnp.int32)
        .at[placed.reshape(-1)]
        .set((all_parents % local_beams).reshape(-1), mode="drop")
    )
    slot_length = jnp.take(cache_lengths, first_beam + local_parent)

    cache_rows = key_value_cache.reshape(
        local_beams, key_value_cache.shape[1], 2 * key_value_cache.shape[-1]
    )
    mixed = attend_slots(incoming, cache_rows, local_parent, slot_length)
    returned = lax.all_to_all(
        mixed.reshape(device_count, capacity, head_count * HEAD_DIM), "dp", 0, 0, tiled=True
    ).reshape(slot_total, head_count * HEAD_DIM)
    attention = jnp.take(returned, target, axis=0)
    attention = jnp.where(my_alive[:, None] > 0, attention, jnp.zeros_like(attention))

    spread = jnp.broadcast_to(attention[None], (device_count,) + attention.shape)
    gathered = lax.all_to_all(spread, "dp", 0, 0, tiled=True).reshape(
        device_count * local_beams, head_count * HEAD_DIM
    )
    partial_sum = jnp.dot(gathered, output_weight, preferred_element_type=jnp.float32)
    total_rows, out_width = partial_sum.shape
    reduced = jnp.sum(
        lax.all_to_all(
            partial_sum.reshape(tensor_count, total_rows // tensor_count, out_width),
            "tensor",
            0,
            0,
            tiled=True,
        ),
        axis=0,
    ).astype(jnp.bfloat16)
    copies = jnp.broadcast_to(reduced[None], (tensor_count,) + reduced.shape)
    return lax.all_to_all(copies, "tensor", 0, 0, tiled=True).reshape(total_rows, out_width)


def solution(mesh):
    placed = (
        P("dp", None),
        P("dp"),
        P("dp", "tensor"),
        P("dp", "tensor"),
        P("dp", "tensor"),
        P("tensor", "dp"),
        P("dp", None, None, "tensor", None),
        P(),
        P(),
        P(),
    )
    return jax.shard_map(body, mesh=mesh, in_specs=placed, out_specs=P(None, "dp"), check_vma=False)
```

time: 548 us -> 322 us (0.59)
  waiting for transfers between devices: 382 us -> 132 us
  blocking collectives: 54.9 us -> 87.4 us
  Pallas kernels: 0 us -> 24.3 us
  local copies, waits for them, and re-layouts: 50 us -> 27.3 us
  starting transfers between devices: 21.7 us -> 37.2 us
  between operations: 13.7 us -> 0.36 us
  other arithmetic: 19.1 us -> 10.9 us
    reduce_scatter x1 -> x0, waiting for transfers between devices: 306 us -> none  [body(): lax.psum_scatter(jnp.concatenate([jnp.dot(scaled, query_weight, preferred...]
    all_to_all x1 -> x3, waiting for transfers between devices: 0.01 us -> 118 us  [the longest x1 109 us: body(): lax.all_to_all(partial.reshape(device_count, local_beams, proj_width), 'd...]
    all_to_all x0 -> x3, blocking collectives: none -> 87.4 us  [the longest x1 47.6 us: body(): lax.all_to_all(spread, 'dp', 0, 0, tiled=True)]
    all_gather x1 -> x0, waiting for transfers between devices: 76 us -> none  [body(): lax.all_gather(attention, 'dp', axis=0, tiled=True)]
    psum x1 -> x0, blocking collectives: 54.9 us -> none  [body(): return lax.psum(partial_sum, 'tensor').astype(jnp.bfloat16)]
    gather x3 -> x4, local copies, waits for them, and re-layouts: 36.2 us -> 2.04 us  [the longest x1 0.73 us: body(): slot_length = jnp.take(cache_lengths, first_beam + local_parent)]
    pallas_call x0 -> x1, Pallas kernels: none -> 24.3 us  [attend_slots(): pl.pallas_call(attend_kernel, grid_spec=grid_spec, out_shape=jax.ShapeDty...]
    all_to_all x1 -> x3, starting transfers between devices: 9.42 us -> 25.2 us  [the longest x1 8.85 us: body(): lax.all_to_all(outgoing.reshape(device_count, capacity, rows, HEAD_DIM),...]
  transfers between devices with their start and end apart: 4 -> 4, of which waited for: 2 -> 4; matrix products, arithmetic and copies ran while one was open for 11% -> 6% of each run, Pallas kernels for 0% -> 0%
where the time goes in v1:
time: 322 us; the launch traced here: 321 us
  waiting for transfers between devices  132 us (41%)
  blocking collectives  87.4 us (27%)
  starting transfers between devices  37.2 us (12%)
  local copies, waits for them, and re-layouts  27.3 us (8%)
  Pallas kernels  24.3 us (8%)
  other arithmetic  10.9 us (3%)
    all_to_all x1, waiting for transfers between devices, body(): lax.all_to_all(partial.reshape(device_count, local_beams, proj_width), 'd...  109 us
    all_to_all x1, blocking collectives, body(): lax.all_to_all(spread, 'dp', 0, 0, tiled=True)  47.6 us
    all_to_all x1, blocking collectives, body(): lax.all_to_all(partial_sum.reshape(tensor_count, total_rows // tensor_cou...  27 us
    pallas_call x1, Pallas kernels, attend_slots(): pl.pallas_call(attend_kernel, grid_spec=grid_spec, out_shape=jax.ShapeDty...  24.3 us
    all_to_all x1, waiting for transfers between devices, body(): lax.all_to_all(hidden_in, 'dp', split_axis=1, concat_axis=0, tiled=True)  13.9 us
    all_to_all x1, blocking collectives, body(): lax.all_to_all(copies, 'tensor', 0, 0, tiled=True)  12.8 us
    all_to_all x1, starting transfers between devices, body(): lax.all_to_all(hidden_in, 'dp', split_axis=1, concat_axis=0, tiled=True)  12 us
    all_to_all x1, starting transfers between devices, body(): lax.all_to_all(outgoing.reshape(device_count, capacity, rows, HEAD_DIM),...  8.85 us
  transfers between devices with their start and end apart: 4, of which 4 were waited for; matrix products, arithmetic and copies ran while one was open for 6% of the time, Pallas kernels for 0%

profile of v1, /device:TPU:1, one launch (start us, length us, event | category | flops | bytes accessed | tf_op | source)
XLA Modules:
  0.0 321.1 jit_solution(16280881729242209883)
XLA Ops:
  0.0 0.0 copy-start
  0.0 2.0 copy.59
  2.0 12.0 %all-to-all-start = ((bf16[32,32,256]{2,0,1:T(8,128)(2,1)}), bf16[32,32,256]{2,0,1:T(8,128)(2,1)S(1)}, u32[]{:S(2)}, u32[]{:S(2)}) async-start(bf16[32,32,256]{2,0,1:T(8,128)(2,1)} %bitcast.33), calls=%async_computation | async-start | bytes 1048576 | tf_op jit(solution)/shard_map/all_to_all | solution.py:121
  14.0 0.7 convert_element_type.66
  14.7 13.9 %all-to-all-done = bf16[32,32,256]{2,0,1:T(8,128)(2,1)S(1)} async-done(((bf16[32,32,256]{2,0,1:T(8,128)(2,1)}), bf16[32,32,256]{2,0,1:T(8,128)(2,1)S(1)}, u32[]{:S(2)}, u32[]{:S(2)}) %all-to-all-start) | async-done | bytes 524320 | tf_op jit(solution)/shard_map/all_to_all | solution.py:121
  28.5 0.1 fusion
  28.6 0.0 copy-done
  28.6 0.0 copy-start.4
  28.6 0.0 copy-start.5
  28.7 0.8 fusion.21
  29.4 0.1 copy-done.4
  29.5 0.3 fusion.22
  29.8 0.3 fusion.23
  30.1 2.8 pad_maximum_fusion
  32.9 5.9 %copy.50 = f32[1024,1280]{1,0:T(8,128)} copy(f32[1024,1280]{0,1:T(8,128)} %pad_maximum_fusion) | data formatting | bytes 10485760 | tf_op jit(solution)/shard_map/concatenate | solution.py:128
  38.8 7.5 %all-to-all-start.1 = ((f32[32,32,1280]{2,1,0:T(8,128)}), f32[32,32,1280]{2,1,0:T(8,128)}, u32[]{:S(2)}, u32[]{:S(2)}) async-start(f32[32,32,1280]{2,1,0:T(8,128)} %bitcast.34), calls=%async_computation.1 | async-start | bytes 10485760 | tf_op jit(solution)/shard_map/all_to_all | solution.py:136
  46.4 0.0 copy-done.6
  46.4 0.1 reshape.307
  46.4 0.1 compare_select_fusion.4
  46.5 0.2 convert_reduce_fusion.1
  46.7 0.6 iota_reduce_fusion
  47.3 0.1 broadcast_in_dim.130
  47.5 0.1 fusion.12
  47.5 0.1 broadcast_in_dim.128
  47.7 0.8 convert_reduce_fusion
  48.5 0.1 broadcast_add_fusion
  48.6 0.1 add.95
  48.7 0.7 gather_fusion.1
  49.4 4.3 %scatter_custom_fusion.parent_ref = s32[64]{0:T(128)S(1)} fusion(s32[1024]{0:T(1024)S(1)} %get-tuple-element.16, s32[1024]{0:T(1024)S(1)} %get-tuple-element.15, s32[]{:T(128)} %constant.107.clone.1), kind=kCustom, calls=%fused_computation.82 | custom fusion | bytes 260 | tf_op jit(solution)/shard_map/scatter | solution.py:188
  53.7 0.0 copy-done.2
  53.7 0.2 multiply_reduce_fusion
  54.0 0.1 multiply_cosine_fusion.1
  54.1 108.9 %all-to-all-done.1 = f32[32,32,1280]{2,1,0:T(8,128)} async-done(((f32[32,32,1280]{2,1,0:T(8,128)}), f32[32,32,1280]{2,1,0:T(8,128)}, u32[]{:S(2)}, u32[]{:S(2)}) %all-to-all-start.1) | async-done | bytes 5242912 | tf_op jit(solution)/shard_map/all_to_all | solution.py:136
  163.1 2.7 reduce_sum.47
  165.8 0.1 broadcast_multiply_fusion
  166.0 0.1 fusion.8
  166.1 0.1 pad_maximum_fusion.2
  166.3 0.1 subtract_convert_fusion
  166.4 0.1 pad_maximum_fusion.1
  166.5 0.6 gather_fusion.2
  167.2 0.3 broadcast_select_fusion.1
  167.5 0.8 copy.54
  168.3 8.9 %all-to-all-start.2 = ((bf16[32,2,10,128]{3,1,2,0:T(2,128)(2,1)}), bf16[32,2,10,128]{3,1,2,0:T(2,128)(2,1)S(1)}, u32[]{:S(2)}, u32[]{:S(2)}) async-start(bf16[32,2,10,128]{3,1,2,0:T(2,128)(2,1)} %copy.54), calls=%async_computation.2 | async-start | bytes 327680 | tf_op jit(solution)/shard_map/all_to_all | solution.py:173
  177.2 0.7 gather_fusion
  177.9 7.6 %reshape.312.refs_0_.refs_1_.refs_2_.refs_3_.refs_4_.refs_5_.refs_6_.refs_7_ = bf16[32,256,256]{2,1,0:T(8,128)(2,1)} reshape(bf16[32,256,2,1,128]{4,2,3,1,0:T(2,128)(2,1)} %param.16) | data formatting | bytes 8388608 | tf_op jit(solution)/shard_map/reshape | solution.py:192
  185.5 0.5 and_select_fusion.1.length_ref
  186.0 0.4 all-to-all-done.2
  186.4 0.7 copy.55
  187.1 24.3 %shard_map.100 = bf16[64,8,128]{2,1,0:T(8,128)(2,1)} custom-call(s32[64]{0:T(128)} %copy-done.7, s32[64]{0:T(128)} %and_select_fusion.1.length_ref, bf16[64,10,128]{2,1,0:T(8,128)(2,1)} %bitcast.39, bf16[32,256,256]{2,1,0:T(8,128)(2,1)} %reshape.312.refs_0_.refs_1_.refs_2_.refs_3_.refs_4_.refs_5_.refs_6_.refs_7_, ...), custom_call_target="tpu_custom_call" | custom-call | tf_op jit(solution)/shard_map/pallas_call | solution.py:93
  211.5 1.7 reshape.313
  213.1 8.8 %all-to-all-start.3 = ((bf16[32,2,1024]{2,1,0:T(2,128)(2,1)}), bf16[32,2,1024]{2,1,0:T(2,128)(2,1)S(1)}, u32[]{:S(2)}, u32[]{:S(2)}) async-start(bf16[32,2,1024]{2,1,0:T(2,128)(2,1)} %reshape.313), calls=%async_computation.3 | async-start | bytes 262144 | tf_op jit(solution)/shard_map/all_to_all | solution.py:196
  222.0 0.8 dynamic-slice_compare_fusion
  222.7 8.4 %all-to-all-done.3 = bf16[32,2,1024]{2,1,0:T(2,128)(2,1)S(1)} async-done(((bf16[32,2,1024]{2,1,0:T(2,128)(2,1)}), bf16[32,2,1024]{2,1,0:T(2,128)(2,1)S(1)}, u32[]{:S(2)}, u32[]{:S(2)}) %all-to-all-start.3) | async-done | bytes 131104 | tf_op jit(solution)/shard_map/all_to_all | solution.py:196
  231.1 0.1 reshape.314
  231.2 0.6 gather_fusion.3
  231.8 0.1 select_select_fusion
  231.9 0.2 broadcast_in_dim.140
  232.2 47.6 %all_to_all.43 = bf16[32,32,1024]{2,1,0:T(8,128)(2,1)S(1)} all-to-all(bf16[32,32,1024]{2,1,0:T(8,128)(2,1)S(1)} %broadcast_in_dim.140), channel_id=1, replica_groups=mesh['dp'=32,'tensor'=8] {'dp'}, dimensions={0} | all-to-all | bytes 4194304 | tf_op jit(solution)/shard_map/all_to_all | solution.py:203
  279.7 0.0 copy-done.3
  279.7 0.7 fusion.1
  280.4 27.0 %all_to_all.44 = f32[8,128,256]{2,1,0:T(8,128)S(1)} all-to-all(f32[8,128,256]{2,1,0:T(8,128)S(1)} %fusion.1), channel_id=1, replica_groups=mesh['dp'=32,'tensor'=8] {'tensor'}, dimensions={0} | all-to-all | bytes 2097152 | tf_op jit(solution)/shard_map/all_to_all | solution.py:209
  307.5 0.1 reduce_sum.49
  307.6 12.8 %all_to_all.45 = bf16[8,128,256]{2,1,0:T(8,128)(2,1)S(1)} all-to-all(bf16[8,128,256]{2,1,0:T(8,128)(2,1)S(1)} %broadcast_in_dim.141), channel_id=1, replica_groups=mesh['dp'=32,'tensor'=8] {'tensor'}, dimensions={0} | all-to-all | bytes 1048576 | tf_op jit(solution)/shard_map/all_to_all | solution.py:219
  320.4 0.8 copy.61
  (32 shorter events, 0.3 us)
Async XLA Ops:
  0.0 28.6 %copy-start = (bf16[256,1024]{1,0:T(8,128)(2,1)S(1)}, bf16[256,1024]{1,0:T(8,128)(2,1)}, u32[]{:S(2)}) copy-start(bf16[256,1024]{1,0:T(8,128)(2,1)} %param.12) | copy-start | bytes 1572868
  2.0 26.6 %all-to-all-start = ((bf16[32,32,256]{2,0,1:T(8,128)(2,1)}), bf16[32,32,256]{2,0,1:T(8,128)(2,1)S(1)}, u32[]{:S(2)}, u32[]{:S(2)}) async-start(bf16[32,32,256]{2,0,1:T(8,128)(2,1)} %bitcast.33), calls=%async_computation | async-start | bytes 1048576 | tf_op jit(solution)/shard_map/all_to_all | solution.py:121
  28.6 0.8 copy-start.4
  28.6 1.1 copy-start.5
  38.8 7.5 %copy-start.6 = (s32[1024]{0:T(1024)S(1)}, s32[1024]{0:T(1024)}, u32[]{:S(2)}) copy-start(s32[1024]{0:T(1024)} %param.18) | copy-start | bytes 12292
  38.8 9.8 %copy-start.1 = (s32[1024]{0:T(1024)S(1)}, s32[1024]{0:T(1024)}, u32[]{:S(2)}) copy-start(s32[1024]{0:T(1024)} %param.17) | copy-start | bytes 12292
  38.8 14.9 %copy-start.2 = (bf16[32,8192]{1,0:T(8,128)(2,1)S(1)}, bf16[32,8192]{1,0:T(8,128)(2,1)}, u32[]{:S(2)}) copy-start(bf16[32,8192]{1,0:T(8,128)(2,1)} %param.10) | copy-start | bytes 1572868
  38.8 124.2 %all-to-all-start.1 = ((f32[32,32,1280]{2,1,0:T(8,128)}), f32[32,32,1280]{2,1,0:T(8,128)}, u32[]{:S(2)}, u32[]{:S(2)}) async-start(f32[32,32,1280]{2,1,0:T(8,128)} %bitcast.34), calls=%async_computation.1 | async-start | bytes 10485760 | tf_op jit(solution)/shard_map/all_to_all | solution.py:136
  53.7 131.8 %copy-start.7 = (s32[64]{0:T(128)}, s32[64]{0:T(128)S(1)}, u32[]{:S(2)}) copy-start(s32[64]{0:T(128)S(1)} %scatter_custom_fusion.parent_ref) | copy-start | bytes 772
  168.3 18.1 %all-to-all-start.2 = ((bf16[32,2,10,128]{3,1,2,0:T(2,128)(2,1)}), bf16[32,2,10,128]{3,1,2,0:T(2,128)(2,1)S(1)}, u32[]{:S(2)}, u32[]{:S(2)}) async-start(bf16[32,2,10,128]{3,1,2,0:T(2,128)(2,1)} %copy.54), calls=%async_computation.2 | async-start | bytes 327680 | tf_op jit(solution)/shard_map/all_to_all | solution.py:173
  211.5 68.2 %copy-start.3 = (bf16[1024,256]{1,0:T(8,128)(2,1)S(1)}, bf16[1024,256]{1,0:T(8,128)(2,1)}, u32[]{:S(2)}) copy-start(bf16[1024,256]{1,0:T(8,128)(2,1)} %param.15) | copy-start | bytes 1572868
  213.1 18.0 %all-to-all-start.3 = ((bf16[32,2,1024]{2,1,0:T(2,128)(2,1)}), bf16[32,2,1024]{2,1,0:T(2,128)(2,1)S(1)}, u32[]{:S(2)}, u32[]{:S(2)}) async-start(bf16[32,2,1024]{2,1,0:T(2,128)(2,1)} %reshape.313), calls=%async_computation.3 | async-start | bytes 262144 | tf_op jit(solution)/shard_map/all_to_all | solution.py:196

commit v2 on v1

--- a/solution.py
+++ b/solution.py
@@ -42,14 +42,26 @@
     step = pl.program_id(0)
     head_width = packed_ref.shape[-1]
     head_total = packed_ref.shape[1] - 2
-    score_scale = 1.0 / math.sqrt(head_width)
     for g in range(group):
         length = length_ref[step * group + g]
+
+        @pl.when(length == 0)
+        def _():
+            out_ref[g] = jnp.zeros(out_ref.shape[1:], out_ref.dtype)
+
+        @pl.when(length > 0)
+        def _():
+            attend_one(packed_ref, cache_refs[g], out_ref, g, length, head_total, head_width)
+
+
+def attend_one(packed_ref, cache_ref, out_ref, g, length, head_total, head_width):
+    score_scale = 1.0 / math.sqrt(head_width)
+    if True:
         row = packed_ref[g].astype(jnp.float32)
         queries = row[:head_total].astype(jnp.bfloat16)
         key_new = row[head_total : head_total + 1]
         value_new = row[head_total + 1 : head_total + 2]
-        block = cache_refs[g][0]
+        block = cache_ref[0]
         keys = block[:, :head_width]
         values = block[:, head_width:]
         cached = (
@@ -118,25 +130,65 @@
 
     hidden_float = hidden_in.astype(jnp.float32)
     inverse = lax.rsqrt(jnp.mean(hidden_float * hidden_float, axis=1) + 1e-06)
-    blocked = lax.all_to_all(hidden_in, "dp", split_axis=1, concat_axis=0, tiled=True)
-    scaled = (blocked.astype(jnp.float32) * norm_gain.astype(jnp.float32)[None, :]).astype(
-        jnp.bfloat16
-    )
+
+    features = query_weight.shape[0]
+    pair_count = device_count // 2
+    is_low = device_rank % 2 == 0
+    partner = [(i, i ^ 1) for i in range(device_count)]
     query_width = query_weight.shape[1]
     key_width = key_weight.shape[1]
-    proj_width = query_width + 2 * key_width
-    partial = jnp.concatenate(
+    query_half = query_width // 2
+    key_half = key_width // 2
+    low_cols = jnp.concatenate(
+        [query_weight[:, :query_half], key_weight[:, :key_half], value_weight[:, :key_half]],
+        axis=1,
+    )
+    high_cols = jnp.concatenate(
+        [query_weight[:, query_half:], key_weight[:, key_half:], value_weight[:, key_half:]],
+        axis=1,
+    )
+    mine = jnp.where(is_low, low_cols, high_cols)
+    received = lax.ppermute(jnp.where(is_low, high_cols, low_cols), "dp", partner)
+    partner_gain = lax.ppermute(norm_gain, "dp", partner)
+    pair_weight = jnp.where(
+        is_low, jnp.concatenate([mine, received], 0), jnp.concatenate([received, mine], 0)
+    )
+    pair_gain = jnp.where(
+        is_low,
+        jnp.concatenate([norm_gain, partner_gain]),
+        jnp.concatenate([partner_gain, norm_gain]),
+    )
+    spread = jnp.swapaxes(
+        jnp.repeat(hidden_in.reshape(local_beams, pair_count, 2 * features), 2, axis=1), 0, 1
+    )
+    blocked = lax.all_to_all(spread, "dp", 0, 0, tiled=True).reshape(
+        device_count * local_beams, 2 * features
+    )
+    scaled = (blocked.astype(jnp.float32) * pair_gain.astype(jnp.float32)[None, :]).astype(
+        jnp.bfloat16
+    )
+    partial = jnp.dot(scaled, pair_weight, preferred_element_type=jnp.float32)
+    half_width = partial.shape[1]
+    arrived = lax.all_to_all(
+        partial.reshape(device_count, local_beams, half_width), "dp", 0, 0, tiled=True
+    )
+    sums = jnp.sum(arrived.reshape(pair_count, 2, local_beams, half_width), axis=0)
+    key_end = query_half + key_half
+    summed = jnp.concatenate(
         [
-            jnp.dot(scaled, query_weight, preferred_element_type=jnp.float32),
-            jnp.dot(scaled, key_weight, preferred_element_type=jnp.float32),
-            jnp.dot(scaled, value_weight, preferred_element_type=jnp.float32),
+            sums[0, :, :query_half],
+            sums[1, :, :query_half],
+            sums[0, :, query_half:key_end],
+            sums[1, :, query_half:key_end],
+            sums[0, :, key_end:],
+            sums[1, :, key_end:],
         ],
         axis=1,
-    )
-    arrived = lax.all_to_all(
-        partial.reshape(device_count, local_beams, proj_width), "dp", 0, 0, tiled=True
-    )
-    summed = jnp.sum(arrived, axis=0) * inverse[:, None]
+    ) * inverse[:, None]
+    cache_rows = key_value_cache.reshape(
+        local_beams, key_value_cache.shape[1], 2 * key_value_cache.shape[-1]
+    )
+    summed, cache_rows = lax.optimization_barrier((summed, cache_rows))
 
     first_beam = device_rank * local_beams
     my_parent = lax.dynamic_slice_in_dim(parent_beam, first_beam, local_beams)
@@ -182,16 +234,13 @@
     placed = jnp.where(
         all_sources == device_rank, destination * capacity + arrival_ranks(all_sources), slot_total
     )
-    local_parent = (
-        jnp.zeros((slot_total,), jnp.int32)
-        .at[placed.reshape(-1)]
-        .set((all_parents % local_beams).reshape(-1), mode="drop")
-    )
-    slot_length = jnp.take(cache_lengths, first_beam + local_parent)
-
-    cache_rows = key_value_cache.reshape(
-        local_beams, key_value_cache.shape[1], 2 * key_value_cache.shape[-1]
-    )
+    chosen = placed.reshape(-1)[None, :] == slot_of[:, None]
+    local_parent = jnp.sum(
+        jnp.where(chosen, (all_parents % local_beams).reshape(-1)[None, :], 0), axis=1
+    )
+    used = jnp.any(chosen, axis=1).astype(jnp.int32)
+    slot_length = jnp.take(cache_lengths, first_beam + local_parent) * used
+
     mixed = attend_slots(incoming, cache_rows, local_parent, slot_length)
     returned = lax.all_to_all(
         mixed.reshape(device_count, capacity, head_count * HEAD_DIM), "dp", 0, 0, tiled=True

time: 322 us -> 264 us (0.82)
  waiting for transfers between devices: 132 us -> 92.9 us
  local copies, waits for them, and re-layouts: 27.3 us -> 17.6 us
  other arithmetic: 10.9 us -> 6.22 us
  Pallas kernels: 24.3 us -> 20.9 us
    all_to_all x2, waiting for transfers between devices: 123 us -> 46.7 us  [the longest x1 46.7 us: body(): lax.all_to_all(partial.reshape(device_count, local_beams, half_width), 'd...]
    ppermute x0 -> x2, waiting for transfers between devices: none -> 29.2 us  [the longest x1 29.2 us: body(): partner_gain = lax.ppermute(norm_gain, 'dp', partner)]
    all_to_all x1, waiting for transfers between devices: 0.36 us -> 8.59 us  [body(): lax.all_to_all(outgoing.reshape(device_count, capacity, rows, HEAD_DIM),...]
    concatenate x1, local copies, waits for them, and re-layouts: 5.92 us -> 0.09 us  [body(): jnp.concatenate([sums[0, :, :query_half], sums[1, :, :query_half], sums[0...]
    scatter x1 -> x0, local copies, waits for them, and re-layouts: 4.3 us -> none  [body(): local_parent = jnp.zeros((slot_total,), jnp.int32).at[placed.reshape(-1)]...]
    all_to_all x1, starting transfers between devices: 8.8 us -> 5.26 us  [body(): lax.all_to_all(mixed.reshape(device_count, capacity, head_count * HEAD_DI...]
    pallas_call x1, Pallas kernels: 24.3 us -> 20.9 us  [attend_slots(): pl.pallas_call(attend_kernel, grid_spec=grid_spec, out_shape=jax.ShapeDty...]
  transfers between devices with their start and end apart: 4 -> 6, of which waited for: 4 -> 4; matrix products, arithmetic and copies ran while one was open for 6% -> 6% of each run, Pallas kernels for 0% -> 0%
where the time goes in v2:
time: 264 us
  waiting for transfers between devices  92.9 us (35%)
  blocking collectives  87.4 us (33%)
  starting transfers between devices  35.2 us (13%)
  Pallas kernels  20.9 us (8%)
  local copies, waits for them, and re-layouts  17.6 us (7%)
  other arithmetic  6.22 us (2%)
  matrix products  3.25 us (1%)
    all_to_all x1, blocking collectives, body(): lax.all_to_all(spread, 'dp', 0, 0, tiled=True)  47.6 us
    all_to_all x1, waiting for transfers between devices, body(): lax.all_to_all(partial.reshape(device_count, local_beams, half_width), 'd...  46.7 us
    ppermute x1, waiting for transfers between devices, body(): partner_gain = lax.ppermute(norm_gain, 'dp', partner)  29.2 us
    all_to_all x1, blocking collectives, body(): lax.all_to_all(partial_sum.reshape(tensor_count, total_rows // tensor_cou...  27.1 us
    pallas_call x1, Pallas kernels, attend_slots(): pl.pallas_call(attend_kernel, grid_spec=grid_spec, out_shape=jax.ShapeDty...  20.9 us
    all_to_all x1, blocking collectives, body(): lax.all_to_all(copies, 'tensor', 0, 0, tiled=True)  12.8 us
    all_to_all x1, starting transfers between devices, body(): lax.all_to_all(spread, 'dp', 0, 0, tiled=True)  12.2 us
    all_to_all x1, starting transfers between devices, body(): lax.all_to_all(partial.reshape(device_count, local_beams, half_width), 'd...  8.8 us
  transfers between devices with their start and end apart: 6, of which 4 were waited for; matrix products, arithmetic and copies ran while one was open for 6% of the time, Pallas kernels for 0%

profile of v2, /device:TPU:1, one launch (start us, length us, event | category | flops | bytes accessed | tf_op | source)
XLA Modules:
  0.0 263.9 jit_solution(2112151404672343034)
XLA Ops:
  0.0 1.1 copy.50
  1.2 0.0 copy-start.3
  1.2 0.0 copy-start.4
  1.2 0.0 copy-start.2
  1.2 1.1 broadcast_in_dim.139
  2.3 12.2 %all-to-all-start = ((bf16[32,32,512]{2,1,0:T(8,128)(2,1)}), bf16[32,32,512]{2,1,0:T(8,128)(2,1)S(1)}, u32[]{:S(2)}, u32[]{:S(2)}) async-start(bf16[32,32,512]{2,1,0:T(8,128)(2,1)} %bitcast.3), calls=%async_computation | async-start | bytes 2097152 | tf_op jit(solution)/shard_map/all_to_all | solution.py:164
  14.5 0.1 fusion.35
  14.7 0.2 broadcast_select_fusion.1
  14.9 1.3 collective-permute-start.1
  16.2 0.2 collective-permute-start
  16.4 29.2 %collective-permute-done = bf16[256]{0:T(256)(128)(2,1)S(1)} collective-permute-done((bf16[256]{0:T(256)(128)(2,1)S(1)}, bf16[256]{0:T(256)(128)(2,1)S(1)}, u32[]{:S(2)}, u32[]{:S(2)}) %collective-permute-start) | collective-permute-done | bytes 544 | tf_op jit(solution)/shard_map/ppermute | solution.py:152
  45.6 0.0 collective-permute-done.1
  45.6 2.5 fusion
  48.2 8.8 %all-to-all-start.1 = ((f32[32,32,640]{2,1,0:T(8,128)}), f32[32,32,640]{2,1,0:T(8,128)S(1)}, u32[]{:S(2)}, u32[]{:S(2)}) async-start(f32[32,32,640]{2,1,0:T(8,128)} %fusion), calls=%async_computation.1 | async-start | bytes 5242880 | tf_op jit(solution)/shard_map/all_to_all | solution.py:172
  57.0 0.0 copy-start.5
  57.0 0.0 copy-start.1
  57.0 7.6 %reshape.402.refs_0_.refs_1_.refs_2_.refs_3_.refs_4_.refs_5_.refs_6_.refs_7_ = bf16[32,256,256]{2,1,0:T(8,128)(2,1)} reshape(bf16[32,256,2,1,128]{4,2,3,1,0:T(2,128)(2,1)} %param.16) | data formatting | bytes 8388608 | tf_op jit(solution)/shard_map/reshape | solution.py:188
  64.6 0.1 reshape.398
  64.7 0.1 compare_select_fusion.4
  64.8 0.2 convert_reduce_fusion.1
  64.9 0.6 iota_reduce_fusion
  65.6 0.1 broadcast_in_dim.137
  65.7 0.1 fusion.22
  65.8 0.1 broadcast_in_dim.135
  65.9 0.8 convert_reduce_fusion
  66.7 0.1 broadcast_add_fusion
  66.8 0.1 add.123
  66.9 0.7 gather_fusion.1
  67.6 0.1 select_reduce_fusion.parent_ref
  67.8 0.7 gather_fusion
  68.5 1.3 multiply_reduce_fusion
  69.8 0.1 multiply_cosine_fusion.1
  69.9 46.7 %all-to-all-done.1 = f32[32,32,640]{2,1,0:T(8,128)S(1)} async-done(((f32[32,32,640]{2,1,0:T(8,128)}), f32[32,32,640]{2,1,0:T(8,128)S(1)}, u32[]{:S(2)}, u32[]{:S(2)}) %all-to-all-start.1) | async-done | bytes 2621472 | tf_op jit(solution)/shard_map/all_to_all | solution.py:172
  116.7 0.1 reduce_sum.57
  116.8 0.1 slice_bitcast_fusion.3
  116.9 0.1 concatenate.54
  117.0 0.1 broadcast_multiply_fusion
  117.1 0.1 fusion.18
  117.3 0.1 pad_maximum_fusion.3
  117.4 0.1 subtract_convert_fusion
  117.5 0.1 pad_maximum_fusion.2
  117.6 0.6 gather_fusion.2
  118.3 0.4 broadcast_select_fusion.3
  118.7 0.8 copy.45
  119.4 7.5 %all-to-all-start.2 = ((bf16[32,2,10,128]{3,1,2,0:T(2,128)(2,1)}), bf16[32,2,10,128]{3,1,2,0:T(2,128)(2,1)S(1)}, u32[]{:S(2)}, u32[]{:S(2)}) async-start(bf16[32,2,10,128]{3,1,2,0:T(2,128)(2,1)} %copy.45), calls=%async_computation.2 | async-start | bytes 327680 | tf_op jit(solution)/shard_map/all_to_all | solution.py:225
  126.9 0.1 fusion.12
  127.0 0.6 fusion.30.length_ref
  127.6 8.6 %all-to-all-done.2 = bf16[32,2,10,128]{3,1,2,0:T(2,128)(2,1)S(1)} async-done(((bf16[32,2,10,128]{3,1,2,0:T(2,128)(2,1)}), bf16[32,2,10,128]{3,1,2,0:T(2,128)(2,1)S(1)}, u32[]{:S(2)}, u32[]{:S(2)}) %all-to-all-start.2) | async-done | bytes 163872 | tf_op jit(solution)/shard_map/all_to_all | solution.py:225
  136.2 0.7 copy.46
  136.9 20.9 %shard_map.100 = bf16[64,8,128]{2,1,0:T(8,128)(2,1)} custom-call(s32[64]{0:T(128)} %copy-done.6, s32[64]{0:T(128)} %fusion.30.length_ref, bf16[64,10,128]{2,1,0:T(8,128)(2,1)} %bitcast.50, bf16[32,256,256]{2,1,0:T(8,128)(2,1)} %reshape.402.refs_0_.refs_1_.refs_2_.refs_3_.refs_4_.refs_5_.refs_6_.refs_7_, ...), custom_call_target="tpu_custom_call" | custom-call | tf_op jit(solution)/shard_map/pallas_call | solution.py:105
  157.8 1.6 reshape.406
  159.4 5.3 %all-to-all-start.3 = ((bf16[32,2,1024]{2,1,0:T(2,128)(2,1)}), bf16[32,2,1024]{2,1,0:T(2,128)(2,1)S(1)}, u32[]{:S(2)}, u32[]{:S(2)}) async-start(bf16[32,2,1024]{2,1,0:T(2,128)(2,1)} %reshape.406), calls=%async_computation.3 | async-start | bytes 262144 | tf_op jit(solution)/shard_map/all_to_all | solution.py:245
  164.7 0.8 dynamic-slice_compare_fusion
  165.4 8.4 %all-to-all-done.3 = bf16[32,2,1024]{2,1,0:T(2,128)(2,1)S(1)} async-done(((bf16[32,2,1024]{2,1,0:T(2,128)(2,1)}), bf16[32,2,1024]{2,1,0:T(2,128)(2,1)S(1)}, u32[]{:S(2)}, u32[]{:S(2)}) %all-to-all-start.3) | async-done | bytes 131104 | tf_op jit(solution)/shard_map/all_to_all | solution.py:245
  173.8 0.1 reshape.407
  173.9 0.6 gather_fusion.3
  174.5 0.1 select_select_fusion
  174.6 0.2 broadcast_in_dim.148
  174.8 47.6 %all_to_all.35 = bf16[32,32,1024]{2,1,0:T(8,128)(2,1)S(1)} all-to-all(bf16[32,32,1024]{2,1,0:T(8,128)(2,1)S(1)} %broadcast_in_dim.148), channel_id=1, replica_groups=mesh['dp'=32,'tensor'=8] {'dp'}, dimensions={0} | all-to-all | bytes 4194304 | tf_op jit(solution)/shard_map/all_to_all | solution.py:252
  222.4 0.7 fusion.10
  223.2 27.1 %all_to_all.36 = f32[8,128,256]{2,1,0:T(8,128)S(1)} all-to-all(f32[8,128,256]{2,1,0:T(8,128)S(1)} %fusion.10), channel_id=1, replica_groups=mesh['dp'=32,'tensor'=8] {'tensor'}, dimensions={0} | all-to-all | bytes 2097152 | tf_op jit(solution)/shard_map/all_to_all | solution.py:258
  250.2 0.1 reduce_sum.59
  250.3 12.8 %all_to_all.37 = bf16[8,128,256]{2,1,0:T(8,128)(2,1)S(1)} all-to-all(bf16[8,128,256]{2,1,0:T(8,128)(2,1)S(1)} %broadcast_in_dim.149), channel_id=1, replica_groups=mesh['dp'=32,'tensor'=8] {'tensor'}, dimensions={0} | all-to-all | bytes 1048576 | tf_op jit(solution)/shard_map/all_to_all | solution.py:268
  263.1 0.8 copy.52
  (39 shorter events, 0.3 us)
Async XLA Ops:
  0.0 222.4 %copy-start = (bf16[1024,256]{1,0:T(8,128)(2,1)S(1)}, bf16[1024,256]{1,0:T(8,128)(2,1)}, u32[]{:S(2)}) copy-start(bf16[1024,256]{1,0:T(8,128)(2,1)} %param.15) | copy-start | bytes 1572868
  1.2 13.3 %copy-start.3 = (bf16[256,128]{1,0:T(8,128)(2,1)S(1)}, bf16[256,128]{1,0:T(8,128)(2,1)}, u32[]{:S(2)}) copy-start(bf16[256,128]{1,0:T(8,128)(2,1)} %param.13) | copy-start | bytes 196612
  1.2 13.3 %copy-start.4 = (bf16[256,128]{1,0:T(8,128)(2,1)S(1)}, bf16[256,128]{1,0:T(8,128)(2,1)}, u32[]{:S(2)}) copy-start(bf16[256,128]{1,0:T(8,128)(2,1)} %param.14) | copy-start | bytes 196612
  1.2 13.4 %copy-start.2 = (bf16[256,1024]{1,0:T(8,128)(2,1)S(1)}, bf16[256,1024]{1,0:T(8,128)(2,1)}, u32[]{:S(2)}) copy-start(bf16[256,1024]{1,0:T(8,128)(2,1)} %param.12) | copy-start | bytes 1572868
  2.3 13.9 %copy-start.7 = (bf16[256]{0:T(256)(128)(2,1)S(1)}, bf16[256]{0:T(256)(128)(2,1)}, u32[]{:S(2)}) copy-start(bf16[256]{0:T(256)(128)(2,1)} %param.11) | copy-start | bytes 1540
  2.3 43.3 %all-to-all-start = ((bf16[32,32,512]{2,1,0:T(8,128)(2,1)}), bf16[32,32,512]{2,1,0:T(8,128)(2,1)S(1)}, u32[]{:S(2)}, u32[]{:S(2)}) async-start(bf16[32,32,512]{2,1,0:T(8,128)(2,1)} %bitcast.3), calls=%async_computation | async-start | bytes 2097152 | tf_op jit(solution)/shard_map/all_to_all | solution.py:164
  14.9 30.8 %collective-permute-start.1 = (bf16[256,640]{1,0:T(8,128)(2,1)S(1)}, bf16[256,640]{1,0:T(8,128)(2,1)S(1)}, u32[]{:S(2)}, u32[]{:S(2)}) collective-permute-start(bf16[256,640]{1,0:T(8,128)(2,1)S(1)} %get-tuple-element.14), channel_id=1, source_target_pairs={{0,8},{8,0},{16,24},{24,16},{32,40},{40,32},{48,56},{56,48},{64,72... | collective-permute-start | bytes 983048 | tf_op jit(solution)/shard_map/ppermute | solution.py:151
  16.2 29.4 %collective-permute-start = (bf16[256]{0:T(256)(128)(2,1)S(1)}, bf16[256]{0:T(256)(128)(2,1)S(1)}, u32[]{:S(2)}, u32[]{:S(2)}) collective-permute-start(bf16[256]{0:T(256)(128)(2,1)S(1)} %copy-done.7), channel_id=1, source_target_pairs={{0,8},{8,0},{16,24},{24,16},{32,40},{40,32},{48,56},{56,48},{64,72... | collective-permute-start | bytes 1544 | tf_op jit(solution)/shard_map/ppermute | solution.py:152
  48.2 68.5 %all-to-all-start.1 = ((f32[32,32,640]{2,1,0:T(8,128)}), f32[32,32,640]{2,1,0:T(8,128)S(1)}, u32[]{:S(2)}, u32[]{:S(2)}) async-start(f32[32,32,640]{2,1,0:T(8,128)} %fusion), calls=%async_computation.1 | async-start | bytes 5242880 | tf_op jit(solution)/shard_map/all_to_all | solution.py:172
  57.0 7.6 %copy-start.5 = (s32[1024]{0:T(1024)S(1)}, s32[1024]{0:T(1024)}, u32[]{:S(2)}) copy-start(s32[1024]{0:T(1024)} %param.18) | copy-start | bytes 12292
  57.0 9.9 %copy-start.1 = (s32[1024]{0:T(1024)S(1)}, s32[1024]{0:T(1024)}, u32[]{:S(2)}) copy-start(s32[1024]{0:T(1024)} %param.17) | copy-start | bytes 12292
  67.7 59.3 %copy-start.6 = (s32[64]{0:T(128)}, s32[64]{0:T(128)S(1)}, u32[]{:S(2)}) copy-start(s32[64]{0:T(128)S(1)} %select_reduce_fusion.parent_ref) | copy-start | bytes 772
  119.4 16.7 %all-to-all-start.2 = ((bf16[32,2,10,128]{3,1,2,0:T(2,128)(2,1)}), bf16[32,2,10,128]{3,1,2,0:T(2,128)(2,1)S(1)}, u32[]{:S(2)}, u32[]{:S(2)}) async-start(bf16[32,2,10,128]{3,1,2,0:T(2,128)(2,1)} %copy.45), calls=%async_computation.2 | async-start | bytes 327680 | tf_op jit(solution)/shard_map/all_to_all | solution.py:225
  159.4 14.4 %all-to-all-start.3 = ((bf16[32,2,1024]{2,1,0:T(2,128)(2,1)}), bf16[32,2,1024]{2,1,0:T(2,128)(2,1)S(1)}, u32[]{:S(2)}, u32[]{:S(2)}) async-start(bf16[32,2,1024]{2,1,0:T(2,128)(2,1)} %reshape.406), calls=%async_computation.3 | async-start | bytes 262144 | tf_op jit(solution)/shard_map/all_to_all | solution.py:245

commit v3 on v2

--- a/solution.py
+++ b/solution.py
@@ -170,9 +170,15 @@
     partial = jnp.dot(scaled, pair_weight, preferred_element_type=jnp.float32)
     half_width = partial.shape[1]
     arrived = lax.all_to_all(
-        partial.reshape(device_count, local_beams, half_width), "dp", 0, 0, tiled=True
-    )
-    sums = jnp.sum(arrived.reshape(pair_count, 2, local_beams, half_width), axis=0)
+        partial.astype(jnp.bfloat16).reshape(device_count, local_beams, half_width),
+        "dp",
+        0,
+        0,
+        tiled=True,
+    )
+    sums = jnp.sum(
+        arrived.astype(jnp.float32).reshape(pair_count, 2, local_beams, half_width), axis=0
+    )
     key_end = query_half + key_half
     summed = jnp.concatenate(
         [

time: 264 us -> 235 us (0.89)
  waiting for transfers between devices: 92.9 us -> 64.6 us
    all_to_all x1, waiting for transfers between devices: 46.7 us -> 19.8 us  [body(): lax.all_to_all(partial.astype(jnp.bfloat16).reshape(device_count, local_b...]
    ppermute x1, waiting for transfers between devices: 29.2 us -> 19.5 us  [body(): partner_gain = lax.ppermute(norm_gain, 'dp', partner)]
    ppermute x1, waiting for transfers between devices: 0.01 us -> 8.42 us  [body(): lax.ppermute(jnp.where(is_low, high_cols, low_cols), 'dp', partner)]
  transfers between devices with their start and end apart: 6 -> 6, of which waited for: 4 -> 5; matrix products, arithmetic and copies ran while one was open for 6% -> 6% of each run, Pallas kernels for 0% -> 0%
where the time goes in v3:
time: 235 us; the launch traced here: 234 us
  blocking collectives  87.5 us (37%)
  waiting for transfers between devices  64.6 us (27%)
  starting transfers between devices  37.2 us (16%)
  Pallas kernels  18.9 us (8%)
  local copies, waits for them, and re-layouts  17.7 us (8%)
  other arithmetic  5.24 us (2%)
  matrix products  2.79 us (1%)
    all_to_all x1, blocking collectives, body(): lax.all_to_all(spread, 'dp', 0, 0, tiled=True)  47.4 us
    all_to_all x1, blocking collectives, body(): lax.all_to_all(partial_sum.reshape(tensor_count, total_rows // tensor_cou...  27.3 us
    all_to_all x1, waiting for transfers between devices, body(): lax.all_to_all(partial.astype(jnp.bfloat16).reshape(device_count, local_b...  19.8 us
    ppermute x1, waiting for transfers between devices, body(): partner_gain = lax.ppermute(norm_gain, 'dp', partner)  19.5 us
    pallas_call x1, Pallas kernels, attend_slots(): pl.pallas_call(attend_kernel, grid_spec=grid_spec, out_shape=jax.ShapeDty...  18.9 us
    all_to_all x1, blocking collectives, body(): lax.all_to_all(copies, 'tensor', 0, 0, tiled=True)  12.8 us
    all_to_all x1, starting transfers between devices, body(): lax.all_to_all(spread, 'dp', 0, 0, tiled=True)  12.2 us
    all_to_all x1, starting transfers between devices, body(): lax.all_to_all(partial.astype(jnp.bfloat16).reshape(device_count, local_b...  8.8 us
  transfers between devices with their start and end apart: 6, of which 5 were waited for; matrix products, arithmetic and copies ran while one was open for 6% of the time, Pallas kernels for 0%

profile of v3, /device:TPU:1, one launch (start us, length us, event | category | flops | bytes accessed | tf_op | source)
XLA Modules:
  0.0 234.2 jit_solution(7777437531286403280)
XLA Ops:
  0.0 1.1 copy.49
  1.2 0.0 copy-start.8
  1.2 0.0 copy-start.4
  1.2 0.0 copy-start.5
  1.2 0.0 copy-start.3
  1.2 1.1 broadcast_in_dim.139
  2.3 12.2 %all-to-all-start = ((bf16[32,32,512]{2,1,0:T(8,128)(2,1)}), bf16[32,32,512]{2,1,0:T(8,128)(2,1)S(1)}, u32[]{:S(2)}, u32[]{:S(2)}) async-start(bf16[32,32,512]{2,1,0:T(8,128)(2,1)} %bitcast.3), calls=%async_computation | async-start | bytes 2097152 | tf_op jit(solution)/shard_map/all_to_all | solution.py:164
  14.5 1.3 collective-permute-start
  15.8 0.1 fusion.34
  16.0 0.2 broadcast_select_fusion.1
  16.2 0.3 collective-permute-start.1
  16.5 0.1 reshape.399
  16.6 0.1 compare_select_fusion.4
  16.7 0.2 convert_reduce_fusion.2
  16.9 0.8 convert_reduce_fusion.1
  17.6 0.1 broadcast_add_fusion
  17.7 19.5 %collective-permute-done = bf16[256]{0:T(256)(128)(2,1)S(1)} collective-permute-done((bf16[256]{0:T(256)(128)(2,1)S(1)}, bf16[256]{0:T(256)(128)(2,1)S(1)}, u32[]{:S(2)}, u32[]{:S(2)}) %collective-permute-start) | collective-permute-done | bytes 544 | tf_op jit(solution)/shard_map/ppermute | solution.py:152
  37.2 8.4 %collective-permute-done.1 = bf16[256,640]{1,0:T(8,128)(2,1)S(1)} collective-permute-done((bf16[256,640]{1,0:T(8,128)(2,1)S(1)}, bf16[256,640]{1,0:T(8,128)(2,1)S(1)}, u32[]{:S(2)}, u32[]{:S(2)}) %collective-permute-start.1) | collective-permute-done | bytes 327712 | tf_op jit(solution)/shard_map/ppermute | solution.py:151
  45.6 2.1 convolution_convert_fusion
  47.7 8.8 %all-to-all-start.1 = ((bf16[32,32,640]{2,1,0:T(8,128)(2,1)}), bf16[32,32,640]{2,1,0:T(8,128)(2,1)S(1)}, u32[]{:S(2)}, u32[]{:S(2)}) async-start(bf16[32,32,640]{2,1,0:T(8,128)(2,1)} %bitcast.5), calls=%async_computation.1 | async-start | bytes 2621440 | tf_op jit(solution)/shard_map/all_to_all | solution.py:172
  56.5 0.1 fusion.21
  56.6 0.1 add.123
  56.7 0.1 broadcast_in_dim.135
  56.8 0.0 copy-start.1
  56.8 7.7 %reshape.405.refs_0_.refs_1_.refs_2_.refs_3_.refs_4_.refs_5_.refs_6_.refs_7_ = bf16[32,256,256]{2,1,0:T(8,128)(2,1)} reshape(bf16[32,256,2,1,128]{4,2,3,1,0:T(2,128)(2,1)} %param.16) | data formatting | bytes 8388608 | tf_op jit(solution)/shard_map/reshape | solution.py:194
  64.5 0.1 select_reduce_fusion.parent_ref
  64.6 0.7 gather_fusion
  65.4 0.7 gather_fusion.1
  66.0 0.6 iota_reduce_fusion
  66.7 0.1 broadcast_in_dim.137
  66.8 0.2 multiply_reduce_fusion
  67.1 0.1 multiply_cosine_fusion.1
  67.2 19.8 %all-to-all-done.1 = bf16[32,32,640]{2,1,0:T(8,128)(2,1)S(1)} async-done(((bf16[32,32,640]{2,1,0:T(8,128)(2,1)}), bf16[32,32,640]{2,1,0:T(8,128)(2,1)S(1)}, u32[]{:S(2)}, u32[]{:S(2)}) %all-to-all-start.1) | async-done | bytes 1310752 | tf_op jit(solution)/shard_map/all_to_all | solution.py:172
  87.0 0.2 convert_reduce_fusion
  87.2 0.1 slice_bitcast_fusion.3
  87.3 0.1 concatenate.54
  87.4 0.1 broadcast_multiply_fusion
  87.5 0.1 fusion.17
  87.6 0.1 pad_maximum_fusion.3
  87.8 0.1 subtract_convert_fusion
  87.9 0.1 pad_maximum_fusion.2
  88.0 0.6 gather_fusion.2
  88.7 0.4 broadcast_select_fusion.3
  89.0 0.8 copy.44
  89.8 8.4 %all-to-all-start.2 = ((bf16[32,2,10,128]{3,1,2,0:T(2,128)(2,1)}), bf16[32,2,10,128]{3,1,2,0:T(2,128)(2,1)S(1)}, u32[]{:S(2)}, u32[]{:S(2)}) async-start(bf16[32,2,10,128]{3,1,2,0:T(2,128)(2,1)} %copy.44), calls=%async_computation.2 | async-start | bytes 327680 | tf_op jit(solution)/shard_map/all_to_all | solution.py:231
  98.2 0.1 fusion.11
  98.3 0.6 fusion.29.length_ref
  98.9 8.6 %all-to-all-done.2 = bf16[32,2,10,128]{3,1,2,0:T(2,128)(2,1)S(1)} async-done(((bf16[32,2,10,128]{3,1,2,0:T(2,128)(2,1)}), bf16[32,2,10,128]{3,1,2,0:T(2,128)(2,1)S(1)}, u32[]{:S(2)}, u32[]{:S(2)}) %all-to-all-start.2) | async-done | bytes 163872 | tf_op jit(solution)/shard_map/all_to_all | solution.py:231
  107.4 0.7 copy.45
  108.2 18.9 %shard_map.100 = bf16[64,8,128]{2,1,0:T(8,128)(2,1)} custom-call(s32[64]{0:T(128)} %copy-done.7, s32[64]{0:T(128)} %fusion.29.length_ref, bf16[64,10,128]{2,1,0:T(8,128)(2,1)} %bitcast.51, bf16[32,256,256]{2,1,0:T(8,128)(2,1)} %reshape.405.refs_0_.refs_1_.refs_2_.refs_3_.refs_4_.refs_5_.refs_6_.refs_7_, ...), custom_call_target="tpu_custom_call" | custom-call | tf_op jit(solution)/shard_map/pallas_call | solution.py:105
  127.1 1.6 reshape.409
  128.7 6.2 %all-to-all-start.3 = ((bf16[32,2,1024]{2,1,0:T(2,128)(2,1)}), bf16[32,2,1024]{2,1,0:T(2,128)(2,1)S(1)}, u32[]{:S(2)}, u32[]{:S(2)}) async-start(bf16[32,2,1024]{2,1,0:T(2,128)(2,1)} %reshape.409), calls=%async_computation.3 | async-start | bytes 262144 | tf_op jit(solution)/shard_map/all_to_all | solution.py:251
  134.9 0.8 dynamic-slice_compare_fusion
  135.7 8.4 %all-to-all-done.3 = bf16[32,2,1024]{2,1,0:T(2,128)(2,1)S(1)} async-done(((bf16[32,2,1024]{2,1,0:T(2,128)(2,1)}), bf16[32,2,1024]{2,1,0:T(2,128)(2,1)S(1)}, u32[]{:S(2)}, u32[]{:S(2)}) %all-to-all-start.3) | async-done | bytes 131104 | tf_op jit(solution)/shard_map/all_to_all | solution.py:251
  144.1 0.1 reshape.410
  144.1 0.6 gather_fusion.3
  144.8 0.1 select_select_fusion
  144.9 0.2 broadcast_in_dim.148
  145.1 47.4 %all_to_all.35 = bf16[32,32,1024]{2,1,0:T(8,128)(2,1)S(1)} all-to-all(bf16[32,32,1024]{2,1,0:T(8,128)(2,1)S(1)} %broadcast_in_dim.148), channel_id=1, replica_groups=mesh['dp'=32,'tensor'=8] {'dp'}, dimensions={0} | all-to-all | bytes 4194304 | tf_op jit(solution)/shard_map/all_to_all | solution.py:258
  192.5 0.7 fusion.9
  193.2 27.3 %all_to_all.36 = f32[8,128,256]{2,1,0:T(8,128)S(1)} all-to-all(f32[8,128,256]{2,1,0:T(8,128)S(1)} %fusion.9), channel_id=1, replica_groups=mesh['dp'=32,'tensor'=8] {'tensor'}, dimensions={0} | all-to-all | bytes 2097152 | tf_op jit(solution)/shard_map/all_to_all | solution.py:264
  220.5 0.1 reduce_sum.59
  220.7 12.8 %all_to_all.37 = bf16[8,128,256]{2,1,0:T(8,128)(2,1)S(1)} all-to-all(bf16[8,128,256]{2,1,0:T(8,128)(2,1)S(1)} %broadcast_in_dim.149), channel_id=1, replica_groups=mesh['dp'=32,'tensor'=8] {'tensor'}, dimensions={0} | all-to-all | bytes 1048576 | tf_op jit(solution)/shard_map/all_to_all | solution.py:274
  233.4 0.8 copy.51
  (41 shorter events, 0.3 us)
Async XLA Ops:
  0.0 192.5 %copy-start = (bf16[1024,256]{1,0:T(8,128)(2,1)S(1)}, bf16[1024,256]{1,0:T(8,128)(2,1)}, u32[]{:S(2)}) copy-start(bf16[1024,256]{1,0:T(8,128)(2,1)} %param.15) | copy-start | bytes 1572868
  1.2 13.3 %copy-start.8 = (bf16[256]{0:T(256)(128)(2,1)S(1)}, bf16[256]{0:T(256)(128)(2,1)}, u32[]{:S(2)}) copy-start(bf16[256]{0:T(256)(128)(2,1)} %param.11) | copy-start | bytes 1540
  1.2 14.6 %copy-start.4 = (bf16[256,128]{1,0:T(8,128)(2,1)S(1)}, bf16[256,128]{1,0:T(8,128)(2,1)}, u32[]{:S(2)}) copy-start(bf16[256,128]{1,0:T(8,128)(2,1)} %param.13) | copy-start | bytes 196612
  1.2 14.6 %copy-start.5 = (bf16[256,128]{1,0:T(8,128)(2,1)S(1)}, bf16[256,128]{1,0:T(8,128)(2,1)}, u32[]{:S(2)}) copy-start(bf16[256,128]{1,0:T(8,128)(2,1)} %param.14) | copy-start | bytes 196612
  1.2 14.7 %copy-start.3 = (bf16[256,1024]{1,0:T(8,128)(2,1)S(1)}, bf16[256,1024]{1,0:T(8,128)(2,1)}, u32[]{:S(2)}) copy-start(bf16[256,1024]{1,0:T(8,128)(2,1)} %param.12) | copy-start | bytes 1572868
  2.3 14.2 %copy-start.6 = (s32[1024]{0:T(1024)S(1)}, s32[1024]{0:T(1024)}, u32[]{:S(2)}) copy-start(s32[1024]{0:T(1024)} %param.18) | copy-start | bytes 12292
  2.3 43.3 %all-to-all-start = ((bf16[32,32,512]{2,1,0:T(8,128)(2,1)}), bf16[32,32,512]{2,1,0:T(8,128)(2,1)S(1)}, u32[]{:S(2)}, u32[]{:S(2)}) async-start(bf16[32,32,512]{2,1,0:T(8,128)(2,1)} %bitcast.3), calls=%async_computation | async-start | bytes 2097152 | tf_op jit(solution)/shard_map/all_to_all | solution.py:164
  14.5 22.7 %collective-permute-start = (bf16[256]{0:T(256)(128)(2,1)S(1)}, bf16[256]{0:T(256)(128)(2,1)S(1)}, u32[]{:S(2)}, u32[]{:S(2)}) collective-permute-start(bf16[256]{0:T(256)(128)(2,1)S(1)} %copy-done.8), channel_id=1, source_target_pairs={{0,8},{8,0},{16,24},{24,16},{32,40},{40,32},{48,56},{56,48},{64,72... | collective-permute-start | bytes 1544 | tf_op jit(solution)/shard_map/ppermute | solution.py:152
  16.2 29.4 %collective-permute-start.1 = (bf16[256,640]{1,0:T(8,128)(2,1)S(1)}, bf16[256,640]{1,0:T(8,128)(2,1)S(1)}, u32[]{:S(2)}, u32[]{:S(2)}) collective-permute-start(bf16[256,640]{1,0:T(8,128)(2,1)S(1)} %get-tuple-element.14), channel_id=1, source_target_pairs={{0,8},{8,0},{16,24},{24,16},{32,40},{40,32},{48,56},{56,48},{64,72... | collective-permute-start | bytes 983048 | tf_op jit(solution)/shard_map/ppermute | solution.py:151
  47.7 39.3 %all-to-all-start.1 = ((bf16[32,32,640]{2,1,0:T(8,128)(2,1)}), bf16[32,32,640]{2,1,0:T(8,128)(2,1)S(1)}, u32[]{:S(2)}, u32[]{:S(2)}) async-start(bf16[32,32,640]{2,1,0:T(8,128)(2,1)} %bitcast.5), calls=%async_computation.1 | async-start | bytes 2621440 | tf_op jit(solution)/shard_map/all_to_all | solution.py:172
  56.8 7.9 %copy-start.1 = (s32[1024]{0:T(1024)S(1)}, s32[1024]{0:T(1024)}, u32[]{:S(2)}) copy-start(s32[1024]{0:T(1024)} %param.17) | copy-start | bytes 12292
  56.8 10.0 %copy-start.2 = (bf16[32,8192]{1,0:T(8,128)(2,1)S(1)}, bf16[32,8192]{1,0:T(8,128)(2,1)}, u32[]{:S(2)}) copy-start(bf16[32,8192]{1,0:T(8,128)(2,1)} %param.10) | copy-start | bytes 1572868
  64.6 33.7 %copy-start.7 = (s32[64]{0:T(128)}, s32[64]{0:T(128)S(1)}, u32[]{:S(2)}) copy-start(s32[64]{0:T(128)S(1)} %select_reduce_fusion.parent_ref) | copy-start | bytes 772
  89.8 17.6 %all-to-all-start.2 = ((bf16[32,2,10,128]{3,1,2,0:T(2,128)(2,1)}), bf16[32,2,10,128]{3,1,2,0:T(2,128)(2,1)S(1)}, u32[]{:S(2)}, u32[]{:S(2)}) async-start(bf16[32,2,10,128]{3,1,2,0:T(2,128)(2,1)} %copy.44), calls=%async_computation.2 | async-start | bytes 327680 | tf_op jit(solution)/shard_map/all_to_all | solution.py:231
  128.7 15.4 %all-to-all-start.3 = ((bf16[32,2,1024]{2,1,0:T(2,128)(2,1)}), bf16[32,2,1024]{2,1,0:T(2,128)(2,1)S(1)}, u32[]{:S(2)}, u32[]{:S(2)}) async-start(bf16[32,2,1024]{2,1,0:T(2,128)(2,1)} %reshape.409), calls=%async_computation.3 | async-start | bytes 262144 | tf_op jit(solution)/shard_map/all_to_all | solution.py:251

commit v4 on v3

--- a/solution.py
+++ b/solution.py
@@ -10,6 +10,9 @@
 
 HEAD_DIM = 128
 SLOTS_PER_STEP = 8
+PLANE_Y = 4
+DP = ("dy", "dz")
+TP = ("tx", "tc")
 
 
 def rotate(vectors, position):
@@ -121,9 +124,8 @@
     parent_beam,
     beam_alive,
 ):
-    device_count = lax.axis_size("dp")
-    device_rank = lax.axis_index("dp")
-    tensor_count = lax.axis_size("tensor")
+    device_count = lax.axis_size(DP)
+    device_rank = lax.axis_index(DP)
     local_beams = hidden_in.shape[0]
     capacity = max(2, (2 * local_beams + device_count - 1) // device_count)
     slot_total = device_count * capacity
@@ -148,8 +150,8 @@
         axis=1,
     )
     mine = jnp.where(is_low, low_cols, high_cols)
-    received = lax.ppermute(jnp.where(is_low, high_cols, low_cols), "dp", partner)
-    partner_gain = lax.ppermute(norm_gain, "dp", partner)
+    received = lax.ppermute(jnp.where(is_low, high_cols, low_cols), DP, partner)
+    partner_gain = lax.ppermute(norm_gain, DP, partner)
     pair_weight = jnp.where(
         is_low, jnp.concatenate([mine, received], 0), jnp.concatenate([received, mine], 0)
     )
@@ -161,7 +163,7 @@
     spread = jnp.swapaxes(
         jnp.repeat(hidden_in.reshape(local_beams, pair_count, 2 * features), 2, axis=1), 0, 1
     )
-    blocked = lax.all_to_all(spread, "dp", 0, 0, tiled=True).reshape(
+    blocked = lax.all_to_all(spread, DP, 0, 0, tiled=True).reshape(
         device_count * local_beams, 2 * features
     )
     scaled = (blocked.astype(jnp.float32) * pair_gain.astype(jnp.float32)[None, :]).astype(
@@ -171,7 +173,7 @@
     half_width = partial.shape[1]
     arrived = lax.all_to_all(
         partial.astype(jnp.bfloat16).reshape(device_count, local_beams, half_width),
-        "dp",
+        DP,
         0,
         0,
         tiled=True,
@@ -229,7 +231,7 @@
         filled[:, None, None], jnp.take(packed, sender, axis=0), jnp.zeros_like(packed[:1])
     )
     incoming = lax.all_to_all(
-        outgoing.reshape(device_count, capacity, rows, HEAD_DIM), "dp", 0, 0, tiled=True
+        outgoing.reshape(device_count, capacity, rows, HEAD_DIM), DP, 0, 0, tiled=True
     ).reshape(slot_total, rows, HEAD_DIM)
 
     all_parents = parent_beam.reshape(device_count, local_beams)
@@ -249,42 +251,51 @@
 
     mixed = attend_slots(incoming, cache_rows, local_parent, slot_length)
     returned = lax.all_to_all(
-        mixed.reshape(device_count, capacity, head_count * HEAD_DIM), "dp", 0, 0, tiled=True
+        mixed.reshape(device_count, capacity, head_count * HEAD_DIM), DP, 0, 0, tiled=True
     ).reshape(slot_total, head_count * HEAD_DIM)
     attention = jnp.take(returned, target, axis=0)
     attention = jnp.where(my_alive[:, None] > 0, attention, jnp.zeros_like(attention))
 
     spread = jnp.broadcast_to(attention[None], (device_count,) + attention.shape)
-    gathered = lax.all_to_all(spread, "dp", 0, 0, tiled=True).reshape(
+    gathered = lax.all_to_all(spread, DP, 0, 0, tiled=True).reshape(
         device_count * local_beams, head_count * HEAD_DIM
     )
     partial_sum = jnp.dot(gathered, output_weight, preferred_element_type=jnp.float32)
     total_rows, out_width = partial_sum.shape
-    reduced = jnp.sum(
+    core_count = lax.axis_size("tc")
+    ring_count = lax.axis_size("tx")
+    on_chip = jnp.sum(
         lax.all_to_all(
-            partial_sum.reshape(tensor_count, total_rows // tensor_count, out_width),
-            "tensor",
-            0,
-            0,
-            tiled=True,
+            partial_sum.reshape(core_count, total_rows // core_count, out_width), "tc", 0, 0, tiled=True
         ),
         axis=0,
+    )
+    chunk_rows = total_rows // (core_count * ring_count)
+    reduced = jnp.sum(
+        lax.all_to_all(on_chip.reshape(ring_count, chunk_rows, out_width), "tx", 0, 0, tiled=True),
+        axis=0,
     ).astype(jnp.bfloat16)
-    copies = jnp.broadcast_to(reduced[None], (tensor_count,) + reduced.shape)
-    return lax.all_to_all(copies, "tensor", 0, 0, tiled=True).reshape(total_rows, out_width)
-
+    ring_copies = lax.all_to_all(
+        jnp.broadcast_to(reduced[None], (ring_count,) + reduced.shape), "tx", 0, 0, tiled=True
+    ).reshape(ring_count * chunk_rows, out_width)
+    return lax.all_to_all(
+        jnp.broadcast_to(ring_copies[None], (core_count,) + ring_copies.shape), "tc", 0, 0, tiled=True
+    ).reshape(total_rows, out_width)
 
 def solution(mesh):
+    y_count = PLANE_Y
+    devices = mesh.devices.reshape(y_count, mesh.devices.shape[0] // y_count, -1, 2)
+    mesh = jax.sharding.Mesh(devices, ("dy", "dz", "tx", "tc"))
     placed = (
-        P("dp", None),
-        P("dp"),
-        P("dp", "tensor"),
-        P("dp", "tensor"),
-        P("dp", "tensor"),
-        P("tensor", "dp"),
-        P("dp", None, None, "tensor", None),
+        P(DP, None),
+        P(DP),
+        P(DP, TP),
+        P(DP, TP),
+        P(DP, TP),
+        P(TP, DP),
+        P(DP, None, None, TP, None),
         P(),
         P(),
         P(),
     )
-    return jax.shard_map(body, mesh=mesh, in_specs=placed, out_specs=P(None, "dp"), check_vma=False)
+    return jax.shard_map(body, mesh=mesh, in_specs=placed, out_specs=P(None, DP), check_vma=False)

time: 235 us -> 236 us (level)
    all_to_all x3 -> x5, blocking collectives: 87.5 us -> 86.9 us  [the longest x1 47.6 us: body(): lax.all_to_all(spread, DP, 0, 0, tiled=True)]
where the time goes in v4:
time: 236 us; the launch traced here: 235 us
  blocking collectives  86.9 us (37%)
  waiting for transfers between devices  64.6 us (27%)
  starting transfers between devices  39.1 us (17%)
  Pallas kernels  18.1 us (8%)
  local copies, waits for them, and re-layouts  17.7 us (8%)
  other arithmetic  5.31 us (2%)
  matrix products  2.79 us (1%)
    all_to_all x1, blocking collectives, body(): lax.all_to_all(spread, DP, 0, 0, tiled=True)  47.6 us
    all_to_all x1, waiting for transfers between devices, body(): lax.all_to_all(partial.astype(jnp.bfloat16).reshape(device_count, local_b...  19.8 us
    ppermute x1, waiting for transfers between devices, body(): partner_gain = lax.ppermute(norm_gain, DP, partner)  19.5 us
    pallas_call x1, Pallas kernels, attend_slots(): pl.pallas_call(attend_kernel, grid_spec=grid_spec, out_shape=jax.ShapeDty...  18.1 us
    all_to_all x1, blocking collectives, body(): lax.all_to_all(on_chip.reshape(ring_count, chunk_rows, out_width), 'tx',...  12.4 us
    all_to_all x1, blocking collectives, body(): lax.all_to_all(partial_sum.reshape(core_count, total_rows // core_count,...  12.3 us
    all_to_all x1, starting transfers between devices, body(): lax.all_to_all(spread, DP, 0, 0, tiled=True)  12.2 us
    all_to_all x1, starting transfers between devices, body(): lax.all_to_all(partial.astype(jnp.bfloat16).reshape(device_count, local_b...  8.8 us
  transfers between devices with their start and end apart: 6, of which 5 were waited for; matrix products, arithmetic and copies ran while one was open for 6% of the time, Pallas kernels for 0%

profile of v4, /device:TPU:1, one launch (start us, length us, event | category | flops | bytes accessed | tf_op | source)
XLA Modules:
  0.0 234.9 jit_solution(3577245659701067013)
XLA Ops:
  0.0 1.1 copy.49
  1.2 0.0 copy-start.8
  1.2 0.0 copy-start.5
  1.2 0.0 copy-start.3
  1.2 1.1 broadcast_in_dim.146
  2.3 12.2 %all-to-all-start = ((bf16[32,32,512]{2,1,0:T(8,128)(2,1)}), bf16[32,32,512]{2,1,0:T(8,128)(2,1)S(1)}, u32[]{:S(2)}, u32[]{:S(2)}) async-start(bf16[32,32,512]{2,1,0:T(8,128)(2,1)} %bitcast.3), calls=%async_computation | async-start | bytes 2097152 | tf_op jit(solution)/shard_map/all_to_all | solution.py:166
  14.5 1.3 collective-permute-start
  15.8 0.1 fusion.34
  16.0 0.2 broadcast_select_fusion.1
  16.2 0.3 collective-permute-start.1
  16.5 0.1 reshape.403
  16.6 0.1 compare_select_fusion.4
  16.7 0.2 convert_reduce_fusion.2
  16.9 0.8 convert_reduce_fusion.1
  17.6 0.1 broadcast_add_fusion
  17.7 19.5 %collective-permute-done = bf16[256]{0:T(256)(128)(2,1)S(1)} collective-permute-done((bf16[256]{0:T(256)(128)(2,1)S(1)}, bf16[256]{0:T(256)(128)(2,1)S(1)}, u32[]{:S(2)}, u32[]{:S(2)}) %collective-permute-start) | collective-permute-done | bytes 544 | tf_op jit(solution)/shard_map/ppermute | solution.py:154
  37.2 8.4 %collective-permute-done.1 = bf16[256,640]{1,0:T(8,128)(2,1)S(1)} collective-permute-done((bf16[256,640]{1,0:T(8,128)(2,1)S(1)}, bf16[256,640]{1,0:T(8,128)(2,1)S(1)}, u32[]{:S(2)}, u32[]{:S(2)}) %collective-permute-start.1) | collective-permute-done | bytes 327712 | tf_op jit(solution)/shard_map/ppermute | solution.py:153
  45.6 2.1 convolution_convert_fusion
  47.7 8.8 %all-to-all-start.1 = ((bf16[32,32,640]{2,1,0:T(8,128)(2,1)}), bf16[32,32,640]{2,1,0:T(8,128)(2,1)S(1)}, u32[]{:S(2)}, u32[]{:S(2)}) async-start(bf16[32,32,640]{2,1,0:T(8,128)(2,1)} %bitcast.5), calls=%async_computation.1 | async-start | bytes 2621440 | tf_op jit(solution)/shard_map/all_to_all | solution.py:174
  56.5 0.1 fusion.21
  56.6 0.1 add.127
  56.7 0.1 broadcast_in_dim.142
  56.8 7.7 %reshape.409.refs_0_.refs_1_.refs_2_.refs_3_.refs_4_.refs_5_.refs_6_.refs_7_ = bf16[32,256,256]{2,1,0:T(8,128)(2,1)} reshape(bf16[32,256,2,1,128]{4,2,3,1,0:T(2,128)(2,1)} %param.16) | data formatting | bytes 8388608 | tf_op jit(solution)/shard_map/reshape | solution.py:196
  64.5 0.1 select_reduce_fusion.parent_ref
  64.6 0.7 gather_fusion
  65.4 0.7 gather_fusion.1
  66.1 0.6 iota_reduce_fusion
  66.7 0.1 broadcast_in_dim.144
  66.8 0.2 multiply_reduce_fusion
  67.1 0.1 multiply_cosine_fusion.1
  67.2 19.8 %all-to-all-done.1 = bf16[32,32,640]{2,1,0:T(8,128)(2,1)S(1)} async-done(((bf16[32,32,640]{2,1,0:T(8,128)(2,1)}), bf16[32,32,640]{2,1,0:T(8,128)(2,1)S(1)}, u32[]{:S(2)}, u32[]{:S(2)}) %all-to-all-start.1) | async-done | bytes 1310752 | tf_op jit(solution)/shard_map/all_to_all | solution.py:174
  87.0 0.2 convert_reduce_fusion
  87.2 0.1 slice_bitcast_fusion.3
  87.3 0.1 concatenate.54
  87.4 0.1 broadcast_multiply_fusion
  87.5 0.1 fusion.17
  87.6 0.1 pad_maximum_fusion.3
  87.8 0.1 subtract_convert_fusion
  87.9 0.1 pad_maximum_fusion.2
  88.0 0.6 gather_fusion.2
  88.7 0.4 broadcast_select_fusion.3
  89.0 0.8 copy.44
  89.8 8.4 %all-to-all-start.2 = ((bf16[32,2,10,128]{3,1,2,0:T(2,128)(2,1)}), bf16[32,2,10,128]{3,1,2,0:T(2,128)(2,1)S(1)}, u32[]{:S(2)}, u32[]{:S(2)}) async-start(bf16[32,2,10,128]{3,1,2,0:T(2,128)(2,1)} %copy.44), calls=%async_computation.2 | async-start | bytes 327680 | tf_op jit(solution)/shard_map/all_to_all | solution.py:233
  98.2 0.1 fusion.11
  98.3 0.6 fusion.29.length_ref
  98.9 8.6 %all-to-all-done.2 = bf16[32,2,10,128]{3,1,2,0:T(2,128)(2,1)S(1)} async-done(((bf16[32,2,10,128]{3,1,2,0:T(2,128)(2,1)}), bf16[32,2,10,128]{3,1,2,0:T(2,128)(2,1)S(1)}, u32[]{:S(2)}, u32[]{:S(2)}) %all-to-all-start.2) | async-done | bytes 163872 | tf_op jit(solution)/shard_map/all_to_all | solution.py:233
  107.5 0.7 copy.45
  108.2 18.1 %shard_map.100 = bf16[64,8,128]{2,1,0:T(8,128)(2,1)} custom-call(s32[64]{0:T(128)} %copy-done.7, s32[64]{0:T(128)} %fusion.29.length_ref, bf16[64,10,128]{2,1,0:T(8,128)(2,1)} %bitcast.54, bf16[32,256,256]{2,1,0:T(8,128)(2,1)} %reshape.409.refs_0_.refs_1_.refs_2_.refs_3_.refs_4_.refs_5_.refs_6_.refs_7_, ...), custom_call_target="tpu_custom_call" | custom-call | tf_op jit(solution)/shard_map/pallas_call | solution.py:108
  126.3 1.6 reshape.413
  127.8 8.2 %all-to-all-start.3 = ((bf16[32,2,1024]{2,1,0:T(2,128)(2,1)}), bf16[32,2,1024]{2,1,0:T(2,128)(2,1)S(1)}, u32[]{:S(2)}, u32[]{:S(2)}) async-start(bf16[32,2,1024]{2,1,0:T(2,128)(2,1)} %reshape.413), calls=%async_computation.3 | async-start | bytes 262144 | tf_op jit(solution)/shard_map/all_to_all | solution.py:253
  136.0 0.8 dynamic-slice_compare_fusion
  136.8 8.4 %all-to-all-done.3 = bf16[32,2,1024]{2,1,0:T(2,128)(2,1)S(1)} async-done(((bf16[32,2,1024]{2,1,0:T(2,128)(2,1)}), bf16[32,2,1024]{2,1,0:T(2,128)(2,1)S(1)}, u32[]{:S(2)}, u32[]{:S(2)}) %all-to-all-start.3) | async-done | bytes 131104 | tf_op jit(solution)/shard_map/all_to_all | solution.py:253
  145.2 0.1 reshape.414
  145.2 0.6 gather_fusion.3
  145.9 0.1 select_select_fusion
  146.0 0.2 broadcast_in_dim.155
  146.2 47.6 %all_to_all.45 = bf16[32,32,1024]{2,1,0:T(8,128)(2,1)S(1)} all-to-all(bf16[32,32,1024]{2,1,0:T(8,128)(2,1)S(1)} %broadcast_in_dim.155), channel_id=1, replica_groups=mesh['dy'=4,'dz'=8,'tx'=4,'tc'=2] {'dy','dz'}, dimensions={0} | all-to-all | bytes 4194304 | tf_op jit(solution)/shard_map/all_to_all | solution.py:260
  193.8 0.7 fusion.9
  194.5 12.3 %all_to_all.46 = f32[2,512,256]{2,1,0:T(8,128)S(1)} all-to-all(f32[2,512,256]{2,1,0:T(8,128)S(1)} %fusion.9), channel_id=1, replica_groups=mesh['dy'=4,'dz'=8,'tx'=4,'tc'=2] {'tc'}, dimensions={0} | all-to-all | bytes 2097152 | tf_op jit(solution)/shard_map/all_to_all | solution.py:268
  206.8 0.1 reduce_sum.68
  206.9 12.4 %all_to_all.47 = f32[4,128,256]{2,1,0:T(8,128)S(1)} all-to-all(f32[4,128,256]{2,1,0:T(8,128)S(1)} %bitcast.51), channel_id=1, replica_groups=mesh['dy'=4,'dz'=8,'tx'=4,'tc'=2] {'tx'}, dimensions={0} | all-to-all | bytes 1048576 | tf_op jit(solution)/shard_map/all_to_all | solution.py:275
  219.4 7.9 %all_to_all.48 = bf16[4,128,256]{2,1,0:T(8,128)(2,1)S(1)} all-to-all(bf16[4,128,256]{2,1,0:T(8,128)(2,1)S(1)} %broadcast_in_dim.156), channel_id=1, replica_groups=mesh['dy'=4,'dz'=8,'tx'=4,'tc'=2] {'tx'}, dimensions={0} | all-to-all | bytes 524288 | tf_op jit(solution)/shard_map/all_to_all | solution.py:278
  227.4 6.7 %all_to_all.49 = bf16[2,512,256]{2,1,0:T(8,128)(2,1)S(1)} all-to-all(bf16[2,512,256]{2,1,0:T(8,128)(2,1)S(1)} %broadcast_in_dim.158), channel_id=1, replica_groups=mesh['dy'=4,'dz'=8,'tx'=4,'tc'=2] {'tc'}, dimensions={0} | all-to-all | bytes 1048576 | tf_op jit(solution)/shard_map/all_to_all | solution.py:281
  234.1 0.8 copy.51
  (45 shorter events, 0.4 us)
Async XLA Ops:
  0.0 193.8 %copy-start = (bf16[1024,256]{1,0:T(8,128)(2,1)S(1)}, bf16[1024,256]{1,0:T(8,128)(2,1)}, u32[]{:S(2)}) copy-start(bf16[1024,256]{1,0:T(8,128)(2,1)} %param.15) | copy-start | bytes 1572868
  1.2 13.3 %copy-start.8 = (bf16[256]{0:T(256)(128)(2,1)S(1)}, bf16[256]{0:T(256)(128)(2,1)}, u32[]{:S(2)}) copy-start(bf16[256]{0:T(256)(128)(2,1)} %param.11) | copy-start | bytes 1540
  1.2 14.6 %copy-start.4 = (bf16[256,128]{1,0:T(8,128)(2,1)S(1)}, bf16[256,128]{1,0:T(8,128)(2,1)}, u32[]{:S(2)}) copy-start(bf16[256,128]{1,0:T(8,128)(2,1)} %param.13) | copy-start | bytes 196612
  1.2 14.6 %copy-start.5 = (bf16[256,128]{1,0:T(8,128)(2,1)S(1)}, bf16[256,128]{1,0:T(8,128)(2,1)}, u32[]{:S(2)}) copy-start(bf16[256,128]{1,0:T(8,128)(2,1)} %param.14) | copy-start | bytes 196612
  1.2 14.7 %copy-start.3 = (bf16[256,1024]{1,0:T(8,128)(2,1)S(1)}, bf16[256,1024]{1,0:T(8,128)(2,1)}, u32[]{:S(2)}) copy-start(bf16[256,1024]{1,0:T(8,128)(2,1)} %param.12) | copy-start | bytes 1572868
  2.3 14.2 %copy-start.6 = (s32[1024]{0:T(1024)S(1)}, s32[1024]{0:T(1024)}, u32[]{:S(2)}) copy-start(s32[1024]{0:T(1024)} %param.18) | copy-start | bytes 12292
  2.3 43.3 %all-to-all-start = ((bf16[32,32,512]{2,1,0:T(8,128)(2,1)}), bf16[32,32,512]{2,1,0:T(8,128)(2,1)S(1)}, u32[]{:S(2)}, u32[]{:S(2)}) async-start(bf16[32,32,512]{2,1,0:T(8,128)(2,1)} %bitcast.3), calls=%async_computation | async-start | bytes 2097152 | tf_op jit(solution)/shard_map/all_to_all | solution.py:166
  14.5 22.7 %collective-permute-start = (bf16[256]{0:T(256)(128)(2,1)S(1)}, bf16[256]{0:T(256)(128)(2,1)S(1)}, u32[]{:S(2)}, u32[]{:S(2)}) collective-permute-start(bf16[256]{0:T(256)(128)(2,1)S(1)} %copy-done.8), channel_id=1, source_target_pairs={{0,8},{8,0},{16,24},{24,16},{32,40},{40,32},{48,56},{56,48},{64,72... | collective-permute-start | bytes 1544 | tf_op jit(solution)/shard_map/ppermute | solution.py:154
  16.2 29.4 %collective-permute-start.1 = (bf16[256,640]{1,0:T(8,128)(2,1)S(1)}, bf16[256,640]{1,0:T(8,128)(2,1)S(1)}, u32[]{:S(2)}, u32[]{:S(2)}) collective-permute-start(bf16[256,640]{1,0:T(8,128)(2,1)S(1)} %get-tuple-element.14), channel_id=1, source_target_pairs={{0,8},{8,0},{16,24},{24,16},{32,40},{40,32},{48,56},{56,48},{64,72... | collective-permute-start | bytes 983048 | tf_op jit(solution)/shard_map/ppermute | solution.py:153
  47.7 39.3 %all-to-all-start.1 = ((bf16[32,32,640]{2,1,0:T(8,128)(2,1)}), bf16[32,32,640]{2,1,0:T(8,128)(2,1)S(1)}, u32[]{:S(2)}, u32[]{:S(2)}) async-start(bf16[32,32,640]{2,1,0:T(8,128)(2,1)} %bitcast.5), calls=%async_computation.1 | async-start | bytes 2621440 | tf_op jit(solution)/shard_map/all_to_all | solution.py:174
  56.8 7.9 %copy-start.1 = (s32[1024]{0:T(1024)S(1)}, s32[1024]{0:T(1024)}, u32[]{:S(2)}) copy-start(s32[1024]{0:T(1024)} %param.17) | copy-start | bytes 12292
  56.8 10.0 %copy-start.2 = (bf16[32,8192]{1,0:T(8,128)(2,1)S(1)}, bf16[32,8192]{1,0:T(8,128)(2,1)}, u32[]{:S(2)}) copy-start(bf16[32,8192]{1,0:T(8,128)(2,1)} %param.10) | copy-start | bytes 1572868
  64.6 33.7 %copy-start.7 = (s32[64]{0:T(128)}, s32[64]{0:T(128)S(1)}, u32[]{:S(2)}) copy-start(s32[64]{0:T(128)S(1)} %select_reduce_fusion.parent_ref) | copy-start | bytes 772
  89.8 17.6 %all-to-all-start.2 = ((bf16[32,2,10,128]{3,1,2,0:T(2,128)(2,1)}), bf16[32,2,10,128]{3,1,2,0:T(2,128)(2,1)S(1)}, u32[]{:S(2)}, u32[]{:S(2)}) async-start(bf16[32,2,10,128]{3,1,2,0:T(2,128)(2,1)} %copy.44), calls=%async_computation.2 | async-start | bytes 327680 | tf_op jit(solution)/shard_map/all_to_all | solution.py:233
  127.8 17.3 %all-to-all-start.3 = ((bf16[32,2,1024]{2,1,0:T(2,128)(2,1)}), bf16[32,2,1024]{2,1,0:T(2,128)(2,1)S(1)}, u32[]{:S(2)}, u32[]{:S(2)}) async-start(bf16[32,2,1024]{2,1,0:T(2,128)(2,1)} %reshape.413), calls=%async_computation.3 | async-start | bytes 262144 | tf_op jit(solution)/shard_map/all_to_all | solution.py:253

commit v5 on v4

--- a/solution.py
+++ b/solution.py
@@ -256,10 +256,14 @@
     attention = jnp.take(returned, target, axis=0)
     attention = jnp.where(my_alive[:, None] > 0, attention, jnp.zeros_like(attention))
 
-    spread = jnp.broadcast_to(attention[None], (device_count,) + attention.shape)
-    gathered = lax.all_to_all(spread, DP, 0, 0, tiled=True).reshape(
-        device_count * local_beams, head_count * HEAD_DIM
-    )
+    z_count = lax.axis_size("dz")
+    y_count = lax.axis_size("dy")
+    along_z = lax.all_to_all(
+        jnp.broadcast_to(attention[None], (z_count,) + attention.shape), "dz", 0, 0, tiled=True
+    ).reshape(z_count * local_beams, head_count * HEAD_DIM)
+    gathered = lax.all_to_all(
+        jnp.broadcast_to(along_z[None], (y_count,) + along_z.shape), "dy", 0, 0, tiled=True
+    ).reshape(device_count * local_beams, head_count * HEAD_DIM)
     partial_sum = jnp.dot(gathered, output_weight, preferred_element_type=jnp.float32)
     total_rows, out_width = partial_sum.shape
     core_count = lax.axis_size("tc")

time: 236 us -> 224 us (0.949)
  blocking collectives: 86.9 us -> 76.5 us
    all_to_all x1 -> x2, blocking collectives: 47.6 us -> 38.9 us  [the longest x1 23.4 us: body(): lax.all_to_all(jnp.broadcast_to(along_z[None], (y_count,) + along_z.shape...]
where the time goes in v5:
time: 224 us; the launch traced here: 222 us
  blocking collectives  76.5 us (34%)
  waiting for transfers between devices  64.6 us (29%)
  starting transfers between devices  37.3 us (17%)
  local copies, waits for them, and re-layouts  17.7 us (8%)
  Pallas kernels  17.5 us (8%)
  other arithmetic  5.31 us (2%)
  matrix products  2.79 us (1%)
    all_to_all x1, blocking collectives, body(): lax.all_to_all(jnp.broadcast_to(along_z[None], (y_count,) + along_z.shape...  23.4 us
    all_to_all x1, waiting for transfers between devices, body(): lax.all_to_all(partial.astype(jnp.bfloat16).reshape(device_count, local_b...  19.8 us
    ppermute x1, waiting for transfers between devices, body(): partner_gain = lax.ppermute(norm_gain, DP, partner)  19.5 us
    pallas_call x1, Pallas kernels, attend_slots(): pl.pallas_call(attend_kernel, grid_spec=grid_spec, out_shape=jax.ShapeDty...  17.5 us
    all_to_all x1, blocking collectives, body(): lax.all_to_all(jnp.broadcast_to(attention[None], (z_count,) + attention.s...  15.4 us
    all_to_all x1, blocking collectives, body(): lax.all_to_all(on_chip.reshape(ring_count, chunk_rows, out_width), 'tx',...  12.4 us
    all_to_all x1, starting transfers between devices, body(): lax.all_to_all(spread, DP, 0, 0, tiled=True)  12.2 us
    all_to_all x1, blocking collectives, body(): lax.all_to_all(partial_sum.reshape(core_count, total_rows // core_count,...  10.5 us
  transfers between devices with their start and end apart: 6, of which 5 were waited for; matrix products, arithmetic and copies ran while one was open for 6% of the time, Pallas kernels for 0%

profile of v5, /device:TPU:1, one launch (start us, length us, event | category | flops | bytes accessed | tf_op | source)
XLA Modules:
  0.0 222.1 jit_solution(2080174318295372607)
XLA Ops:
  0.0 1.1 copy.49
  1.2 0.0 copy-start.8
  1.2 1.1 broadcast_in_dim.153
  2.3 12.2 %all-to-all-start = ((bf16[32,32,512]{2,1,0:T(8,128)(2,1)}), bf16[32,32,512]{2,1,0:T(8,128)(2,1)S(1)}, u32[]{:S(2)}, u32[]{:S(2)}) async-start(bf16[32,32,512]{2,1,0:T(8,128)(2,1)} %bitcast.3), calls=%async_computation | async-start | bytes 2097152 | tf_op jit(solution)/shard_map/all_to_all | solution.py:166
  14.5 1.3 collective-permute-start
  15.8 0.1 fusion.34
  16.0 0.2 broadcast_select_fusion.1
  16.2 0.3 collective-permute-start.1
  16.5 0.1 reshape.404
  16.6 0.1 compare_select_fusion.4
  16.7 0.2 convert_reduce_fusion.2
  16.9 0.8 convert_reduce_fusion.1
  17.6 0.1 broadcast_add_fusion
  17.7 19.5 %collective-permute-done = bf16[256]{0:T(256)(128)(2,1)S(1)} collective-permute-done((bf16[256]{0:T(256)(128)(2,1)S(1)}, bf16[256]{0:T(256)(128)(2,1)S(1)}, u32[]{:S(2)}, u32[]{:S(2)}) %collective-permute-start) | collective-permute-done | bytes 544 | tf_op jit(solution)/shard_map/ppermute | solution.py:154
  37.2 8.4 %collective-permute-done.1 = bf16[256,640]{1,0:T(8,128)(2,1)S(1)} collective-permute-done((bf16[256,640]{1,0:T(8,128)(2,1)S(1)}, bf16[256,640]{1,0:T(8,128)(2,1)S(1)}, u32[]{:S(2)}, u32[]{:S(2)}) %collective-permute-start.1) | collective-permute-done | bytes 327712 | tf_op jit(solution)/shard_map/ppermute | solution.py:153
  45.6 2.1 convolution_convert_fusion
  47.7 8.8 %all-to-all-start.1 = ((bf16[32,32,640]{2,1,0:T(8,128)(2,1)}), bf16[32,32,640]{2,1,0:T(8,128)(2,1)S(1)}, u32[]{:S(2)}, u32[]{:S(2)}) async-start(bf16[32,32,640]{2,1,0:T(8,128)(2,1)} %bitcast.5), calls=%async_computation.1 | async-start | bytes 2621440 | tf_op jit(solution)/shard_map/all_to_all | solution.py:174
  56.5 0.1 fusion.21
  56.6 0.1 add.127
  56.7 0.1 broadcast_in_dim.149
  56.8 7.7 %reshape.410.refs_0_.refs_1_.refs_2_.refs_3_.refs_4_.refs_5_.refs_6_.refs_7_ = bf16[32,256,256]{2,1,0:T(8,128)(2,1)} reshape(bf16[32,256,2,1,128]{4,2,3,1,0:T(2,128)(2,1)} %param.16) | data formatting | bytes 8388608 | tf_op jit(solution)/shard_map/reshape | solution.py:196
  64.5 0.1 select_reduce_fusion.parent_ref
  64.6 0.7 gather_fusion
  65.4 0.7 gather_fusion.1
  66.1 0.6 iota_reduce_fusion
  66.7 0.1 broadcast_in_dim.151
  66.8 0.2 multiply_reduce_fusion
  67.1 0.1 multiply_cosine_fusion.1
  67.2 19.8 %all-to-all-done.1 = bf16[32,32,640]{2,1,0:T(8,128)(2,1)S(1)} async-done(((bf16[32,32,640]{2,1,0:T(8,128)(2,1)}), bf16[32,32,640]{2,1,0:T(8,128)(2,1)S(1)}, u32[]{:S(2)}, u32[]{:S(2)}) %all-to-all-start.1) | async-done | bytes 1310752 | tf_op jit(solution)/shard_map/all_to_all | solution.py:174
  87.0 0.2 convert_reduce_fusion
  87.2 0.1 slice_bitcast_fusion.3
  87.3 0.1 concatenate.54
  87.4 0.1 broadcast_multiply_fusion
  87.5 0.1 fusion.17
  87.6 0.1 pad_maximum_fusion.3
  87.8 0.1 subtract_convert_fusion
  87.9 0.1 pad_maximum_fusion.2
  88.0 0.6 gather_fusion.2
  88.7 0.4 broadcast_select_fusion.3
  89.0 0.8 copy.44
  89.8 8.4 %all-to-all-start.2 = ((bf16[32,2,10,128]{3,1,2,0:T(2,128)(2,1)}), bf16[32,2,10,128]{3,1,2,0:T(2,128)(2,1)S(1)}, u32[]{:S(2)}, u32[]{:S(2)}) async-start(bf16[32,2,10,128]{3,1,2,0:T(2,128)(2,1)} %copy.44), calls=%async_computation.2 | async-start | bytes 327680 | tf_op jit(solution)/shard_map/all_to_all | solution.py:233
  98.2 0.1 fusion.11
  98.3 0.6 fusion.29.length_ref
  98.9 8.6 %all-to-all-done.2 = bf16[32,2,10,128]{3,1,2,0:T(2,128)(2,1)S(1)} async-done(((bf16[32,2,10,128]{3,1,2,0:T(2,128)(2,1)}), bf16[32,2,10,128]{3,1,2,0:T(2,128)(2,1)S(1)}, u32[]{:S(2)}, u32[]{:S(2)}) %all-to-all-start.2) | async-done | bytes 163872 | tf_op jit(solution)/shard_map/all_to_all | solution.py:233
  107.5 0.7 copy.45
  108.2 17.5 %shard_map.100 = bf16[64,8,128]{2,1,0:T(8,128)(2,1)} custom-call(s32[64]{0:T(128)} %copy-done.7, s32[64]{0:T(128)} %fusion.29.length_ref, bf16[64,10,128]{2,1,0:T(8,128)(2,1)} %bitcast.56, bf16[32,256,256]{2,1,0:T(8,128)(2,1)} %reshape.410.refs_0_.refs_1_.refs_2_.refs_3_.refs_4_.refs_5_.refs_6_.refs_7_, ...), custom_call_target="tpu_custom_call" | custom-call | tf_op jit(solution)/shard_map/pallas_call | solution.py:108
  125.7 1.6 reshape.414
  127.3 6.3 %all-to-all-start.3 = ((bf16[32,2,1024]{2,1,0:T(2,128)(2,1)}), bf16[32,2,1024]{2,1,0:T(2,128)(2,1)S(1)}, u32[]{:S(2)}, u32[]{:S(2)}) async-start(bf16[32,2,1024]{2,1,0:T(2,128)(2,1)} %reshape.414), calls=%async_computation.3 | async-start | bytes 262144 | tf_op jit(solution)/shard_map/all_to_all | solution.py:253
  133.7 0.8 dynamic-slice_compare_fusion
  134.4 8.4 %all-to-all-done.3 = bf16[32,2,1024]{2,1,0:T(2,128)(2,1)S(1)} async-done(((bf16[32,2,1024]{2,1,0:T(2,128)(2,1)}), bf16[32,2,1024]{2,1,0:T(2,128)(2,1)S(1)}, u32[]{:S(2)}, u32[]{:S(2)}) %all-to-all-start.3) | async-done | bytes 131104 | tf_op jit(solution)/shard_map/all_to_all | solution.py:253
  142.8 0.1 reshape.415
  142.9 0.6 gather_fusion.3
  143.5 0.1 select_select_fusion
  143.6 0.1 broadcast_in_dim.162
  143.6 15.4 %all_to_all.50 = bf16[8,32,1024]{2,1,0:T(8,128)(2,1)S(1)} all-to-all(bf16[8,32,1024]{2,1,0:T(8,128)(2,1)S(1)} %broadcast_in_dim.162), channel_id=1, replica_groups=mesh['dy'=4,'dz'=8,'tx'=4,'tc'=2] {'dz'}, dimensions={0} | all-to-all | bytes 1048576 | tf_op jit(solution)/shard_map/all_to_all | solution.py:261
  159.1 0.3 broadcast_in_dim.164
  159.3 23.4 %all_to_all.51 = bf16[4,256,1024]{2,1,0:T(8,128)(2,1)S(1)} all-to-all(bf16[4,256,1024]{2,1,0:T(8,128)(2,1)S(1)} %broadcast_in_dim.164), channel_id=1, replica_groups=mesh['dy'=4,'dz'=8,'tx'=4,'tc'=2] {'dy'}, dimensions={0} | all-to-all | bytes 4194304 | tf_op jit(solution)/shard_map/all_to_all | solution.py:264
  182.8 0.7 fusion.9
  183.5 10.5 %all_to_all.52 = f32[2,512,256]{2,1,0:T(8,128)S(1)} all-to-all(f32[2,512,256]{2,1,0:T(8,128)S(1)} %fusion.9), channel_id=1, replica_groups=mesh['dy'=4,'dz'=8,'tx'=4,'tc'=2] {'tc'}, dimensions={0} | all-to-all | bytes 2097152 | tf_op jit(solution)/shard_map/all_to_all | solution.py:272
  194.0 0.1 reduce_sum.68
  194.1 12.4 %all_to_all.53 = f32[4,128,256]{2,1,0:T(8,128)S(1)} all-to-all(f32[4,128,256]{2,1,0:T(8,128)S(1)} %bitcast.53), channel_id=1, replica_groups=mesh['dy'=4,'dz'=8,'tx'=4,'tc'=2] {'tx'}, dimensions={0} | all-to-all | bytes 1048576 | tf_op jit(solution)/shard_map/all_to_all | solution.py:279
  206.6 7.9 %all_to_all.54 = bf16[4,128,256]{2,1,0:T(8,128)(2,1)S(1)} all-to-all(bf16[4,128,256]{2,1,0:T(8,128)(2,1)S(1)} %broadcast_in_dim.165), channel_id=1, replica_groups=mesh['dy'=4,'dz'=8,'tx'=4,'tc'=2] {'tx'}, dimensions={0} | all-to-all | bytes 524288 | tf_op jit(solution)/shard_map/all_to_all | solution.py:282
  214.6 6.7 %all_to_all.55 = bf16[2,512,256]{2,1,0:T(8,128)(2,1)S(1)} all-to-all(bf16[2,512,256]{2,1,0:T(8,128)(2,1)S(1)} %broadcast_in_dim.167), channel_id=1, replica_groups=mesh['dy'=4,'dz'=8,'tx'=4,'tc'=2] {'tc'}, dimensions={0} | all-to-all | bytes 1048576 | tf_op jit(solution)/shard_map/all_to_all | solution.py:285
  221.3 0.8 copy.51
  (47 shorter events, 0.4 us)
Async XLA Ops:
  0.0 182.8 %copy-start = (bf16[1024,256]{1,0:T(8,128)(2,1)S(1)}, bf16[1024,256]{1,0:T(8,128)(2,1)}, u32[]{:S(2)}) copy-start(bf16[1024,256]{1,0:T(8,128)(2,1)} %param.15) | copy-start | bytes 1572868
  1.2 13.3 %copy-start.8 = (bf16[256]{0:T(256)(128)(2,1)S(1)}, bf16[256]{0:T(256)(128)(2,1)}, u32[]{:S(2)}) copy-start(bf16[256]{0:T(256)(128)(2,1)} %param.11) | copy-start | bytes 1540
  1.2 14.6 %copy-start.4 = (bf16[256,128]{1,0:T(8,128)(2,1)S(1)}, bf16[256,128]{1,0:T(8,128)(2,1)}, u32[]{:S(2)}) copy-start(bf16[256,128]{1,0:T(8,128)(2,1)} %param.13) | copy-start | bytes 196612
  1.2 14.6 %copy-start.5 = (bf16[256,128]{1,0:T(8,128)(2,1)S(1)}, bf16[256,128]{1,0:T(8,128)(2,1)}, u32[]{:S(2)}) copy-start(bf16[256,128]{1,0:T(8,128)(2,1)} %param.14) | copy-start | bytes 196612
  1.2 14.7 %copy-start.3 = (bf16[256,1024]{1,0:T(8,128)(2,1)S(1)}, bf16[256,1024]{1,0:T(8,128)(2,1)}, u32[]{:S(2)}) copy-start(bf16[256,1024]{1,0:T(8,128)(2,1)} %param.12) | copy-start | bytes 1572868
  2.3 14.2 %copy-start.6 = (s32[1024]{0:T(1024)S(1)}, s32[1024]{0:T(1024)}, u32[]{:S(2)}) copy-start(s32[1024]{0:T(1024)} %param.18) | copy-start | bytes 12292
  2.3 43.3 %all-to-all-start = ((bf16[32,32,512]{2,1,0:T(8,128)(2,1)}), bf16[32,32,512]{2,1,0:T(8,128)(2,1)S(1)}, u32[]{:S(2)}, u32[]{:S(2)}) async-start(bf16[32,32,512]{2,1,0:T(8,128)(2,1)} %bitcast.3), calls=%async_computation | async-start | bytes 2097152 | tf_op jit(solution)/shard_map/all_to_all | solution.py:166
  14.5 22.7 %collective-permute-start = (bf16[256]{0:T(256)(128)(2,1)S(1)}, bf16[256]{0:T(256)(128)(2,1)S(1)}, u32[]{:S(2)}, u32[]{:S(2)}) collective-permute-start(bf16[256]{0:T(256)(128)(2,1)S(1)} %copy-done.8), channel_id=1, source_target_pairs={{0,8},{8,0},{16,24},{24,16},{32,40},{40,32},{48,56},{56,48},{64,72... | collective-permute-start | bytes 1544 | tf_op jit(solution)/shard_map/ppermute | solution.py:154
  16.2 29.4 %collective-permute-start.1 = (bf16[256,640]{1,0:T(8,128)(2,1)S(1)}, bf16[256,640]{1,0:T(8,128)(2,1)S(1)}, u32[]{:S(2)}, u32[]{:S(2)}) collective-permute-start(bf16[256,640]{1,0:T(8,128)(2,1)S(1)} %get-tuple-element.14), channel_id=1, source_target_pairs={{0,8},{8,0},{16,24},{24,16},{32,40},{40,32},{48,56},{56,48},{64,72... | collective-permute-start | bytes 983048 | tf_op jit(solution)/shard_map/ppermute | solution.py:153
  47.7 39.3 %all-to-all-start.1 = ((bf16[32,32,640]{2,1,0:T(8,128)(2,1)}), bf16[32,32,640]{2,1,0:T(8,128)(2,1)S(1)}, u32[]{:S(2)}, u32[]{:S(2)}) async-start(bf16[32,32,640]{2,1,0:T(8,128)(2,1)} %bitcast.5), calls=%async_computation.1 | async-start | bytes 2621440 | tf_op jit(solution)/shard_map/all_to_all | solution.py:174
  56.8 7.9 %copy-start.1 = (s32[1024]{0:T(1024)S(1)}, s32[1024]{0:T(1024)}, u32[]{:S(2)}) copy-start(s32[1024]{0:T(1024)} %param.17) | copy-start | bytes 12292
  56.8 10.0 %copy-start.2 = (bf16[32,8192]{1,0:T(8,128)(2,1)S(1)}, bf16[32,8192]{1,0:T(8,128)(2,1)}, u32[]{:S(2)}) copy-start(bf16[32,8192]{1,0:T(8,128)(2,1)} %param.10) | copy-start | bytes 1572868
  64.6 33.7 %copy-start.7 = (s32[64]{0:T(128)}, s32[64]{0:T(128)S(1)}, u32[]{:S(2)}) copy-start(s32[64]{0:T(128)S(1)} %select_reduce_fusion.parent_ref) | copy-start | bytes 772
  89.8 17.6 %all-to-all-start.2 = ((bf16[32,2,10,128]{3,1,2,0:T(2,128)(2,1)}), bf16[32,2,10,128]{3,1,2,0:T(2,128)(2,1)S(1)}, u32[]{:S(2)}, u32[]{:S(2)}) async-start(bf16[32,2,10,128]{3,1,2,0:T(2,128)(2,1)} %copy.44), calls=%async_computation.2 | async-start | bytes 327680 | tf_op jit(solution)/shard_map/all_to_all | solution.py:233
  127.3 15.5 %all-to-all-start.3 = ((bf16[32,2,1024]{2,1,0:T(2,128)(2,1)}), bf16[32,2,1024]{2,1,0:T(2,128)(2,1)S(1)}, u32[]{:S(2)}, u32[]{:S(2)}) async-start(bf16[32,2,1024]{2,1,0:T(2,128)(2,1)} %reshape.414), calls=%async_computation.3 | async-start | bytes 262144 | tf_op jit(solution)/shard_map/all_to_all | solution.py:253

commit v6 on v5

--- a/solution.py
+++ b/solution.py
@@ -39,9 +39,10 @@
 
 
 def attend_kernel(parent_ref, length_ref, packed_ref, *refs):
-    cache_refs = refs[:-1]
     out_ref = refs[-1]
-    group = len(cache_refs)
+    group = (len(refs) - 1) // 2
+    key_refs = refs[:group]
+    value_refs = refs[group : 2 * group]
     step = pl.program_id(0)
     head_width = packed_ref.shape[-1]
     head_total = packed_ref.shape[1] - 2
@@ -54,25 +55,19 @@
 
         @pl.when(length > 0)
         def _():
-            attend_one(packed_ref, cache_refs[g], out_ref, g, length, head_total, head_width)
-
-
-def attend_one(packed_ref, cache_ref, out_ref, g, length, head_total, head_width):
+            attend_one(packed_ref, key_refs[g], value_refs[g], out_ref, g, length, head_total, head_width)
+
+
+def attend_one(packed_ref, key_ref, value_ref, out_ref, g, length, head_total, head_width):
     score_scale = 1.0 / math.sqrt(head_width)
     if True:
         row = packed_ref[g].astype(jnp.float32)
         queries = row[:head_total].astype(jnp.bfloat16)
         key_new = row[head_total : head_total + 1]
         value_new = row[head_total + 1 : head_total + 2]
-        block = cache_ref[0]
-        keys = block[:, :head_width]
-        values = block[:, head_width:]
-        cached = (
-            lax.dot_general(
-                queries, keys, (((1,), (1,)), ((), ())), preferred_element_type=jnp.float32
-            )
-            * score_scale
-        )
+        keys_t = key_ref[0]
+        values = value_ref[0]
+        cached = jnp.dot(queries, keys_t, preferred_element_type=jnp.float32) * score_scale
         latest = (
             jnp.sum(row[:head_total] * key_new, axis=-1, keepdims=True) * score_scale
         )
@@ -89,11 +84,11 @@
         out_ref[g] = mixture.astype(out_ref.dtype)
 
 
-def attend_slots(packed, cache_rows, parents, lengths):
+def attend_slots(packed, keys_t, values, parents, lengths):
     slot_total, rows, head_width = packed.shape
     head_total = rows - 2
     group = SLOTS_PER_STEP
-    cache_len, row_width = cache_rows.shape[1], cache_rows.shape[2]
+    cache_len = values.shape[1]
 
     def cache_map(g):
         return lambda i, parent_ref, length_ref: (parent_ref[i * group + g], 0, 0)
@@ -102,15 +97,15 @@
         num_scalar_prefetch=2,
         grid=(slot_total // group,),
         in_specs=[pl.BlockSpec((group, rows, head_width), lambda i, p, l: (i, 0, 0))]
-        + [pl.BlockSpec((1, cache_len, row_width), cache_map(g)) for g in range(group)],
+        + [pl.BlockSpec((1, head_width, cache_len), cache_map(g)) for g in range(group)]
+        + [pl.BlockSpec((1, cache_len, head_width), cache_map(g)) for g in range(group)],
         out_specs=pl.BlockSpec((group, head_total, head_width), lambda i, p, l: (i, 0, 0)),
     )
     return pl.pallas_call(
         attend_kernel,
         grid_spec=grid_spec,
         out_shape=jax.ShapeDtypeStruct((slot_total, head_total, head_width), jnp.bfloat16),
-    )(parents, lengths, packed, *([cache_rows] * group))
-
+    )(parents, lengths, packed, *([keys_t] * group), *([values] * group))
 
 def body(
     hidden_in,
@@ -193,10 +188,9 @@
         ],
         axis=1,
     ) * inverse[:, None]
-    cache_rows = key_value_cache.reshape(
-        local_beams, key_value_cache.shape[1], 2 * key_value_cache.shape[-1]
-    )
-    summed, cache_rows = lax.optimization_barrier((summed, cache_rows))
+    keys_t = jnp.swapaxes(key_value_cache[:, :, 0, 0, :], 1, 2)
+    values = key_value_cache[:, :, 1, 0, :]
+    summed, keys_t, values = lax.optimization_barrier((summed, keys_t, values))
 
     first_beam = device_rank * local_beams
     my_parent = lax.dynamic_slice_in_dim(parent_beam, first_beam, local_beams)
@@ -249,7 +243,7 @@
     used = jnp.any(chosen, axis=1).astype(jnp.int32)
     slot_length = jnp.take(cache_lengths, first_beam + local_parent) * used
 
-    mixed = attend_slots(incoming, cache_rows, local_parent, slot_length)
+    mixed = attend_slots(incoming, keys_t, values, local_parent, slot_length)
     returned = lax.all_to_all(
         mixed.reshape(device_count, capacity, head_count * HEAD_DIM), DP, 0, 0, tiled=True
     ).reshape(slot_total, head_count * HEAD_DIM)

time: 224 us -> 221 us (0.987)
  waiting for transfers between devices: 64.6 us -> 45.5 us
  local copies, waits for them, and re-layouts: 17.7 us -> 34.8 us
    ppermute x1, waiting for transfers between devices: 19.5 us -> 0.01 us  [body(): partner_gain = lax.ppermute(norm_gain, DP, partner)]
    all_to_all x1, waiting for transfers between devices: 0.01 us -> 14 us  [body(): lax.all_to_all(spread, DP, 0, 0, tiled=True)]
    unnamed x21 -> x17, local copies, waits for them, and re-layouts: 0.88 us -> 14.5 us
    slice x0 -> x1, local copies, waits for them, and re-layouts: none -> 10.1 us  [body(): values = key_value_cache[:, :, 1, 0, :]]
    ppermute x1, waiting for transfers between devices: 8.42 us -> 0.01 us  [body(): received = lax.ppermute(jnp.where(is_low, high_cols, low_cols), DP, partner)]
    reshape x1 -> x0, local copies, waits for them, and re-layouts: 7.66 us -> none  [body(): key_value_cache.reshape(local_beams, key_value_cache.shape[1], 2 * key_va...]
    all_to_all x1, waiting for transfers between devices: 19.8 us -> 14.6 us  [body(): lax.all_to_all(partial.astype(jnp.bfloat16).reshape(device_count, local_b...]
    all_to_all x1, starting transfers between devices: 6.34 us -> 9.39 us  [body(): lax.all_to_all(mixed.reshape(device_count, capacity, head_count * HEAD_DI...]
  transfers between devices with their start and end apart: 6 -> 6, of which waited for: 5 -> 4; matrix products, arithmetic and copies ran while one was open for 6% -> 14% of each run, Pallas kernels for 0% -> 0%
where the time goes in v6:
time: 221 us; the launch traced here: 220 us
  blocking collectives  76.5 us (35%)
  waiting for transfers between devices  45.5 us (21%)
  starting transfers between devices  38.4 us (17%)
  local copies, waits for them, and re-layouts  34.8 us (16%)
  Pallas kernels  16.7 us (8%)
  other arithmetic  5.29 us (2%)
  matrix products  2.8 us (1%)
    all_to_all x1, blocking collectives, body(): lax.all_to_all(jnp.broadcast_to(along_z[None], (y_count,) + along_z.shape...  23.5 us
    pallas_call x1, Pallas kernels, attend_slots(): pl.pallas_call(attend_kernel, grid_spec=grid_spec, out_shape=jax.ShapeDty...  16.7 us
    all_to_all x1, blocking collectives, body(): lax.all_to_all(jnp.broadcast_to(attention[None], (z_count,) + attention.s...  15.5 us
    all_to_all x1, waiting for transfers between devices, body(): lax.all_to_all(partial.astype(jnp.bfloat16).reshape(device_count, local_b...  14.6 us
    unnamed x17, local copies, waits for them, and re-layouts  14.5 us
    all_to_all x1, waiting for transfers between devices, body(): lax.all_to_all(spread, DP, 0, 0, tiled=True)  14 us
    all_to_all x1, blocking collectives, body(): lax.all_to_all(on_chip.reshape(ring_count, chunk_rows, out_width), 'tx',...  12.4 us
    all_to_all x1, starting transfers between devices, body(): lax.all_to_all(spread, DP, 0, 0, tiled=True)  10.9 us
  transfers between devices with their start and end apart: 6, of which 4 were waited for; matrix products, arithmetic and copies ran while one was open for 14% of the time, Pallas kernels for 0%

profile of v6, /device:TPU:1, one launch (start us, length us, event | category | flops | bytes accessed | tf_op | source)
XLA Modules:
  0.0 220.4 jit_solution(3890891514577086644)
XLA Ops:
  0.0 1.1 fusion.34
  1.2 1.0 fusion.35
  2.2 0.2 broadcast_select_fusion.1
  2.4 2.5 %collective-permute-start.1 = (bf16[256,640]{1,0:T(8,128)(2,1)S(1)}, bf16[256,640]{1,0:T(8,128)(2,1)S(1)}, u32[]{:S(2)}, u32[]{:S(2)}) collective-permute-start(bf16[256,640]{1,0:T(8,128)(2,1)S(1)} %get-tuple-element.18), channel_id=1, source_target_pairs={{0,8},{8,0},{16,24},{24,16},{32,40},{40,32},{48,56},{56,48},{64,72... | collective-permute-start | bytes 983048 | tf_op jit(solution)/shard_map/ppermute | solution.py:148
  5.0 0.1 collective-permute-start
  5.1 1.2 broadcast_in_dim.153
  6.3 10.9 %all-to-all-start = ((bf16[32,32,512]{2,1,0:T(8,128)(2,1)}), bf16[32,32,512]{2,1,0:T(8,128)(2,1)S(1)}, u32[]{:S(2)}, u32[]{:S(2)}) async-start(bf16[32,32,512]{2,1,0:T(8,128)(2,1)} %bitcast.3), calls=%async_computation | async-start | bytes 2097152 | tf_op jit(solution)/shard_map/all_to_all | solution.py:161
  17.3 0.1 compare_select_fusion.4
  17.4 0.2 convert_reduce_fusion.2
  17.6 0.6 iota_reduce_fusion
  18.2 0.1 reshape.401
  18.3 10.1 %fusion.33 = (bf16[32,256,1,1,128]{4,2,3,1,0:T(2,128)(2,1)}, bf16[32,256,1,1,128]{4,2,3,1,0:T(2,128)(2,1)}) fusion(bf16[32,256,2,1,128]{4,2,3,1,0:T(2,128)(2,1)} %param.16), kind=kLoop, calls=%fused_computation.110 | loop fusion | bytes 8388608 | tf_op jit(solution)/shard_map/slice | solution.py:192
  28.4 0.1 fusion.21
  28.5 14.0 %all-to-all-done = bf16[32,32,512]{2,1,0:T(8,128)(2,1)S(1)} async-done(((bf16[32,32,512]{2,1,0:T(8,128)(2,1)}), bf16[32,32,512]{2,1,0:T(8,128)(2,1)S(1)}, u32[]{:S(2)}, u32[]{:S(2)}) %all-to-all-start) | async-done | bytes 1048608 | tf_op jit(solution)/shard_map/all_to_all | solution.py:161
  42.4 2.1 convolution_convert_fusion
  44.5 8.0 %all-to-all-start.1 = ((bf16[32,32,640]{2,1,0:T(8,128)(2,1)}), bf16[32,32,640]{2,1,0:T(8,128)(2,1)S(1)}, u32[]{:S(2)}, u32[]{:S(2)}) async-start(bf16[32,32,640]{2,1,0:T(8,128)(2,1)} %bitcast.75), calls=%async_computation.1 | async-start | bytes 2621440 | tf_op jit(solution)/shard_map/all_to_all | solution.py:169
  52.6 9.8 %copy.62 = bf16[32,256,1,1,128]{1,4,0,3,2:T(8,128)(2,1)} copy(bf16[32,256,1,1,128]{4,2,3,1,0:T(2,128)(2,1)} %get-tuple-element.16) | data formatting | bytes 4194304
  62.4 3.9 %copy.68 = bf16[32,256,1,1,128]{4,1,0,3,2:T(8,128)(2,1)} copy(bf16[32,256,1,1,128]{4,2,3,1,0:T(2,128)(2,1)} %get-tuple-element.15) | data formatting | bytes 4194304
  66.2 0.1 broadcast_in_dim.151
  66.3 0.1 broadcast_in_dim.149
  66.5 0.8 convert_reduce_fusion.1
  67.2 0.1 broadcast_add_fusion
  67.3 0.1 add.127
  67.4 0.7 gather_fusion.1
  68.1 0.1 select_reduce_fusion.parent_ref
  68.3 0.7 gather_fusion
  69.0 0.2 multiply_reduce_fusion
  69.3 0.1 multiply_cosine_fusion.1
  69.4 14.6 %all-to-all-done.1 = bf16[32,32,640]{2,1,0:T(8,128)(2,1)S(1)} async-done(((bf16[32,32,640]{2,1,0:T(8,128)(2,1)}), bf16[32,32,640]{2,1,0:T(8,128)(2,1)S(1)}, u32[]{:S(2)}, u32[]{:S(2)}) %all-to-all-start.1) | async-done | bytes 1310752 | tf_op jit(solution)/shard_map/all_to_all | solution.py:169
  84.0 0.2 convert_reduce_fusion
  84.2 0.1 slice_bitcast_fusion.3
  84.3 0.1 concatenate.54
  84.4 0.1 broadcast_multiply_fusion
  84.5 0.1 fusion.17
  84.7 0.1 pad_maximum_fusion.3
  84.8 0.1 subtract_convert_fusion
  84.9 0.1 pad_maximum_fusion.2
  85.0 0.6 gather_fusion.2
  85.7 0.3 broadcast_select_fusion.3
  86.1 0.8 copy.60
  86.8 7.4 %all-to-all-start.2 = ((bf16[32,2,10,128]{3,1,2,0:T(2,128)(2,1)}), bf16[32,2,10,128]{3,1,2,0:T(2,128)(2,1)S(1)}, u32[]{:S(2)}, u32[]{:S(2)}) async-start(bf16[32,2,10,128]{3,1,2,0:T(2,128)(2,1)} %copy.60), calls=%async_computation.2 | async-start | bytes 327680 | tf_op jit(solution)/shard_map/all_to_all | solution.py:227
  94.2 0.1 fusion.11
  94.4 0.5 fusion.29.length_ref
  94.9 8.6 %all-to-all-done.2 = bf16[32,2,10,128]{3,1,2,0:T(2,128)(2,1)S(1)} async-done(((bf16[32,2,10,128]{3,1,2,0:T(2,128)(2,1)}), bf16[32,2,10,128]{3,1,2,0:T(2,128)(2,1)S(1)}, u32[]{:S(2)}, u32[]{:S(2)}) %all-to-all-start.2) | async-done | bytes 163872 | tf_op jit(solution)/shard_map/all_to_all | solution.py:227
  103.5 0.7 copy.61
  104.2 16.7 %shard_map.100 = bf16[64,8,128]{2,1,0:T(8,128)(2,1)} custom-call(s32[64]{0:T(128)} %copy-done.4, s32[64]{0:T(128)} %fusion.29.length_ref, bf16[64,10,128]{2,1,0:T(8,128)(2,1)} %bitcast.77, bf16[32,128,256]{2,1,0:T(8,128)(2,1)} %bitcast.52, bf16[32,128,256]{2,1,0:T(8,128)(2,1)} %bitcast.53, bf16[32,128,256]{2,1,0:T(8,128)(2,1)} %bitcast.54, ...), custom_call_target="tpu_custom_call" | custom-call | tf_op jit(solution)/shard_map/pallas_call | solution.py:104
  120.9 1.6 reshape.410
  122.5 9.4 %all-to-all-start.3 = ((bf16[32,2,1024]{2,1,0:T(2,128)(2,1)}), bf16[32,2,1024]{2,1,0:T(2,128)(2,1)S(1)}, u32[]{:S(2)}, u32[]{:S(2)}) async-start(bf16[32,2,1024]{2,1,0:T(2,128)(2,1)} %reshape.410), calls=%async_computation.3 | async-start | bytes 262144 | tf_op jit(solution)/shard_map/all_to_all | solution.py:247
  131.9 0.8 dynamic-slice_compare_fusion
  132.7 8.4 %all-to-all-done.3 = bf16[32,2,1024]{2,1,0:T(2,128)(2,1)S(1)} async-done(((bf16[32,2,1024]{2,1,0:T(2,128)(2,1)}), bf16[32,2,1024]{2,1,0:T(2,128)(2,1)S(1)}, u32[]{:S(2)}, u32[]{:S(2)}) %all-to-all-start.3) | async-done | bytes 131104 | tf_op jit(solution)/shard_map/all_to_all | solution.py:247
  141.1 0.1 reshape.411
  141.1 0.6 gather_fusion.3
  141.7 0.1 select_select_fusion
  141.8 0.1 broadcast_in_dim.162
  141.9 15.5 %all_to_all.50 = bf16[8,32,1024]{2,1,0:T(8,128)(2,1)S(1)} all-to-all(bf16[8,32,1024]{2,1,0:T(8,128)(2,1)S(1)} %broadcast_in_dim.162), channel_id=1, replica_groups=mesh['dy'=4,'dz'=8,'tx'=4,'tc'=2] {'dz'}, dimensions={0} | all-to-all | bytes 1048576 | tf_op jit(solution)/shard_map/all_to_all | solution.py:255
  157.3 0.3 broadcast_in_dim.164
  157.6 23.5 %all_to_all.51 = bf16[4,256,1024]{2,1,0:T(8,128)(2,1)S(1)} all-to-all(bf16[4,256,1024]{2,1,0:T(8,128)(2,1)S(1)} %broadcast_in_dim.164), channel_id=1, replica_groups=mesh['dy'=4,'dz'=8,'tx'=4,'tc'=2] {'dy'}, dimensions={0} | all-to-all | bytes 4194304 | tf_op jit(solution)/shard_map/all_to_all | solution.py:258
  181.1 0.7 fusion.9
  181.8 10.5 %all_to_all.52 = f32[2,512,256]{2,1,0:T(8,128)S(1)} all-to-all(f32[2,512,256]{2,1,0:T(8,128)S(1)} %fusion.9), channel_id=1, replica_groups=mesh['dy'=4,'dz'=8,'tx'=4,'tc'=2] {'tc'}, dimensions={0} | all-to-all | bytes 2097152 | tf_op jit(solution)/shard_map/all_to_all | solution.py:266
  192.3 0.1 reduce_sum.68
  192.4 12.4 %all_to_all.53 = f32[4,128,256]{2,1,0:T(8,128)S(1)} all-to-all(f32[4,128,256]{2,1,0:T(8,128)S(1)} %bitcast.73), channel_id=1, replica_groups=mesh['dy'=4,'dz'=8,'tx'=4,'tc'=2] {'tx'}, dimensions={0} | all-to-all | bytes 1048576 | tf_op jit(solution)/shard_map/all_to_all | solution.py:273
  204.9 7.9 %all_to_all.54 = bf16[4,128,256]{2,1,0:T(8,128)(2,1)S(1)} all-to-all(bf16[4,128,256]{2,1,0:T(8,128)(2,1)S(1)} %broadcast_in_dim.165), channel_id=1, replica_groups=mesh['dy'=4,'dz'=8,'tx'=4,'tc'=2] {'tx'}, dimensions={0} | all-to-all | bytes 524288 | tf_op jit(solution)/shard_map/all_to_all | solution.py:276
  212.9 6.7 %all_to_all.55 = bf16[2,512,256]{2,1,0:T(8,128)(2,1)S(1)} all-to-all(bf16[2,512,256]{2,1,0:T(8,128)(2,1)S(1)} %broadcast_in_dim.167), channel_id=1, replica_groups=mesh['dy'=4,'dz'=8,'tx'=4,'tc'=2] {'tc'}, dimensions={0} | all-to-all | bytes 1048576 | tf_op jit(solution)/shard_map/all_to_all | solution.py:279
  219.6 0.8 copy.71
  (43 shorter events, 0.4 us)
Async XLA Ops:
  0.0 181.1 %copy-start = (bf16[1024,256]{1,0:T(8,128)(2,1)S(1)}, bf16[1024,256]{1,0:T(8,128)(2,1)}, u32[]{:S(2)}) copy-start(bf16[1024,256]{1,0:T(8,128)(2,1)} %param.15) | copy-start | bytes 1572868
  0.0 4.9 %copy-start.5 = (bf16[256]{0:T(256)(128)(2,1)S(1)}, bf16[256]{0:T(256)(128)(2,1)}, u32[]{:S(2)}) copy-start(bf16[256]{0:T(256)(128)(2,1)} %param.11) | copy-start | bytes 1540
  0.0 5.1 %copy-start.2 = (bf16[32,8192]{1,0:T(8,128)(2,1)S(1)}, bf16[32,8192]{1,0:T(8,128)(2,1)}, u32[]{:S(2)}) copy-start(bf16[32,8192]{1,0:T(8,128)(2,1)} %param.10) | copy-start | bytes 1572868
  2.4 26.1 %collective-permute-start.1 = (bf16[256,640]{1,0:T(8,128)(2,1)S(1)}, bf16[256,640]{1,0:T(8,128)(2,1)S(1)}, u32[]{:S(2)}, u32[]{:S(2)}) collective-permute-start(bf16[256,640]{1,0:T(8,128)(2,1)S(1)} %get-tuple-element.18), channel_id=1, source_target_pairs={{0,8},{8,0},{16,24},{24,16},{32,40},{40,32},{48,56},{56,48},{64,72... | collective-permute-start | bytes 983048 | tf_op jit(solution)/shard_map/ppermute | solution.py:148
  5.0 23.5 %collective-permute-start = (bf16[256]{0:T(256)(128)(2,1)S(1)}, bf16[256]{0:T(256)(128)(2,1)S(1)}, u32[]{:S(2)}, u32[]{:S(2)}) collective-permute-start(bf16[256]{0:T(256)(128)(2,1)S(1)} %copy-done.5), channel_id=1, source_target_pairs={{0,8},{8,0},{16,24},{24,16},{32,40},{40,32},{48,56},{56,48},{64,72... | collective-permute-start | bytes 1544 | tf_op jit(solution)/shard_map/ppermute | solution.py:149
  5.1 12.2 %copy-start.3 = (s32[1024]{0:T(1024)S(1)}, s32[1024]{0:T(1024)}, u32[]{:S(2)}) copy-start(s32[1024]{0:T(1024)} %param.18) | copy-start | bytes 12292
  6.3 36.1 %all-to-all-start = ((bf16[32,32,512]{2,1,0:T(8,128)(2,1)}), bf16[32,32,512]{2,1,0:T(8,128)(2,1)S(1)}, u32[]{:S(2)}, u32[]{:S(2)}) async-start(bf16[32,32,512]{2,1,0:T(8,128)(2,1)} %bitcast.3), calls=%async_computation | async-start | bytes 2097152 | tf_op jit(solution)/shard_map/all_to_all | solution.py:161
  44.5 39.5 %all-to-all-start.1 = ((bf16[32,32,640]{2,1,0:T(8,128)(2,1)}), bf16[32,32,640]{2,1,0:T(8,128)(2,1)S(1)}, u32[]{:S(2)}, u32[]{:S(2)}) async-start(bf16[32,32,640]{2,1,0:T(8,128)(2,1)} %bitcast.75), calls=%async_computation.1 | async-start | bytes 2621440 | tf_op jit(solution)/shard_map/all_to_all | solution.py:169
  62.4 5.0 %copy-start.1 = (s32[1024]{0:T(1024)S(1)}, s32[1024]{0:T(1024)}, u32[]{:S(2)}) copy-start(s32[1024]{0:T(1024)} %param.17) | copy-start | bytes 12292
  68.2 26.1 %copy-start.4 = (s32[64]{0:T(128)}, s32[64]{0:T(128)S(1)}, u32[]{:S(2)}) copy-start(s32[64]{0:T(128)S(1)} %select_reduce_fusion.parent_ref) | copy-start | bytes 772
  86.8 16.6 %all-to-all-start.2 = ((bf16[32,2,10,128]{3,1,2,0:T(2,128)(2,1)}), bf16[32,2,10,128]{3,1,2,0:T(2,128)(2,1)S(1)}, u32[]{:S(2)}, u32[]{:S(2)}) async-start(bf16[32,2,10,128]{3,1,2,0:T(2,128)(2,1)} %copy.60), calls=%async_computation.2 | async-start | bytes 327680 | tf_op jit(solution)/shard_map/all_to_all | solution.py:227
  122.5 18.6 %all-to-all-start.3 = ((bf16[32,2,1024]{2,1,0:T(2,128)(2,1)}), bf16[32,2,1024]{2,1,0:T(2,128)(2,1)S(1)}, u32[]{:S(2)}, u32[]{:S(2)}) async-start(bf16[32,2,1024]{2,1,0:T(2,128)(2,1)} %reshape.410), calls=%async_computation.3 | async-start | bytes 262144 | tf_op jit(solution)/shard_map/all_to_all | solution.py:247

commit v7 on v6

--- a/solution.py
+++ b/solution.py
@@ -46,15 +46,14 @@
     step = pl.program_id(0)
     head_width = packed_ref.shape[-1]
     head_total = packed_ref.shape[1] - 2
-    for g in range(group):
-        length = length_ref[step * group + g]
-
-        @pl.when(length == 0)
-        def _():
-            out_ref[g] = jnp.zeros(out_ref.shape[1:], out_ref.dtype)
-
-        @pl.when(length > 0)
-        def _():
+    @pl.when(length_ref[step * group] == 0)
+    def _():
+        out_ref[...] = jnp.zeros(out_ref.shape, out_ref.dtype)
+
+    @pl.when(length_ref[step * group] > 0)
+    def _():
+        for g in range(group):
+            length = length_ref[step * group + g]
             attend_one(packed_ref, key_refs[g], value_refs[g], out_ref, g, length, head_total, head_width)
 
 
@@ -243,7 +242,19 @@
     used = jnp.any(chosen, axis=1).astype(jnp.int32)
     slot_length = jnp.take(cache_lengths, first_beam + local_parent) * used
 
-    mixed = attend_slots(incoming, keys_t, values, local_parent, slot_length)
+    real_rank = jnp.cumsum(used) - 1
+    pad_rank = jnp.sum(used) + jnp.cumsum(1 - used) - 1
+    order = jnp.where(used > 0, real_rank, pad_rank)
+    moved = order[None, :] == slot_of[:, None]
+    sorted_from = jnp.sum(jnp.where(moved, slot_of[None, :], 0), axis=1)
+    mixed_sorted = attend_slots(
+        jnp.take(incoming, sorted_from, axis=0),
+        keys_t,
+        values,
+        jnp.take(local_parent, sorted_from),
+        jnp.take(slot_length, sorted_from),
+    )
+    mixed = jnp.take(mixed_sorted, order, axis=0)
     returned = lax.all_to_all(
         mixed.reshape(device_count, capacity, head_count * HEAD_DIM), DP, 0, 0, tiled=True
     ).reshape(slot_total, head_count * HEAD_DIM)

time: 221 us -> 217 us (0.982)
  Pallas kernels: 16.7 us -> 8.36 us
  other arithmetic: 5.29 us -> 9.61 us
  starting transfers between devices: 38.4 us -> 35.1 us
  local copies, waits for them, and re-layouts: 34.8 us -> 37.1 us
    all_to_all x1, waiting for transfers between devices: 14 us -> 0.01 us  [body(): lax.all_to_all(spread, DP, 0, 0, tiled=True)]
    all_to_all x1, waiting for transfers between devices: 14.6 us -> 27.3 us  [body(): lax.all_to_all(partial.astype(jnp.bfloat16).reshape(device_count, local_b...]
    pallas_call x1, Pallas kernels: 16.7 us -> 8.36 us  [attend_slots(): pl.pallas_call(attend_kernel, grid_spec=grid_spec, out_shape=jax.ShapeDty...]
    all_to_all x1, starting transfers between devices: 9.39 us -> 4.69 us  [body(): lax.all_to_all(mixed.reshape(device_count, capacity, head_count * HEAD_DI...]
    select_n x1 -> x9, other arithmetic: 0.01 us -> 3.79 us  [the longest x2 1.66 us: body(): mixed = jnp.take(mixed_sorted, order, axis=0)]
    gather x0 -> x5, local copies, waits for them, and re-layouts: none -> 3.76 us  [the longest x2 1.58 us: body(): mixed = jnp.take(mixed_sorted, order, axis=0)]
    unnamed x17 -> x15, local copies, waits for them, and re-layouts: 14.5 us -> 14.5 us
  transfers between devices with their start and end apart: 6 -> 6, of which waited for: 4 -> 3; matrix products, arithmetic and copies ran while one was open for 14% -> 16% of each run, Pallas kernels for 0% -> 0%
where the time goes in v7:
time: 217 us; the launch traced here: 215 us
  blocking collectives  76.5 us (35%)
  waiting for transfers between devices  44.9 us (21%)
  local copies, waits for them, and re-layouts  37.1 us (17%)
  starting transfers between devices  35.1 us (16%)
  other arithmetic  9.61 us (4%)
  Pallas kernels  8.36 us (4%)
  matrix products  2.81 us (1%)
    all_to_all x1, waiting for transfers between devices, body(): lax.all_to_all(partial.astype(jnp.bfloat16).reshape(device_count, local_b...  27.3 us
    all_to_all x1, blocking collectives, body(): lax.all_to_all(jnp.broadcast_to(along_z[None], (y_count,) + along_z.shape...  23.5 us
    all_to_all x1, blocking collectives, body(): lax.all_to_all(jnp.broadcast_to(attention[None], (z_count,) + attention.s...  15.5 us
    unnamed x15, local copies, waits for them, and re-layouts  14.5 us
    all_to_all x1, blocking collectives, body(): lax.all_to_all(on_chip.reshape(ring_count, chunk_rows, out_width), 'tx',...  12.4 us
    all_to_all x1, starting transfers between devices, body(): lax.all_to_all(spread, DP, 0, 0, tiled=True)  10.9 us
    all_to_all x1, blocking collectives, body(): lax.all_to_all(partial_sum.reshape(core_count, total_rows // core_count,...  10.5 us
    slice x1, local copies, waits for them, and re-layouts, body(): values = key_value_cache[:, :, 1, 0, :]  10.1 us
  transfers between devices with their start and end apart: 6, of which 3 were waited for; matrix products, arithmetic and copies ran while one was open for 16% of the time, Pallas kernels for 0%

profile of v7, /device:TPU:1, one launch (start us, length us, event | category | flops | bytes accessed | tf_op | source)
XLA Modules:
  0.0 214.9 jit_solution(11407752602881121173)
XLA Ops:
  0.0 1.1 fusion.38
  1.2 1.0 fusion.39
  2.2 0.2 broadcast_select_fusion.1
  2.4 2.5 %collective-permute-start.1 = (bf16[256,640]{1,0:T(8,128)(2,1)S(1)}, bf16[256,640]{1,0:T(8,128)(2,1)S(1)}, u32[]{:S(2)}, u32[]{:S(2)}) collective-permute-start(bf16[256,640]{1,0:T(8,128)(2,1)S(1)} %get-tuple-element.24), channel_id=1, source_target_pairs={{0,8},{8,0},{16,24},{24,16},{32,40},{40,32},{48,56},{56,48},{64,72... | collective-permute-start | bytes 983048 | tf_op jit(solution)/shard_map/ppermute | solution.py:147
  5.0 0.1 collective-permute-start
  5.1 1.1 broadcast_in_dim.198
  6.2 10.9 %all-to-all-start = ((bf16[32,32,512]{2,1,0:T(8,128)(2,1)}), bf16[32,32,512]{2,1,0:T(8,128)(2,1)S(1)}, u32[]{:S(2)}, u32[]{:S(2)}) async-start(bf16[32,32,512]{2,1,0:T(8,128)(2,1)} %bitcast.3), calls=%async_computation | async-start | bytes 2097152 | tf_op jit(solution)/shard_map/all_to_all | solution.py:160
  17.3 0.8 convert_reduce_fusion.1
  18.2 0.1 fusion.11
  18.4 10.1 %fusion.37 = (bf16[32,256,1,1,128]{4,2,3,1,0:T(2,128)(2,1)}, bf16[32,256,1,1,128]{4,2,3,1,0:T(2,128)(2,1)}) fusion(bf16[32,256,2,1,128]{4,2,3,1,0:T(2,128)(2,1)} %param.18), kind=kLoop, calls=%fused_computation.140 | loop fusion | bytes 8388608 | tf_op jit(solution)/shard_map/slice | solution.py:191
  28.5 9.8 %copy.137 = bf16[32,256,1,1,128]{1,4,0,3,2:T(8,128)(2,1)} copy(bf16[32,256,1,1,128]{4,2,3,1,0:T(2,128)(2,1)} %get-tuple-element.22) | data formatting | bytes 4194304
  38.7 0.1 select_reduce_fusion
  39.0 0.6 convert_reduce_fusion.3
  39.6 0.1 fusion.12
  39.7 0.2 convert_reduce_fusion.2
  40.0 0.8 fusion.14
  40.8 0.6 iota_reduce_fusion
  41.4 3.9 %copy.143 = bf16[32,256,1,1,128]{4,1,0,3,2:T(8,128)(2,1)} copy(bf16[32,256,1,1,128]{4,2,3,1,0:T(2,128)(2,1)} %get-tuple-element.21) | data formatting | bytes 4194304
  45.3 0.1 broadcast_in_dim.196
  45.4 0.1 broadcast_in_dim.194
  45.5 0.7 gather_fusion.1
  46.2 0.7 gather_fusion
  47.0 0.1 sub.51
  47.2 2.1 convolution_convert_fusion
  49.3 9.2 %all-to-all-start.1 = ((bf16[32,32,640]{2,1,0:T(8,128)(2,1)}), bf16[32,32,640]{2,1,0:T(8,128)(2,1)S(1)}, u32[]{:S(2)}, u32[]{:S(2)}) async-start(bf16[32,32,640]{2,1,0:T(8,128)(2,1)} %bitcast.78), calls=%async_computation.1 | async-start | bytes 2621440 | tf_op jit(solution)/shard_map/all_to_all | solution.py:168
  58.6 0.1 select_reduce_fusion.1
  58.8 0.8 gather_fusion.6
  59.6 0.8 gather_fusion.7
  60.3 0.1 gt.42
  60.5 0.1 fusion.13
  60.6 0.2 multiply_reduce_fusion
  60.9 0.6 broadcast_select_fusion.6
  61.5 0.6 broadcast_select_fusion.7.parent_ref
  62.0 0.1 multiply_cosine_fusion.1
  62.2 27.3 %all-to-all-done.1 = bf16[32,32,640]{2,1,0:T(8,128)(2,1)S(1)} async-done(((bf16[32,32,640]{2,1,0:T(8,128)(2,1)}), bf16[32,32,640]{2,1,0:T(8,128)(2,1)S(1)}, u32[]{:S(2)}, u32[]{:S(2)}) %all-to-all-start.1) | async-done | bytes 1310752 | tf_op jit(solution)/shard_map/all_to_all | solution.py:168
  89.5 0.2 convert_reduce_fusion
  90.0 0.1 fusion.21
  90.3 0.1 subtract_convert_fusion
  90.5 0.6 gather_fusion.2
  91.2 0.3 broadcast_select_fusion.3
  91.5 0.8 copy.130
  92.3 7.6 %all-to-all-start.2 = ((bf16[32,2,10,128]{3,1,2,0:T(2,128)(2,1)}), bf16[32,2,10,128]{3,1,2,0:T(2,128)(2,1)S(1)}, u32[]{:S(2)}, u32[]{:S(2)}) async-start(bf16[32,2,10,128]{3,1,2,0:T(2,128)(2,1)} %copy.130), calls=%async_computation.2 | async-start | bytes 327680 | tf_op jit(solution)/shard_map/all_to_all | solution.py:226
  100.0 9.2 %all-to-all-done.2 = bf16[32,2,10,128]{3,1,2,0:T(2,128)(2,1)S(1)} async-done(((bf16[32,2,10,128]{3,1,2,0:T(2,128)(2,1)}), bf16[32,2,10,128]{3,1,2,0:T(2,128)(2,1)S(1)}, u32[]{:S(2)}, u32[]{:S(2)}) %all-to-all-start.2) | async-done | bytes 163872 | tf_op jit(solution)/shard_map/all_to_all | solution.py:226
  109.2 0.1 copy.131
  109.3 0.1 copy.135
  109.5 0.6 gather_fusion.3
  110.1 0.8 broadcast_select_fusion.4.packed_ref
  110.9 8.4 %shard_map.100 = bf16[64,8,128]{2,1,0:T(8,128)(2,1)} custom-call(s32[64]{0:T(128)} %broadcast_select_fusion.7.parent_ref, s32[64]{0:T(128)} %get-tuple-element.19.length_ref, bf16[64,10,128]{2,1,0:T(8,128)(2,1)} %broadcast_select_fusion.4.packed_ref, bf16[32,128,256]{2,1,0:T(8,128)(2,1)} %bitcast.55, bf16[32,128,256]{2,1,0:T(8,128)(2,1)} %bitcast.56, ...), custom_call_target="tpu_custom_call" | custom-call | tf_op jit(solution)/shard_map/pallas_call | solution.py:103
  119.3 1.5 gather_fusion.4
  120.9 0.9 broadcast_select_fusion.5
  121.8 4.7 %all-to-all-start.3 = ((bf16[32,2,1024]{2,1,0:T(2,128)(2,1)}), bf16[32,2,1024]{2,1,0:T(2,128)(2,1)S(1)}, u32[]{:S(2)}, u32[]{:S(2)}) async-start(bf16[32,2,1024]{2,1,0:T(2,128)(2,1)} %broadcast_select_fusion.5), calls=%async_computation.3 | async-start | bytes 262144 | tf_op jit(solution)/shard_map/all_to_all | solution.py:258
  126.5 0.8 dynamic-slice_compare_fusion
  127.2 8.4 %all-to-all-done.3 = bf16[32,2,1024]{2,1,0:T(2,128)(2,1)S(1)} async-done(((bf16[32,2,1024]{2,1,0:T(2,128)(2,1)}), bf16[32,2,1024]{2,1,0:T(2,128)(2,1)S(1)}, u32[]{:S(2)}, u32[]{:S(2)}) %all-to-all-start.3) | async-done | bytes 131104 | tf_op jit(solution)/shard_map/all_to_all | solution.py:258
  135.7 0.6 gather_fusion.5
  136.4 15.5 %all_to_all.50 = bf16[8,32,1024]{2,1,0:T(8,128)(2,1)S(1)} all-to-all(bf16[8,32,1024]{2,1,0:T(8,128)(2,1)S(1)} %broadcast_in_dim.209), channel_id=1, replica_groups=mesh['dy'=4,'dz'=8,'tx'=4,'tc'=2] {'dz'}, dimensions={0} | all-to-all | bytes 1048576 | tf_op jit(solution)/shard_map/all_to_all | solution.py:266
  151.9 0.3 broadcast_in_dim.211
  152.2 23.5 %all_to_all.51 = bf16[4,256,1024]{2,1,0:T(8,128)(2,1)S(1)} all-to-all(bf16[4,256,1024]{2,1,0:T(8,128)(2,1)S(1)} %broadcast_in_dim.211), channel_id=1, replica_groups=mesh['dy'=4,'dz'=8,'tx'=4,'tc'=2] {'dy'}, dimensions={0} | all-to-all | bytes 4194304 | tf_op jit(solution)/shard_map/all_to_all | solution.py:269
  175.7 0.7 fusion.9
  176.4 10.5 %all_to_all.52 = f32[2,512,256]{2,1,0:T(8,128)S(1)} all-to-all(f32[2,512,256]{2,1,0:T(8,128)S(1)} %fusion.9), channel_id=1, replica_groups=mesh['dy'=4,'dz'=8,'tx'=4,'tc'=2] {'tc'}, dimensions={0} | all-to-all | bytes 2097152 | tf_op jit(solution)/shard_map/all_to_all | solution.py:277
  186.8 0.1 reduce_sum.91
  186.9 12.4 %all_to_all.53 = f32[4,128,256]{2,1,0:T(8,128)S(1)} all-to-all(f32[4,128,256]{2,1,0:T(8,128)S(1)} %bitcast.76), channel_id=1, replica_groups=mesh['dy'=4,'dz'=8,'tx'=4,'tc'=2] {'tx'}, dimensions={0} | all-to-all | bytes 1048576 | tf_op jit(solution)/shard_map/all_to_all | solution.py:284
  199.5 7.9 %all_to_all.54 = bf16[4,128,256]{2,1,0:T(8,128)(2,1)S(1)} all-to-all(bf16[4,128,256]{2,1,0:T(8,128)(2,1)S(1)} %broadcast_in_dim.212), channel_id=1, replica_groups=mesh['dy'=4,'dz'=8,'tx'=4,'tc'=2] {'tx'}, dimensions={0} | all-to-all | bytes 524288 | tf_op jit(solution)/shard_map/all_to_all | solution.py:287
  207.4 6.7 %all_to_all.55 = bf16[2,512,256]{2,1,0:T(8,128)(2,1)S(1)} all-to-all(bf16[2,512,256]{2,1,0:T(8,128)(2,1)S(1)} %broadcast_in_dim.214), channel_id=1, replica_groups=mesh['dy'=4,'dz'=8,'tx'=4,'tc'=2] {'tc'}, dimensions={0} | all-to-all | bytes 1048576 | tf_op jit(solution)/shard_map/all_to_all | solution.py:290
  214.1 0.8 copy.146
  (71 shorter events, 2.2 us)
Async XLA Ops:
  0.0 175.7 %copy-start = (bf16[1024,256]{1,0:T(8,128)(2,1)S(1)}, bf16[1024,256]{1,0:T(8,128)(2,1)}, u32[]{:S(2)}) copy-start(bf16[1024,256]{1,0:T(8,128)(2,1)} %param.17) | copy-start | bytes 1572868
  0.0 4.9 %copy-start.4 = (bf16[256]{0:T(256)(128)(2,1)S(1)}, bf16[256]{0:T(256)(128)(2,1)}, u32[]{:S(2)}) copy-start(bf16[256]{0:T(256)(128)(2,1)} %param.13) | copy-start | bytes 1540
  0.0 5.1 %copy-start.2 = (bf16[32,8192]{1,0:T(8,128)(2,1)S(1)}, bf16[32,8192]{1,0:T(8,128)(2,1)}, u32[]{:S(2)}) copy-start(bf16[32,8192]{1,0:T(8,128)(2,1)} %param.12) | copy-start | bytes 1572868
  2.4 44.8 %collective-permute-start.1 = (bf16[256,640]{1,0:T(8,128)(2,1)S(1)}, bf16[256,640]{1,0:T(8,128)(2,1)S(1)}, u32[]{:S(2)}, u32[]{:S(2)}) collective-permute-start(bf16[256,640]{1,0:T(8,128)(2,1)S(1)} %get-tuple-element.24), channel_id=1, source_target_pairs={{0,8},{8,0},{16,24},{24,16},{32,40},{40,32},{48,56},{56,48},{64,72... | collective-permute-start | bytes 983048 | tf_op jit(solution)/shard_map/ppermute | solution.py:147
  5.0 42.2 %collective-permute-start = (bf16[256]{0:T(256)(128)(2,1)S(1)}, bf16[256]{0:T(256)(128)(2,1)S(1)}, u32[]{:S(2)}, u32[]{:S(2)}) collective-permute-start(bf16[256]{0:T(256)(128)(2,1)S(1)} %copy-done.4), channel_id=1, source_target_pairs={{0,8},{8,0},{16,24},{24,16},{32,40},{40,32},{48,56},{56,48},{64,72... | collective-permute-start | bytes 1544 | tf_op jit(solution)/shard_map/ppermute | solution.py:148
  5.1 12.1 %copy-start.3 = (s32[1024]{0:T(1024)S(1)}, s32[1024]{0:T(1024)}, u32[]{:S(2)}) copy-start(s32[1024]{0:T(1024)} %param.20) | copy-start | bytes 12292
  6.2 41.0 %all-to-all-start = ((bf16[32,32,512]{2,1,0:T(8,128)(2,1)}), bf16[32,32,512]{2,1,0:T(8,128)(2,1)S(1)}, u32[]{:S(2)}, u32[]{:S(2)}) async-start(bf16[32,32,512]{2,1,0:T(8,128)(2,1)} %bitcast.3), calls=%async_computation | async-start | bytes 2097152 | tf_op jit(solution)/shard_map/all_to_all | solution.py:160
  41.4 4.1 %copy-start.1 = (s32[1024]{0:T(1024)S(1)}, s32[1024]{0:T(1024)}, u32[]{:S(2)}) copy-start(s32[1024]{0:T(1024)} %param.19) | copy-start | bytes 12292
  49.3 40.2 %all-to-all-start.1 = ((bf16[32,32,640]{2,1,0:T(8,128)(2,1)}), bf16[32,32,640]{2,1,0:T(8,128)(2,1)S(1)}, u32[]{:S(2)}, u32[]{:S(2)}) async-start(bf16[32,32,640]{2,1,0:T(8,128)(2,1)} %bitcast.78), calls=%async_computation.1 | async-start | bytes 2621440 | tf_op jit(solution)/shard_map/all_to_all | solution.py:168
  92.3 16.9 %all-to-all-start.2 = ((bf16[32,2,10,128]{3,1,2,0:T(2,128)(2,1)}), bf16[32,2,10,128]{3,1,2,0:T(2,128)(2,1)S(1)}, u32[]{:S(2)}, u32[]{:S(2)}) async-start(bf16[32,2,10,128]{3,1,2,0:T(2,128)(2,1)} %copy.130), calls=%async_computation.2 | async-start | bytes 327680 | tf_op jit(solution)/shard_map/all_to_all | solution.py:226
  121.8 13.8 %all-to-all-start.3 = ((bf16[32,2,1024]{2,1,0:T(2,128)(2,1)}), bf16[32,2,1024]{2,1,0:T(2,128)(2,1)S(1)}, u32[]{:S(2)}, u32[]{:S(2)}) async-start(bf16[32,2,1024]{2,1,0:T(2,128)(2,1)} %broadcast_select_fusion.5), calls=%async_computation.3 | async-start | bytes 262144 | tf_op jit(solution)/shard_map/all_to_all | solution.py:258

commit v8 on v7

--- a/solution.py
+++ b/solution.py
@@ -261,35 +261,43 @@
     attention = jnp.take(returned, target, axis=0)
     attention = jnp.where(my_alive[:, None] > 0, attention, jnp.zeros_like(attention))
 
+    tensor_count = lax.axis_size(TP)
+    tensor_rank = lax.axis_index(TP)
+    share = local_beams // tensor_count
+    width = head_count * HEAD_DIM
+    heads_all = lax.all_to_all(
+        attention.reshape(tensor_count, share, width), TP, 0, 0, tiled=True
+    )
+    mine = jnp.swapaxes(heads_all, 0, 1).reshape(share, tensor_count * width)
     z_count = lax.axis_size("dz")
     y_count = lax.axis_size("dy")
     along_z = lax.all_to_all(
-        jnp.broadcast_to(attention[None], (z_count,) + attention.shape), "dz", 0, 0, tiled=True
-    ).reshape(z_count * local_beams, head_count * HEAD_DIM)
+        jnp.broadcast_to(mine[None], (z_count,) + mine.shape), "dz", 0, 0, tiled=True
+    ).reshape(z_count * share, tensor_count * width)
     gathered = lax.all_to_all(
         jnp.broadcast_to(along_z[None], (y_count,) + along_z.shape), "dy", 0, 0, tiled=True
-    ).reshape(device_count * local_beams, head_count * HEAD_DIM)
-    partial_sum = jnp.dot(gathered, output_weight, preferred_element_type=jnp.float32)
-    total_rows, out_width = partial_sum.shape
-    core_count = lax.axis_size("tc")
-    ring_count = lax.axis_size("tx")
-    on_chip = jnp.sum(
-        lax.all_to_all(
-            partial_sum.reshape(core_count, total_rows // core_count, out_width), "tc", 0, 0, tiled=True
-        ),
-        axis=0,
-    )
-    chunk_rows = total_rows // (core_count * ring_count)
-    reduced = jnp.sum(
-        lax.all_to_all(on_chip.reshape(ring_count, chunk_rows, out_width), "tx", 0, 0, tiled=True),
-        axis=0,
-    ).astype(jnp.bfloat16)
-    ring_copies = lax.all_to_all(
-        jnp.broadcast_to(reduced[None], (ring_count,) + reduced.shape), "tx", 0, 0, tiled=True
-    ).reshape(ring_count * chunk_rows, out_width)
-    return lax.all_to_all(
-        jnp.broadcast_to(ring_copies[None], (core_count,) + ring_copies.shape), "tc", 0, 0, tiled=True
-    ).reshape(total_rows, out_width)
+    ).reshape(device_count * share, tensor_count * width)
+    blocks = output_weight
+    bit = 1
+    while bit < tensor_count:
+        pairs = [(i, i ^ bit) for i in range(tensor_count)]
+        blocks = jnp.concatenate([blocks, lax.ppermute(blocks, TP, pairs)], axis=0)
+        bit *= 2
+    rows_per = output_weight.shape[0]
+    order = jnp.arange(tensor_count, dtype=jnp.int32) ^ tensor_rank
+    full_weight = jnp.take(
+        blocks.reshape(tensor_count, rows_per, output_weight.shape[1]), order, axis=0
+    ).reshape(tensor_count * rows_per, output_weight.shape[1])
+    out_rows = jnp.dot(gathered, full_weight, preferred_element_type=jnp.float32).astype(
+        jnp.bfloat16
+    )
+    out_width = out_rows.shape[1]
+    copies = lax.all_to_all(
+        jnp.broadcast_to(out_rows[None], (tensor_count,) + out_rows.shape), TP, 0, 0, tiled=True
+    )
+    return jnp.swapaxes(
+        copies.reshape(tensor_count, device_count, share, out_width), 0, 1
+    ).reshape(device_count * local_beams, out_width)
 
 def solution(mesh):
     y_count = PLANE_Y

time: 217 us -> 228 us (1.051)
  blocking collectives: 76.5 us -> 30.3 us
  starting transfers between devices: 35.1 us -> 51.9 us
  waiting for transfers between devices: 44.9 us -> 61.5 us
  other arithmetic: 9.61 us -> 21.3 us
  local copies, waits for them, and re-layouts: 37.1 us -> 46.4 us
    all_to_all x6 -> x2, blocking collectives: 76.5 us -> 30.3 us  [the longest x1 15.3 us: body(): lax.all_to_all(attention.reshape(tensor_count, share, width), TP, 0, 0, t...]
    all_to_all x0 -> x2, waiting for transfers between devices: none -> 30.5 us  [the longest x1 17.9 us: body(): lax.all_to_all(jnp.broadcast_to(mine[None], (z_count,) + mine.shape), 'dz...]
    all_to_all x1, waiting for transfers between devices: 27.3 us -> 9.96 us  [body(): lax.all_to_all(partial.astype(jnp.bfloat16).reshape(device_count, local_b...]
    all_to_all x0 -> x2, starting transfers between devices: none -> 10.1 us  [the longest x1 6.13 us: body(): lax.all_to_all(jnp.broadcast_to(mine[None], (z_count,) + mine.shape), 'dz...]
    all_to_all x1, waiting for transfers between devices: 0.01 us -> 8.13 us  [body(): lax.all_to_all(spread, DP, 0, 0, tiled=True)]
    all_to_all x1, waiting for transfers between devices: 9.22 us -> 1.61 us  [body(): lax.all_to_all(outgoing.reshape(device_count, capacity, rows, HEAD_DIM),...]
    concatenate x0 -> x3, other arithmetic: none -> 7.25 us  [body(): blocks = jnp.concatenate([blocks, lax.ppermute(blocks, TP, pairs)], axis=0)]
    ppermute x0 -> x3, starting transfers between devices: none -> 5.56 us  [body(): blocks = jnp.concatenate([blocks, lax.ppermute(blocks, TP, pairs)], axis=0)]
  transfers between devices with their start and end apart: 6 -> 11, of which waited for: 3 -> 7; matrix products, arithmetic and copies ran while one was open for 16% -> 29% of each run, Pallas kernels for 0% -> 4%
where the time goes in v8:
time: 228 us; the launch traced here: 226 us
  waiting for transfers between devices  61.5 us (27%)
  starting transfers between devices  51.9 us (23%)
  local copies, waits for them, and re-layouts  46.4 us (20%)
  blocking collectives  30.3 us (13%)
  other arithmetic  21.3 us (9%)
  Pallas kernels  8.81 us (4%)
  matrix products  5.03 us (2%)
    all_to_all x1, waiting for transfers between devices, body(): lax.all_to_all(jnp.broadcast_to(mine[None], (z_count,) + mine.shape), 'dz...  17.9 us
    all_to_all x1, blocking collectives, body(): lax.all_to_all(attention.reshape(tensor_count, share, width), TP, 0, 0, t...  15.3 us
    all_to_all x1, blocking collectives, body(): lax.all_to_all(jnp.broadcast_to(out_rows[None], (tensor_count,) + out_row...  15 us
    unnamed x14, local copies, waits for them, and re-layouts  13.7 us
    all_to_all x1, waiting for transfers between devices, body(): lax.all_to_all(jnp.broadcast_to(along_z[None], (y_count,) + along_z.shape...  12.6 us
    all_to_all x1, starting transfers between devices, body(): lax.all_to_all(spread, DP, 0, 0, tiled=True)  10.9 us
    slice x1, local copies, waits for them, and re-layouts, body(): values = key_value_cache[:, :, 1, 0, :]  10.1 us
    all_to_all x1, waiting for transfers between devices, body(): lax.all_to_all(partial.astype(jnp.bfloat16).reshape(device_count, local_b...  9.96 us
  transfers between devices with their start and end apart: 11, of which 7 were waited for; matrix products, arithmetic and copies ran while one was open for 29% of the time, Pallas kernels for 4%

profile of v8, /device:TPU:1, one launch (start us, length us, event | category | flops | bytes accessed | tf_op | source)
XLA Modules:
  0.0 225.9 jit_solution(2016904088161658498)
XLA Ops:
  0.0 1.1 fusion.37
  1.2 1.0 fusion.38
  2.2 0.2 broadcast_select_fusion.2
  2.4 2.5 %collective-permute-start.1 = (bf16[256,640]{1,0:T(8,128)(2,1)S(1)}, bf16[256,640]{1,0:T(8,128)(2,1)S(1)}, u32[]{:S(2)}, u32[]{:S(2)}) collective-permute-start(bf16[256,640]{1,0:T(8,128)(2,1)S(1)} %get-tuple-element.24), channel_id=1, source_target_pairs={{0,8},{8,0},{16,24},{24,16},{32,40},{40,32},{48,56},{56,48},{64,72... | collective-permute-start | bytes 983048 | tf_op jit(solution)/shard_map/ppermute | solution.py:147
  5.0 1.1 copy.171
  6.1 1.2 broadcast_in_dim.208
  7.3 10.9 %all-to-all-start = ((bf16[32,32,512]{2,1,0:T(8,128)(2,1)}), bf16[32,32,512]{2,1,0:T(8,128)(2,1)S(1)}, u32[]{:S(2)}, u32[]{:S(2)}) async-start(bf16[32,32,512]{2,1,0:T(8,128)(2,1)} %bitcast.3), calls=%async_computation | async-start | bytes 2097152 | tf_op jit(solution)/shard_map/all_to_all | solution.py:160
  18.3 1.6 collective-permute-start.2
  20.0 0.2 convert_reduce_fusion.2
  20.2 0.6 iota_reduce_fusion
  21.0 0.8 convert_reduce_fusion.1
  22.1 0.6 convert_reduce_fusion.3
  23.5 0.7 gather_fusion
  24.2 0.8 fusion.12
  25.1 10.1 %fusion.36 = (bf16[32,256,1,1,128]{4,2,3,1,0:T(2,128)(2,1)}, bf16[32,256,1,1,128]{4,2,3,1,0:T(2,128)(2,1)}) fusion(bf16[32,256,2,1,128]{4,2,3,1,0:T(2,128)(2,1)} %param.18), kind=kLoop, calls=%fused_computation.149 | loop fusion | bytes 8388608 | tf_op jit(solution)/shard_map/slice | solution.py:191
  35.3 8.1 %all-to-all-done = bf16[32,32,512]{2,1,0:T(8,128)(2,1)S(1)} async-done(((bf16[32,32,512]{2,1,0:T(8,128)(2,1)}), bf16[32,32,512]{2,1,0:T(8,128)(2,1)S(1)}, u32[]{:S(2)}, u32[]{:S(2)}) %all-to-all-start) | async-done | bytes 1048608 | tf_op jit(solution)/shard_map/all_to_all | solution.py:160
  43.4 2.1 convolution_convert_fusion
  45.5 8.0 %all-to-all-start.1 = ((bf16[32,32,640]{2,1,0:T(8,128)(2,1)}), bf16[32,32,640]{2,1,0:T(8,128)(2,1)S(1)}, u32[]{:S(2)}, u32[]{:S(2)}) async-start(bf16[32,32,640]{2,1,0:T(8,128)(2,1)} %bitcast.82), calls=%async_computation.1 | async-start | bytes 2621440 | tf_op jit(solution)/shard_map/all_to_all | solution.py:168
  53.6 0.8 dynamic-slice_compare_fusion
  54.5 9.8 %copy.164 = bf16[32,256,1,1,128]{1,4,0,3,2:T(8,128)(2,1)} copy(bf16[32,256,1,1,128]{4,2,3,1,0:T(2,128)(2,1)} %get-tuple-element.22) | data formatting | bytes 4194304
  64.3 3.9 %copy.170 = bf16[32,256,1,1,128]{4,1,0,3,2:T(8,128)(2,1)} copy(bf16[32,256,1,1,128]{4,2,3,1,0:T(2,128)(2,1)} %get-tuple-element.21) | data formatting | bytes 4194304
  68.2 0.7 gather_fusion.1
  69.2 0.8 gather_fusion.7
  70.0 0.8 gather_fusion.8
  71.3 0.2 multiply_reduce_fusion
  71.5 0.5 broadcast_select_fusion.7
  72.0 0.5 broadcast_select_fusion.8.parent_ref
  72.6 0.1 multiply_cosine_fusion.1
  72.8 1.1 pad_maximum_fusion.2
  73.8 1.2 collective-permute-start.3
  75.1 10.0 %all-to-all-done.1 = bf16[32,32,640]{2,1,0:T(8,128)(2,1)S(1)} async-done(((bf16[32,32,640]{2,1,0:T(8,128)(2,1)}), bf16[32,32,640]{2,1,0:T(8,128)(2,1)S(1)}, u32[]{:S(2)}, u32[]{:S(2)}) %all-to-all-start.1) | async-done | bytes 1310752 | tf_op jit(solution)/shard_map/all_to_all | solution.py:168
  85.0 0.2 convert_reduce_fusion
  85.5 0.1 fusion.19
  86.0 0.6 gather_fusion.2
  86.7 0.4 broadcast_select_fusion.4
  87.1 0.8 copy.155
  87.8 7.4 %all-to-all-start.2 = ((bf16[32,2,10,128]{3,1,2,0:T(2,128)(2,1)}), bf16[32,2,10,128]{3,1,2,0:T(2,128)(2,1)S(1)}, u32[]{:S(2)}, u32[]{:S(2)}) async-start(bf16[32,2,10,128]{3,1,2,0:T(2,128)(2,1)} %copy.155), calls=%async_computation.2 | async-start | bytes 327680 | tf_op jit(solution)/shard_map/all_to_all | solution.py:226
  95.2 2.2 collective-permute-done.3
  97.4 2.7 %pad_maximum_fusion.1 = bf16[4096,256]{1,0:T(8,128)(2,1)} fusion(bf16[2048,256]{1,0:T(8,128)(2,1)} %collective-permute-done.3, bf16[1024,256]{1,0:T(8,128)(2,1)S(1)} %collective-permute-done.2, bf16[1024,256]{1,0:T(8,128)(2,1)S(1)} %copy-done.1), kind=kLoop, calls=%fused_computation.12 | loop fusion | flops 6291456 | bytes 4194304 | tf_op jit(solution)/shard_map/concatenate | solution.py:284
  100.1 2.8 %collective-permute-start.4 = (bf16[4096,256]{1,0:T(8,128)(2,1)}, bf16[4096,256]{1,0:T(8,128)(2,1)}, u32[]{:S(2)}, u32[]{:S(2)}) collective-permute-start(bf16[4096,256]{1,0:T(8,128)(2,1)} %pad_maximum_fusion.1), channel_id=1, source_target_pairs={{0,4},{1,5},{2,6},{3,7},{4,0},{5,1},{6,2},{7,3},{8,12},{9,13},{10,... | collective-permute-start | bytes 6291464 | tf_op jit(solution)/shard_map/ppermute | solution.py:284
  102.9 1.6 all-to-all-done.2
  104.7 0.6 gather_fusion.3
  105.4 0.8 broadcast_select_fusion.5.packed_ref
  106.2 8.8 %shard_map.100 = bf16[64,8,128]{2,1,0:T(8,128)(2,1)} custom-call(s32[64]{0:T(128)} %broadcast_select_fusion.8.parent_ref, s32[64]{0:T(128)} %get-tuple-element.19.length_ref, bf16[64,10,128]{2,1,0:T(8,128)(2,1)} %broadcast_select_fusion.5.packed_ref, bf16[32,128,256]{2,1,0:T(8,128)(2,1)} %bitcast.59, bf16[32,128,256]{2,1,0:T(8,128)(2,1)} %bitcast.60, ...), custom_call_target="tpu_custom_call" | custom-call | tf_op jit(solution)/shard_map/pallas_call | solution.py:103
  115.0 1.5 gather_fusion.4
  116.6 0.9 broadcast_select_fusion.6
  117.5 7.3 %all-to-all-start.3 = ((bf16[32,2,1024]{2,1,0:T(2,128)(2,1)}), bf16[32,2,1024]{2,1,0:T(2,128)(2,1)S(1)}, u32[]{:S(2)}, u32[]{:S(2)}) async-start(bf16[32,2,1024]{2,1,0:T(2,128)(2,1)} %broadcast_select_fusion.6), calls=%async_computation.3 | async-start | bytes 262144 | tf_op jit(solution)/shard_map/all_to_all | solution.py:258
  124.8 9.1 %all-to-all-done.3 = bf16[32,2,1024]{2,1,0:T(2,128)(2,1)S(1)} async-done(((bf16[32,2,1024]{2,1,0:T(2,128)(2,1)}), bf16[32,2,1024]{2,1,0:T(2,128)(2,1)S(1)}, u32[]{:S(2)}, u32[]{:S(2)}) %all-to-all-start.3) | async-done | bytes 131104 | tf_op jit(solution)/shard_map/all_to_all | solution.py:258
  134.0 0.6 gather_fusion.5
  134.8 15.3 %all_to_all.40 = bf16[8,4,1024]{2,1,0:T(4,128)(2,1)S(1)} all-to-all(bf16[8,4,1024]{2,1,0:T(4,128)(2,1)S(1)} %select_select_fusion), channel_id=1, replica_groups=mesh['dy'=4,'dz'=8,'tx'=4,'tc'=2] {'tx','tc'}, dimensions={0} | all-to-all | bytes 131072 | tf_op jit(solution)/shard_map/all_to_all | solution.py:268
  150.1 0.9 broadcast_in_dim.220
  151.0 6.1 %all-to-all-start.5 = ((bf16[8,4,8192]{2,1,0:T(4,128)(2,1)}), bf16[8,4,8192]{2,1,0:T(4,128)(2,1)S(1)}, u32[]{:S(2)}, u32[]{:S(2)}) async-start(bf16[8,4,8192]{2,1,0:T(4,128)(2,1)} %broadcast_in_dim.220), calls=%async_computation.5 | async-start | bytes 1048576 | tf_op jit(solution)/shard_map/all_to_all | solution.py:274
  157.1 17.9 %all-to-all-done.5 = bf16[8,4,8192]{2,1,0:T(4,128)(2,1)S(1)} async-done(((bf16[8,4,8192]{2,1,0:T(4,128)(2,1)}), bf16[8,4,8192]{2,1,0:T(4,128)(2,1)S(1)}, u32[]{:S(2)}, u32[]{:S(2)}) %all-to-all-start.5) | async-done | bytes 524320 | tf_op jit(solution)/shard_map/all_to_all | solution.py:274
  175.2 1.6 broadcast_in_dim.222
  176.8 4.0 %all-to-all-start.6 = ((bf16[4,32,8192]{2,1,0:T(8,128)(2,1)}), bf16[4,32,8192]{2,1,0:T(8,128)(2,1)S(1)}, u32[]{:S(2)}, u32[]{:S(2)}) async-start(bf16[4,32,8192]{2,1,0:T(8,128)(2,1)} %broadcast_in_dim.222), calls=%async_computation.6 | async-start | bytes 4194304 | tf_op jit(solution)/shard_map/all_to_all | solution.py:277
  180.8 3.5 %pad_maximum_fusion = bf16[8192,256]{1,0:T(8,128)(2,1)} fusion(bf16[4096,256]{1,0:T(8,128)(2,1)} %collective-permute-done.4, bf16[2048,256]{1,0:T(8,128)(2,1)} %collective-permute-done.3, bf16[1024,256]{1,0:T(8,128)(2,1)S(1)} %collective-permute-done.2, bf16[1024,256]{1,0:T(8,128)(2,1)S(1)} %copy-done.1), kind=kLoop, calls=%fused_computation.9 | loop fusion | flops 16777216 | bytes 8388608 | tf_op jit(solution)/shard_map/concatenate | solution.py:284
  184.3 5.0 %gather_fusion.6 = bf16[8,1024,256]{2,1,0:T(8,128)(2,1)} fusion(bf16[8,1024,256]{2,1,0:T(8,128)(2,1)} %bitcast.76, s32[1024]{0:T(1024)S(1)} %pad_clamp_fusion), kind=kCustom, calls=%fused_computation.8 | custom fusion | bytes 8388640 | tf_op jit(solution)/shard_map/jit(_take)/gather | solution.py:288
  189.3 4.6 %broadcast_select_fusion = bf16[8,1024,256]{2,1,0:T(8,128)(2,1)} fusion(bf16[8,1024,256]{2,1,0:T(8,128)(2,1)} %gather_fusion.6, pred[8]{0:T(512)(128)(4,1)S(1)} %compare_and_fusion.2), kind=kLoop, calls=%fused_computation.10 | loop fusion | flops 2097152 | bytes 8388616 | tf_op jit(solution)/shard_map/jit(_take)/select_n | solution.py:288
  193.9 12.6 %all-to-all-done.6 = bf16[4,32,8192]{2,1,0:T(8,128)(2,1)S(1)} async-done(((bf16[4,32,8192]{2,1,0:T(8,128)(2,1)}), bf16[4,32,8192]{2,1,0:T(8,128)(2,1)S(1)}, u32[]{:S(2)}, u32[]{:S(2)}) %all-to-all-start.6) | async-done | bytes 2097184 | tf_op jit(solution)/shard_map/all_to_all | solution.py:277
  206.4 2.9 %convolution_convert_fusion.1 = bf16[128,256]{1,0:T(8,128)(2,1)S(1)} fusion(bf16[128,8192]{1,0:T(8,128)(2,1)S(1)} %bitcast.77, bf16[8192,256]{1,0:T(8,128)(2,1)} %bitcast.75), kind=kOutput, calls=%fused_computation.17 | convolution fusion | flops 536903680 | bytes 6356992 | tf_op jit(solution)/shard_map/dot_general | solution.py:291
  209.4 15.0 %all_to_all.41 = bf16[8,128,256]{2,1,0:T(8,128)(2,1)S(1)} all-to-all(bf16[8,128,256]{2,1,0:T(8,128)(2,1)S(1)} %broadcast_in_dim.225), channel_id=1, replica_groups=mesh['dy'=4,'dz'=8,'tx'=4,'tc'=2] {'tx','tc'}, dimensions={0} | all-to-all | bytes 1048576 | tf_op jit(solution)/shard_map/all_to_all | solution.py:295
  224.4 0.3 copy.162
  224.7 0.2 copy.163
  225.0 0.9 reshape.574
  (88 shorter events, 3.9 us)
Async XLA Ops:
  0.0 23.4 %copy-start = (s32[1024]{0:T(1024)S(1)}, s32[1024]{0:T(1024)}, u32[]{:S(2)}) copy-start(s32[1024]{0:T(1024)} %param.19) | copy-start | bytes 12292
  0.0 18.3 %copy-start.1 = (bf16[1024,256]{1,0:T(8,128)(2,1)S(1)}, bf16[1024,256]{1,0:T(8,128)(2,1)}, u32[]{:S(2)}) copy-start(bf16[1024,256]{1,0:T(8,128)(2,1)} %param.17) | copy-start | bytes 1572868
  0.0 19.9 %copy-start.3 = (s32[1024]{0:T(1024)S(1)}, s32[1024]{0:T(1024)}, u32[]{:S(2)}) copy-start(s32[1024]{0:T(1024)} %param.20) | copy-start | bytes 12292
  2.4 32.9 %collective-permute-start.1 = (bf16[256,640]{1,0:T(8,128)(2,1)S(1)}, bf16[256,640]{1,0:T(8,128)(2,1)S(1)}, u32[]{:S(2)}, u32[]{:S(2)}) collective-permute-start(bf16[256,640]{1,0:T(8,128)(2,1)S(1)} %get-tuple-element.24), channel_id=1, source_target_pairs={{0,8},{8,0},{16,24},{24,16},{32,40},{40,32},{48,56},{56,48},{64,72... | collective-permute-start | bytes 983048 | tf_op jit(solution)/shard_map/ppermute | solution.py:147
  4.9 30.3 %collective-permute-start = (bf16[256]{0:T(256)(128)(2,1)}, bf16[256]{0:T(256)(128)(2,1)S(1)}, u32[]{:S(2)}, u32[]{:S(2)}) collective-permute-start(bf16[256]{0:T(256)(128)(2,1)} %param.13), channel_id=1, source_target_pairs={{0,8},{8,0},{16,24},{24,16},{32,40},{40,32},{48,56},{56,48},{64,72... | collective-permute-start | bytes 1544 | tf_op jit(solution)/shard_map/ppermute | solution.py:148
  7.3 36.1 %all-to-all-start = ((bf16[32,32,512]{2,1,0:T(8,128)(2,1)}), bf16[32,32,512]{2,1,0:T(8,128)(2,1)S(1)}, u32[]{:S(2)}, u32[]{:S(2)}) async-start(bf16[32,32,512]{2,1,0:T(8,128)(2,1)} %bitcast.3), calls=%async_computation | async-start | bytes 2097152 | tf_op jit(solution)/shard_map/all_to_all | solution.py:160
  18.3 54.5 %collective-permute-start.2 = (bf16[1024,256]{1,0:T(8,128)(2,1)S(1)}, bf16[1024,256]{1,0:T(8,128)(2,1)S(1)}, u32[]{:S(2)}, u32[]{:S(2)}) collective-permute-start(bf16[1024,256]{1,0:T(8,128)(2,1)S(1)} %copy-done.1), channel_id=1, source_target_pairs={{0,1},{1,0},{2,3},{3,2},{4,5},{5,4},{6,7},{7,6},{8,9},{9,8},{10,11... | collective-permute-start | bytes 1572872 | tf_op jit(solution)/shard_map/ppermute | solution.py:284
  25.1 10.1 %copy-start.4 = (bf16[256]{0:T(256)(128)(2,1)S(1)}, bf16[256]{0:T(256)(128)(2,1)}, u32[]{:S(2)}) copy-start(bf16[256]{0:T(256)(128)(2,1)} %param.13) | copy-start | bytes 1540
  45.5 39.5 %all-to-all-start.1 = ((bf16[32,32,640]{2,1,0:T(8,128)(2,1)}), bf16[32,32,640]{2,1,0:T(8,128)(2,1)S(1)}, u32[]{:S(2)}, u32[]{:S(2)}) async-start(bf16[32,32,640]{2,1,0:T(8,128)(2,1)} %bitcast.82), calls=%async_computation.1 | async-start | bytes 2621440 | tf_op jit(solution)/shard_map/all_to_all | solution.py:168
  64.3 6.9 %copy-start.2 = (bf16[32,8192]{1,0:T(8,128)(2,1)S(1)}, bf16[32,8192]{1,0:T(8,128)(2,1)}, u32[]{:S(2)}) copy-start(bf16[32,8192]{1,0:T(8,128)(2,1)} %param.12) | copy-start | bytes 1572868
  73.8 23.6 %collective-permute-start.3 = (bf16[2048,256]{1,0:T(8,128)(2,1)}, bf16[2048,256]{1,0:T(8,128)(2,1)}, u32[]{:S(2)}, u32[]{:S(2)}) collective-permute-start(bf16[2048,256]{1,0:T(8,128)(2,1)} %pad_maximum_fusion.2), channel_id=1, source_target_pairs={{0,2},{1,3},{2,0},{3,1},{4,6},{5,7},{6,4},{7,5},{8,10},{9,11},{10,... | collective-permute-start | bytes 3145736 | tf_op jit(solution)/shard_map/ppermute | solution.py:284
  87.8 16.6 %all-to-all-start.2 = ((bf16[32,2,10,128]{3,1,2,0:T(2,128)(2,1)}), bf16[32,2,10,128]{3,1,2,0:T(2,128)(2,1)S(1)}, u32[]{:S(2)}, u32[]{:S(2)}) async-start(bf16[32,2,10,128]{3,1,2,0:T(2,128)(2,1)} %copy.155), calls=%async_computation.2 | async-start | bytes 327680 | tf_op jit(solution)/shard_map/all_to_all | solution.py:226
  100.1 80.7 %collective-permute-start.4 = (bf16[4096,256]{1,0:T(8,128)(2,1)}, bf16[4096,256]{1,0:T(8,128)(2,1)}, u32[]{:S(2)}, u32[]{:S(2)}) collective-permute-start(bf16[4096,256]{1,0:T(8,128)(2,1)} %pad_maximum_fusion.1), channel_id=1, source_target_pairs={{0,4},{1,5},{2,6},{3,7},{4,0},{5,1},{6,2},{7,3},{8,12},{9,13},{10,... | collective-permute-start | bytes 6291464 | tf_op jit(solution)/shard_map/ppermute | solution.py:284
  117.5 16.4 %all-to-all-start.3 = ((bf16[32,2,1024]{2,1,0:T(2,128)(2,1)}), bf16[32,2,1024]{2,1,0:T(2,128)(2,1)S(1)}, u32[]{:S(2)}, u32[]{:S(2)}) async-start(bf16[32,2,1024]{2,1,0:T(2,128)(2,1)} %broadcast_select_fusion.6), calls=%async_computation.3 | async-start | bytes 262144 | tf_op jit(solution)/shard_map/all_to_all | solution.py:258
  151.0 24.1 %all-to-all-start.5 = ((bf16[8,4,8192]{2,1,0:T(4,128)(2,1)}), bf16[8,4,8192]{2,1,0:T(4,128)(2,1)S(1)}, u32[]{:S(2)}, u32[]{:S(2)}) async-start(bf16[8,4,8192]{2,1,0:T(4,128)(2,1)} %broadcast_in_dim.220), calls=%async_computation.5 | async-start | bytes 1048576 | tf_op jit(solution)/shard_map/all_to_all | solution.py:274
  176.8 29.6 %all-to-all-start.6 = ((bf16[4,32,8192]{2,1,0:T(8,128)(2,1)}), bf16[4,32,8192]{2,1,0:T(8,128)(2,1)S(1)}, u32[]{:S(2)}, u32[]{:S(2)}) async-start(bf16[4,32,8192]{2,1,0:T(8,128)(2,1)} %broadcast_in_dim.222), calls=%async_computation.6 | async-start | bytes 4194304 | tf_op jit(solution)/shard_map/all_to_all | solution.py:277

commit v9 on v7

--- a/solution.py
+++ b/solution.py
@@ -154,11 +154,15 @@
         jnp.concatenate([norm_gain, partner_gain]),
         jnp.concatenate([partner_gain, norm_gain]),
     )
-    spread = jnp.swapaxes(
-        jnp.repeat(hidden_in.reshape(local_beams, pair_count, 2 * features), 2, axis=1), 0, 1
-    )
-    blocked = lax.all_to_all(spread, DP, 0, 0, tiled=True).reshape(
-        device_count * local_beams, 2 * features
+    spread = jnp.swapaxes(hidden_in.reshape(local_beams, device_count, features), 0, 1)
+    own_rows = lax.all_to_all(spread, DP, 0, 0, tiled=True).reshape(
+        device_count * local_beams, features
+    )
+    partner_rows = lax.ppermute(own_rows, DP, partner)
+    blocked = jnp.where(
+        is_low,
+        jnp.concatenate([own_rows, partner_rows], 1),
+        jnp.concatenate([partner_rows, own_rows], 1),
     )
     scaled = (blocked.astype(jnp.float32) * pair_gain.astype(jnp.float32)[None, :]).astype(
         jnp.bfloat16

time: 217 us -> 220 us (1.014)
  waiting for transfers between devices: 44.9 us -> 47.5 us
    ppermute x0 -> x1, waiting for transfers between devices: none -> 4.36 us  [body(): partner_rows = lax.ppermute(own_rows, DP, partner)]
    unnamed x15 -> x16, local copies, waits for them, and re-layouts: 14.5 us -> 14.6 us
  transfers between devices with their start and end apart: 6 -> 7, of which waited for: 3 -> 4; matrix products, arithmetic and copies ran while one was open for 16% -> 16% of each run, Pallas kernels for 0% -> 0%
where the time goes in v9:
time: 220 us; the launch traced here: 218 us
  blocking collectives  75.6 us (34%)
  waiting for transfers between devices  47.5 us (22%)
  local copies, waits for them, and re-layouts  37.1 us (17%)
  starting transfers between devices  36.8 us (17%)
  other arithmetic  9.69 us (4%)
  Pallas kernels  7.9 us (4%)
  matrix products  2.9 us (1%)
    all_to_all x1, waiting for transfers between devices, body(): lax.all_to_all(partial.astype(jnp.bfloat16).reshape(device_count, local_b...  25.5 us
    all_to_all x1, blocking collectives, body(): lax.all_to_all(jnp.broadcast_to(along_z[None], (y_count,) + along_z.shape...  22.1 us
    all_to_all x1, blocking collectives, body(): lax.all_to_all(jnp.broadcast_to(attention[None], (z_count,) + attention.s...  14.6 us
    unnamed x16, local copies, waits for them, and re-layouts  14.6 us
    all_to_all x1, blocking collectives, body(): lax.all_to_all(on_chip.reshape(ring_count, chunk_rows, out_width), 'tx',...  12.4 us
    all_to_all x1, blocking collectives, body(): lax.all_to_all(partial_sum.reshape(core_count, total_rows // core_count,...  11.8 us
    all_to_all x1, starting transfers between devices, body(): lax.all_to_all(spread, DP, 0, 0, tiled=True)  10.9 us
    slice x1, local copies, waits for them, and re-layouts, body(): values = key_value_cache[:, :, 1, 0, :]  10.1 us
  transfers between devices with their start and end apart: 7, of which 4 were waited for; matrix products, arithmetic and copies ran while one was open for 16% of the time, Pallas kernels for 0%

profile of v9, /device:TPU:1, one launch (start us, length us, event | category | flops | bytes accessed | tf_op | source)
XLA Modules:
  0.0 218.1 jit_solution(14440532950765790829)
XLA Ops:
  0.0 1.1 fusion.42
  1.2 1.0 fusion.43
  2.2 0.2 broadcast_select_fusion.1
  2.4 2.5 %collective-permute-start.2 = (bf16[256,640]{1,0:T(8,128)(2,1)S(1)}, bf16[256,640]{1,0:T(8,128)(2,1)S(1)}, u32[]{:S(2)}, u32[]{:S(2)}) collective-permute-start(bf16[256,640]{1,0:T(8,128)(2,1)S(1)} %get-tuple-element.24), channel_id=1, source_target_pairs={{0,8},{8,0},{16,24},{24,16},{32,40},{40,32},{48,56},{56,48},{64,72... | collective-permute-start | bytes 983048 | tf_op jit(solution)/shard_map/ppermute | solution.py:147
  5.0 0.1 collective-permute-start.1
  5.1 0.1 copy.152
  5.2 1.1 copy.137
  6.3 10.9 %all-to-all-start = ((bf16[32,32,256]{2,1,0:T(8,128)(2,1)}), bf16[32,32,256]{2,1,0:T(8,128)(2,1)S(1)}, u32[]{:S(2)}, u32[]{:S(2)}) async-start(bf16[32,32,256]{2,1,0:T(8,128)(2,1)} %copy.137), calls=%async_computation | async-start | bytes 1048576 | tf_op jit(solution)/shard_map/all_to_all | solution.py:158
  17.3 0.8 convert_reduce_fusion.1
  18.3 0.1 fusion.15
  18.4 0.7 convert_reduce_fusion.3
  19.1 10.1 %fusion.41 = (bf16[32,256,1,1,128]{4,2,3,1,0:T(2,128)(2,1)}, bf16[32,256,1,1,128]{4,2,3,1,0:T(2,128)(2,1)}) fusion(bf16[32,256,2,1,128]{4,2,3,1,0:T(2,128)(2,1)} %param.18), kind=kLoop, calls=%fused_computation.145 | loop fusion | bytes 8388608 | tf_op jit(solution)/shard_map/slice | solution.py:195
  29.2 9.8 %copy.150 = bf16[32,256,1,1,128]{1,4,0,3,2:T(8,128)(2,1)} copy(bf16[32,256,1,1,128]{4,2,3,1,0:T(2,128)(2,1)} %get-tuple-element.22) | data formatting | bytes 4194304
  39.4 0.1 select_reduce_fusion
  39.7 0.1 fusion.16
  39.8 0.2 convert_reduce_fusion.2
  40.1 0.8 fusion.18
  40.9 1.3 collective-permute-start
  42.3 0.6 iota_reduce_fusion
  42.9 3.9 %copy.155 = bf16[32,256,1,1,128]{4,1,0,3,2:T(8,128)(2,1)} copy(bf16[32,256,1,1,128]{4,2,3,1,0:T(2,128)(2,1)} %get-tuple-element.21) | data formatting | bytes 4194304
  46.7 0.1 broadcast_in_dim.193
  46.8 0.1 broadcast_in_dim.191
  47.0 0.7 gather_fusion.1
  47.6 0.7 gather_fusion
  48.6 4.4 %collective-permute-done = bf16[1024,256]{1,0:T(8,128)(2,1)S(1)} collective-permute-done((bf16[1024,256]{1,0:T(8,128)(2,1)S(1)}, bf16[1024,256]{1,0:T(8,128)(2,1)S(1)}, u32[]{:S(2)}, u32[]{:S(2)}) %collective-permute-start) | collective-permute-done | bytes 524320 | tf_op jit(solution)/shard_map/ppermute | solution.py:161
  53.0 2.2 %convolution_convert_fusion = bf16[1024,640]{1,0:T(8,128)(2,1)} fusion(bf16[1024,256]{1,0:T(8,128)(2,1)S(1)} %collective-permute-done, bf16[1024,256]{1,0:T(8,128)(2,1)S(1)} %bitcast.80, f32[512]{0:T(512)S(1)} %fusion.36, pred[]{:T(512)S(6)} %eq.99, bf16[256,640]{1,0:T(8,128)(2,1)S(1)} %collective-permute-done.2, bf16[256,640]{1,0:T(8,128)(2,1)S(1)} %get-tuple-element.23), kind=kOutput, calls=%fused_computation.11 | convolution fusion | flops 680984576 | bytes 3016705 | tf_op jit(solution)/shard_map/dot_general | solution.py:170
  55.2 8.9 %all-to-all-start.1 = ((bf16[32,32,640]{2,1,0:T(8,128)(2,1)}), bf16[32,32,640]{2,1,0:T(8,128)(2,1)S(1)}, u32[]{:S(2)}, u32[]{:S(2)}) async-start(bf16[32,32,640]{2,1,0:T(8,128)(2,1)} %bitcast.74), calls=%async_computation.1 | async-start | bytes 2621440 | tf_op jit(solution)/shard_map/all_to_all | solution.py:172
  64.2 0.1 select_reduce_fusion.1
  64.4 0.8 gather_fusion.6
  65.2 0.8 gather_fusion.7
  65.9 0.1 gt.42
  66.2 0.2 multiply_reduce_fusion
  66.5 0.6 broadcast_select_fusion.6
  67.1 0.6 broadcast_select_fusion.7.parent_ref
  67.6 0.1 multiply_cosine_fusion.1
  67.8 25.5 %all-to-all-done.1 = bf16[32,32,640]{2,1,0:T(8,128)(2,1)S(1)} async-done(((bf16[32,32,640]{2,1,0:T(8,128)(2,1)}), bf16[32,32,640]{2,1,0:T(8,128)(2,1)S(1)}, u32[]{:S(2)}, u32[]{:S(2)}) %all-to-all-start.1) | async-done | bytes 1310752 | tf_op jit(solution)/shard_map/all_to_all | solution.py:172
  93.3 0.2 convert_reduce_fusion
  93.8 0.1 fusion.25
  94.1 0.1 subtract_convert_fusion
  94.3 0.6 gather_fusion.2
  95.0 0.3 broadcast_select_fusion.3
  95.3 0.8 copy.143
  96.1 7.9 %all-to-all-start.2 = ((bf16[32,2,10,128]{3,1,2,0:T(2,128)(2,1)}), bf16[32,2,10,128]{3,1,2,0:T(2,128)(2,1)S(1)}, u32[]{:S(2)}, u32[]{:S(2)}) async-start(bf16[32,2,10,128]{3,1,2,0:T(2,128)(2,1)} %copy.143), calls=%async_computation.2 | async-start | bytes 327680 | tf_op jit(solution)/shard_map/all_to_all | solution.py:230
  104.1 9.2 %all-to-all-done.2 = bf16[32,2,10,128]{3,1,2,0:T(2,128)(2,1)S(1)} async-done(((bf16[32,2,10,128]{3,1,2,0:T(2,128)(2,1)}), bf16[32,2,10,128]{3,1,2,0:T(2,128)(2,1)S(1)}, u32[]{:S(2)}, u32[]{:S(2)}) %all-to-all-start.2) | async-done | bytes 163872 | tf_op jit(solution)/shard_map/all_to_all | solution.py:230
  113.3 0.1 copy.144
  113.5 0.1 copy.148
  113.6 0.6 gather_fusion.3
  114.2 0.8 broadcast_select_fusion.4.packed_ref
  115.1 7.9 %shard_map.100 = bf16[64,8,128]{2,1,0:T(8,128)(2,1)} custom-call(s32[64]{0:T(128)} %broadcast_select_fusion.7.parent_ref, s32[64]{0:T(128)} %get-tuple-element.19.length_ref, bf16[64,10,128]{2,1,0:T(8,128)(2,1)} %broadcast_select_fusion.4.packed_ref, bf16[32,128,256]{2,1,0:T(8,128)(2,1)} %bitcast.51, bf16[32,128,256]{2,1,0:T(8,128)(2,1)} %bitcast.52, ...), custom_call_target="tpu_custom_call" | custom-call | tf_op jit(solution)/shard_map/pallas_call | solution.py:103
  123.0 1.5 gather_fusion.4
  124.5 0.9 broadcast_select_fusion.5
  125.4 5.1 %all-to-all-start.3 = ((bf16[32,2,1024]{2,1,0:T(2,128)(2,1)}), bf16[32,2,1024]{2,1,0:T(2,128)(2,1)S(1)}, u32[]{:S(2)}, u32[]{:S(2)}) async-start(bf16[32,2,1024]{2,1,0:T(2,128)(2,1)} %broadcast_select_fusion.5), calls=%async_computation.3 | async-start | bytes 262144 | tf_op jit(solution)/shard_map/all_to_all | solution.py:262
  130.5 0.8 dynamic-slice_compare_fusion
  131.3 8.4 %all-to-all-done.3 = bf16[32,2,1024]{2,1,0:T(2,128)(2,1)S(1)} async-done(((bf16[32,2,1024]{2,1,0:T(2,128)(2,1)}), bf16[32,2,1024]{2,1,0:T(2,128)(2,1)S(1)}, u32[]{:S(2)}, u32[]{:S(2)}) %all-to-all-start.3) | async-done | bytes 131104 | tf_op jit(solution)/shard_map/all_to_all | solution.py:262
  139.7 0.6 gather_fusion.5
  140.4 14.6 %all_to_all.50 = bf16[8,32,1024]{2,1,0:T(8,128)(2,1)S(1)} all-to-all(bf16[8,32,1024]{2,1,0:T(8,128)(2,1)S(1)} %broadcast_in_dim.205), channel_id=1, replica_groups=mesh['dy'=4,'dz'=8,'tx'=4,'tc'=2] {'dz'}, dimensions={0} | all-to-all | bytes 1048576 | tf_op jit(solution)/shard_map/all_to_all | solution.py:270
  155.0 0.3 broadcast_in_dim.207
  155.3 22.1 %all_to_all.51 = bf16[4,256,1024]{2,1,0:T(8,128)(2,1)S(1)} all-to-all(bf16[4,256,1024]{2,1,0:T(8,128)(2,1)S(1)} %broadcast_in_dim.207), channel_id=1, replica_groups=mesh['dy'=4,'dz'=8,'tx'=4,'tc'=2] {'dy'}, dimensions={0} | all-to-all | bytes 4194304 | tf_op jit(solution)/shard_map/all_to_all | solution.py:273
  177.4 0.7 fusion.13
  178.1 11.8 %all_to_all.52 = f32[2,512,256]{2,1,0:T(8,128)S(1)} all-to-all(f32[2,512,256]{2,1,0:T(8,128)S(1)} %fusion.13), channel_id=1, replica_groups=mesh['dy'=4,'dz'=8,'tx'=4,'tc'=2] {'tc'}, dimensions={0} | all-to-all | bytes 2097152 | tf_op jit(solution)/shard_map/all_to_all | solution.py:281
  190.1 12.4 %all_to_all.53 = f32[4,128,256]{2,1,0:T(8,128)S(1)} all-to-all(f32[4,128,256]{2,1,0:T(8,128)S(1)} %bitcast.71), channel_id=1, replica_groups=mesh['dy'=4,'dz'=8,'tx'=4,'tc'=2] {'tx'}, dimensions={0} | all-to-all | bytes 1048576 | tf_op jit(solution)/shard_map/all_to_all | solution.py:288
  202.6 7.9 %all_to_all.54 = bf16[4,128,256]{2,1,0:T(8,128)(2,1)S(1)} all-to-all(bf16[4,128,256]{2,1,0:T(8,128)(2,1)S(1)} %broadcast_in_dim.208), channel_id=1, replica_groups=mesh['dy'=4,'dz'=8,'tx'=4,'tc'=2] {'tx'}, dimensions={0} | all-to-all | bytes 524288 | tf_op jit(solution)/shard_map/all_to_all | solution.py:291
  210.6 6.7 %all_to_all.55 = bf16[2,512,256]{2,1,0:T(8,128)(2,1)S(1)} all-to-all(bf16[2,512,256]{2,1,0:T(8,128)(2,1)S(1)} %broadcast_in_dim.210), channel_id=1, replica_groups=mesh['dy'=4,'dz'=8,'tx'=4,'tc'=2] {'tc'}, dimensions={0} | all-to-all | bytes 1048576 | tf_op jit(solution)/shard_map/all_to_all | solution.py:294
  217.3 0.8 copy.157
  (73 shorter events, 2.4 us)
Async XLA Ops:
  0.0 177.4 %copy-start = (bf16[1024,256]{1,0:T(8,128)(2,1)S(1)}, bf16[1024,256]{1,0:T(8,128)(2,1)}, u32[]{:S(2)}) copy-start(bf16[1024,256]{1,0:T(8,128)(2,1)} %param.17) | copy-start | bytes 1572868
  0.0 5.0 %copy-start.4 = (bf16[256]{0:T(256)(128)(2,1)S(1)}, bf16[256]{0:T(256)(128)(2,1)}, u32[]{:S(2)}) copy-start(bf16[256]{0:T(256)(128)(2,1)} %param.13) | copy-start | bytes 1540
  0.0 5.1 %copy-start.2 = (bf16[32,8192]{1,0:T(8,128)(2,1)S(1)}, bf16[32,8192]{1,0:T(8,128)(2,1)}, u32[]{:S(2)}) copy-start(bf16[32,8192]{1,0:T(8,128)(2,1)} %param.12) | copy-start | bytes 1572868
  2.2 15.0 %copy-start.3 = (s32[1024]{0:T(1024)S(1)}, s32[1024]{0:T(1024)}, u32[]{:S(2)}) copy-start(s32[1024]{0:T(1024)} %param.20) | copy-start | bytes 12292
  2.4 46.2 %collective-permute-start.2 = (bf16[256,640]{1,0:T(8,128)(2,1)S(1)}, bf16[256,640]{1,0:T(8,128)(2,1)S(1)}, u32[]{:S(2)}, u32[]{:S(2)}) collective-permute-start(bf16[256,640]{1,0:T(8,128)(2,1)S(1)} %get-tuple-element.24), channel_id=1, source_target_pairs={{0,8},{8,0},{16,24},{24,16},{32,40},{40,32},{48,56},{56,48},{64,72... | collective-permute-start | bytes 983048 | tf_op jit(solution)/shard_map/ppermute | solution.py:147
  5.0 43.6 %collective-permute-start.1 = (bf16[256]{0:T(256)(128)(2,1)S(1)}, bf16[256]{0:T(256)(128)(2,1)S(1)}, u32[]{:S(2)}, u32[]{:S(2)}) collective-permute-start(bf16[256]{0:T(256)(128)(2,1)S(1)} %copy-done.4), channel_id=1, source_target_pairs={{0,8},{8,0},{16,24},{24,16},{32,40},{40,32},{48,56},{56,48},{64,72... | collective-permute-start | bytes 1544 | tf_op jit(solution)/shard_map/ppermute | solution.py:148
  6.3 34.7 %all-to-all-start = ((bf16[32,32,256]{2,1,0:T(8,128)(2,1)}), bf16[32,32,256]{2,1,0:T(8,128)(2,1)S(1)}, u32[]{:S(2)}, u32[]{:S(2)}) async-start(bf16[32,32,256]{2,1,0:T(8,128)(2,1)} %copy.137), calls=%async_computation | async-start | bytes 1048576 | tf_op jit(solution)/shard_map/all_to_all | solution.py:158
  40.9 12.1 %collective-permute-start = (bf16[1024,256]{1,0:T(8,128)(2,1)S(1)}, bf16[1024,256]{1,0:T(8,128)(2,1)S(1)}, u32[]{:S(2)}, u32[]{:S(2)}) collective-permute-start(bf16[1024,256]{1,0:T(8,128)(2,1)S(1)} %bitcast.79), channel_id=1, source_target_pairs={{0,8},{8,0},{16,24},{24,16},{32,40},{40,32},{48,56},{56,48},{64,72... | collective-permute-start | bytes 1572872 | tf_op jit(solution)/shard_map/ppermute | solution.py:161
  42.9 4.1 %copy-start.1 = (s32[1024]{0:T(1024)S(1)}, s32[1024]{0:T(1024)}, u32[]{:S(2)}) copy-start(s32[1024]{0:T(1024)} %param.19) | copy-start | bytes 12292
  55.2 38.1 %all-to-all-start.1 = ((bf16[32,32,640]{2,1,0:T(8,128)(2,1)}), bf16[32,32,640]{2,1,0:T(8,128)(2,1)S(1)}, u32[]{:S(2)}, u32[]{:S(2)}) async-start(bf16[32,32,640]{2,1,0:T(8,128)(2,1)} %bitcast.74), calls=%async_computation.1 | async-start | bytes 2621440 | tf_op jit(solution)/shard_map/all_to_all | solution.py:172
  96.1 17.2 %all-to-all-start.2 = ((bf16[32,2,10,128]{3,1,2,0:T(2,128)(2,1)}), bf16[32,2,10,128]{3,1,2,0:T(2,128)(2,1)S(1)}, u32[]{:S(2)}, u32[]{:S(2)}) async-start(bf16[32,2,10,128]{3,1,2,0:T(2,128)(2,1)} %copy.143), calls=%async_computation.2 | async-start | bytes 327680 | tf_op jit(solution)/shard_map/all_to_all | solution.py:230
  125.4 14.2 %all-to-all-start.3 = ((bf16[32,2,1024]{2,1,0:T(2,128)(2,1)}), bf16[32,2,1024]{2,1,0:T(2,128)(2,1)S(1)}, u32[]{:S(2)}, u32[]{:S(2)}) async-start(bf16[32,2,1024]{2,1,0:T(2,128)(2,1)} %broadcast_select_fusion.5), calls=%async_computation.3 | async-start | bytes 262144 | tf_op jit(solution)/shard_map/all_to_all | solution.py:262

commit v10 on v7

--- a/solution.py
+++ b/solution.py
@@ -128,9 +128,9 @@
     inverse = lax.rsqrt(jnp.mean(hidden_float * hidden_float, axis=1) + 1e-06)
 
     features = query_weight.shape[0]
-    pair_count = device_count // 2
-    is_low = device_rank % 2 == 0
-    partner = [(i, i ^ 1) for i in range(device_count)]
+    z_count = device_count // PLANE_Y
+    is_low = (device_rank // z_count) % 2 == 0
+    partner = [(i, i ^ z_count) for i in range(device_count)]
     query_width = query_weight.shape[1]
     key_width = key_weight.shape[1]
     query_half = query_width // 2
@@ -154,8 +154,15 @@
         jnp.concatenate([norm_gain, partner_gain]),
         jnp.concatenate([partner_gain, norm_gain]),
     )
+    pair_blocks = jnp.swapaxes(
+        hidden_in.reshape(local_beams, PLANE_Y // 2, 2, z_count, features), 2, 3
+    ).reshape(local_beams, PLANE_Y // 2, 1, z_count, 2 * features)
     spread = jnp.swapaxes(
-        jnp.repeat(hidden_in.reshape(local_beams, pair_count, 2 * features), 2, axis=1), 0, 1
+        jnp.broadcast_to(
+            pair_blocks, (local_beams, PLANE_Y // 2, 2, z_count, 2 * features)
+        ).reshape(local_beams, device_count, 2 * features),
+        0,
+        1,
     )
     blocked = lax.all_to_all(spread, DP, 0, 0, tiled=True).reshape(
         device_count * local_beams, 2 * features
@@ -173,7 +180,10 @@
         tiled=True,
     )
     sums = jnp.sum(
-        arrived.astype(jnp.float32).reshape(pair_count, 2, local_beams, half_width), axis=0
+        arrived.astype(jnp.float32).reshape(
+            PLANE_Y // 2, 2, z_count, local_beams, half_width
+        ),
+        axis=(0, 2),
     )
     key_end = query_half + key_half
     summed = jnp.concatenate(

time: 217 us -> 218 us (level)
    unnamed x15 -> x16, local copies, waits for them, and re-layouts: 14.5 us -> 14.6 us
  transfers between devices with their start and end apart: 6 -> 6, of which waited for: 3 -> 3; matrix products, arithmetic and copies ran while one was open for 16% -> 17% of each run, Pallas kernels for 0% -> 0%
where the time goes in v10:
time: 218 us; the launch traced here: 217 us
  blocking collectives  76.5 us (35%)
  waiting for transfers between devices  44.9 us (21%)
  local copies, waits for them, and re-layouts  38.3 us (18%)
  starting transfers between devices  35.7 us (16%)
  other arithmetic  9.61 us (4%)
  Pallas kernels  8.19 us (4%)
  matrix products  2.81 us (1%)
    all_to_all x1, waiting for transfers between devices, body(): lax.all_to_all(partial.astype(jnp.bfloat16).reshape(device_count, local_b...  27.3 us
    all_to_all x1, blocking collectives, body(): lax.all_to_all(jnp.broadcast_to(along_z[None], (y_count,) + along_z.shape...  23.4 us
    all_to_all x1, blocking collectives, body(): lax.all_to_all(jnp.broadcast_to(attention[None], (z_count,) + attention.s...  15.4 us
    unnamed x16, local copies, waits for them, and re-layouts  14.6 us
    all_to_all x1, blocking collectives, body(): lax.all_to_all(on_chip.reshape(ring_count, chunk_rows, out_width), 'tx',...  12.4 us
    all_to_all x1, starting transfers between devices, body(): lax.all_to_all(spread, DP, 0, 0, tiled=True)  11.3 us
    all_to_all x1, blocking collectives, body(): lax.all_to_all(partial_sum.reshape(core_count, total_rows // core_count,...  10.5 us
    slice x1, local copies, waits for them, and re-layouts, body(): values = key_value_cache[:, :, 1, 0, :]  10.1 us
  transfers between devices with their start and end apart: 6, of which 3 were waited for; matrix products, arithmetic and copies ran while one was open for 17% of the time, Pallas kernels for 0%

profile of v10, /device:TPU:1, one launch (start us, length us, event | category | flops | bytes accessed | tf_op | source)
XLA Modules:
  0.0 216.5 jit_solution(3784141423737693768)
XLA Ops:
  0.0 1.1 fusion.38
  1.2 1.0 fusion.39
  2.2 0.2 broadcast_select_fusion.1
  2.4 2.2 %collective-permute-start.1 = (bf16[256,640]{1,0:T(8,128)(2,1)S(1)}, bf16[256,640]{1,0:T(8,128)(2,1)S(1)}, u32[]{:S(2)}, u32[]{:S(2)}) collective-permute-start(bf16[256,640]{1,0:T(8,128)(2,1)S(1)} %get-tuple-element.24), channel_id=1, source_target_pairs={{0,64},{8,72},{16,80},{24,88},{32,96},{40,104},{48,112},{56,120},{... | collective-permute-start | bytes 983048 | tf_op jit(solution)/shard_map/ppermute | solution.py:147
  4.6 0.1 collective-permute-start
  4.7 0.1 copy.159
  4.9 0.5 copy.164
  5.4 0.3 broadcast_in_dim.202
  5.7 0.3 copy.144
  6.0 1.1 broadcast_in_dim.203
  7.2 11.3 %all-to-all-start = ((bf16[32,32,512]{2,1,0:T(8,128)(2,1)}), bf16[32,32,512]{2,1,0:T(8,128)(2,1)S(1)}, u32[]{:S(2)}, u32[]{:S(2)}) async-start(bf16[32,32,512]{2,1,0:T(8,128)(2,1)} %bitcast.4), calls=%async_computation | async-start | bytes 2097152 | tf_op jit(solution)/shard_map/all_to_all | solution.py:167
  18.6 0.8 convert_reduce_fusion.1
  19.5 0.1 fusion.11
  19.7 10.1 %fusion.37 = (bf16[32,256,1,1,128]{4,2,3,1,0:T(2,128)(2,1)}, bf16[32,256,1,1,128]{4,2,3,1,0:T(2,128)(2,1)}) fusion(bf16[32,256,2,1,128]{4,2,3,1,0:T(2,128)(2,1)} %param.18), kind=kLoop, calls=%fused_computation.140 | loop fusion | bytes 8388608 | tf_op jit(solution)/shard_map/slice | solution.py:201
  29.8 9.8 %copy.157 = bf16[32,256,1,1,128]{1,4,0,3,2:T(8,128)(2,1)} copy(bf16[32,256,1,1,128]{4,2,3,1,0:T(2,128)(2,1)} %get-tuple-element.22) | data formatting | bytes 4194304
  39.9 0.1 select_reduce_fusion
  40.2 0.6 convert_reduce_fusion.3
  41.0 0.2 convert_reduce_fusion.2
  41.3 0.8 fusion.14
  42.1 0.6 iota_reduce_fusion
  42.7 3.9 %copy.163 = bf16[32,256,1,1,128]{4,1,0,3,2:T(8,128)(2,1)} copy(bf16[32,256,1,1,128]{4,2,3,1,0:T(2,128)(2,1)} %get-tuple-element.21) | data formatting | bytes 4194304
  46.6 0.1 broadcast_in_dim.200
  46.7 0.1 broadcast_in_dim.198
  46.8 0.7 gather_fusion.1
  47.5 0.7 gather_fusion
  48.5 2.1 convolution_convert_fusion
  50.6 9.2 %all-to-all-start.1 = ((bf16[32,32,640]{2,1,0:T(8,128)(2,1)}), bf16[32,32,640]{2,1,0:T(8,128)(2,1)S(1)}, u32[]{:S(2)}, u32[]{:S(2)}) async-start(bf16[32,32,640]{2,1,0:T(8,128)(2,1)} %bitcast.81), calls=%async_computation.1 | async-start | bytes 2621440 | tf_op jit(solution)/shard_map/all_to_all | solution.py:175
  59.8 0.1 select_reduce_fusion.1
  60.0 0.8 gather_fusion.6
  60.8 0.8 gather_fusion.7
  61.6 0.1 gt.42
  61.8 0.1 fusion.13
  61.9 0.2 multiply_reduce_fusion
  62.1 0.6 broadcast_select_fusion.6
  62.7 0.6 broadcast_select_fusion.7.parent_ref
  63.3 0.1 multiply_cosine_fusion.1
  63.4 27.3 %all-to-all-done.1 = bf16[32,32,640]{2,1,0:T(8,128)(2,1)S(1)} async-done(((bf16[32,32,640]{2,1,0:T(8,128)(2,1)}), bf16[32,32,640]{2,1,0:T(8,128)(2,1)S(1)}, u32[]{:S(2)}, u32[]{:S(2)}) %all-to-all-start.1) | async-done | bytes 1310752 | tf_op jit(solution)/shard_map/all_to_all | solution.py:175
  90.8 0.2 convert_reduce_fusion
  91.3 0.1 fusion.21
  91.8 0.6 gather_fusion.2
  92.5 0.3 broadcast_select_fusion.3
  92.8 0.8 copy.150
  93.6 7.6 %all-to-all-start.2 = ((bf16[32,2,10,128]{3,1,2,0:T(2,128)(2,1)}), bf16[32,2,10,128]{3,1,2,0:T(2,128)(2,1)S(1)}, u32[]{:S(2)}, u32[]{:S(2)}) async-start(bf16[32,2,10,128]{3,1,2,0:T(2,128)(2,1)} %copy.150), calls=%async_computation.2 | async-start | bytes 327680 | tf_op jit(solution)/shard_map/all_to_all | solution.py:236
  101.2 9.2 %all-to-all-done.2 = bf16[32,2,10,128]{3,1,2,0:T(2,128)(2,1)S(1)} async-done(((bf16[32,2,10,128]{3,1,2,0:T(2,128)(2,1)}), bf16[32,2,10,128]{3,1,2,0:T(2,128)(2,1)S(1)}, u32[]{:S(2)}, u32[]{:S(2)}) %all-to-all-start.2) | async-done | bytes 163872 | tf_op jit(solution)/shard_map/all_to_all | solution.py:236
  110.5 0.1 copy.151
  110.6 0.1 copy.155
  110.7 0.6 gather_fusion.3
  111.4 0.8 broadcast_select_fusion.4.packed_ref
  112.2 8.2 %shard_map.100 = bf16[64,8,128]{2,1,0:T(8,128)(2,1)} custom-call(s32[64]{0:T(128)} %broadcast_select_fusion.7.parent_ref, s32[64]{0:T(128)} %get-tuple-element.19.length_ref, bf16[64,10,128]{2,1,0:T(8,128)(2,1)} %broadcast_select_fusion.4.packed_ref, bf16[32,128,256]{2,1,0:T(8,128)(2,1)} %bitcast.57, bf16[32,128,256]{2,1,0:T(8,128)(2,1)} %bitcast.58, ...), custom_call_target="tpu_custom_call" | custom-call | tf_op jit(solution)/shard_map/pallas_call | solution.py:103
  120.4 1.5 gather_fusion.4
  122.0 0.9 broadcast_select_fusion.5
  122.8 5.2 %all-to-all-start.3 = ((bf16[32,2,1024]{2,1,0:T(2,128)(2,1)}), bf16[32,2,1024]{2,1,0:T(2,128)(2,1)S(1)}, u32[]{:S(2)}, u32[]{:S(2)}) async-start(bf16[32,2,1024]{2,1,0:T(2,128)(2,1)} %broadcast_select_fusion.5), calls=%async_computation.3 | async-start | bytes 262144 | tf_op jit(solution)/shard_map/all_to_all | solution.py:268
  128.1 0.8 dynamic-slice_compare_fusion
  128.9 8.4 %all-to-all-done.3 = bf16[32,2,1024]{2,1,0:T(2,128)(2,1)S(1)} async-done(((bf16[32,2,1024]{2,1,0:T(2,128)(2,1)}), bf16[32,2,1024]{2,1,0:T(2,128)(2,1)S(1)}, u32[]{:S(2)}, u32[]{:S(2)}) %all-to-all-start.3) | async-done | bytes 131104 | tf_op jit(solution)/shard_map/all_to_all | solution.py:268
  137.3 0.6 gather_fusion.5
  138.1 15.4 %all_to_all.50 = bf16[8,32,1024]{2,1,0:T(8,128)(2,1)S(1)} all-to-all(bf16[8,32,1024]{2,1,0:T(8,128)(2,1)S(1)} %broadcast_in_dim.214), channel_id=1, replica_groups=mesh['dy'=4,'dz'=8,'tx'=4,'tc'=2] {'dz'}, dimensions={0} | all-to-all | bytes 1048576 | tf_op jit(solution)/shard_map/all_to_all | solution.py:276
  153.5 0.3 broadcast_in_dim.216
  153.8 23.4 %all_to_all.51 = bf16[4,256,1024]{2,1,0:T(8,128)(2,1)S(1)} all-to-all(bf16[4,256,1024]{2,1,0:T(8,128)(2,1)S(1)} %broadcast_in_dim.216), channel_id=1, replica_groups=mesh['dy'=4,'dz'=8,'tx'=4,'tc'=2] {'dy'}, dimensions={0} | all-to-all | bytes 4194304 | tf_op jit(solution)/shard_map/all_to_all | solution.py:279
  177.2 0.7 fusion.9
  177.9 10.5 %all_to_all.52 = f32[2,512,256]{2,1,0:T(8,128)S(1)} all-to-all(f32[2,512,256]{2,1,0:T(8,128)S(1)} %fusion.9), channel_id=1, replica_groups=mesh['dy'=4,'dz'=8,'tx'=4,'tc'=2] {'tc'}, dimensions={0} | all-to-all | bytes 2097152 | tf_op jit(solution)/shard_map/all_to_all | solution.py:287
  188.6 12.4 %all_to_all.53 = f32[4,128,256]{2,1,0:T(8,128)S(1)} all-to-all(f32[4,128,256]{2,1,0:T(8,128)S(1)} %bitcast.78), channel_id=1, replica_groups=mesh['dy'=4,'dz'=8,'tx'=4,'tc'=2] {'tx'}, dimensions={0} | all-to-all | bytes 1048576 | tf_op jit(solution)/shard_map/all_to_all | solution.py:294
  201.1 7.9 %all_to_all.54 = bf16[4,128,256]{2,1,0:T(8,128)(2,1)S(1)} all-to-all(bf16[4,128,256]{2,1,0:T(8,128)(2,1)S(1)} %broadcast_in_dim.217), channel_id=1, replica_groups=mesh['dy'=4,'dz'=8,'tx'=4,'tc'=2] {'tx'}, dimensions={0} | all-to-all | bytes 524288 | tf_op jit(solution)/shard_map/all_to_all | solution.py:297
  209.0 6.7 %all_to_all.55 = bf16[2,512,256]{2,1,0:T(8,128)(2,1)S(1)} all-to-all(bf16[2,512,256]{2,1,0:T(8,128)(2,1)S(1)} %broadcast_in_dim.219), channel_id=1, replica_groups=mesh['dy'=4,'dz'=8,'tx'=4,'tc'=2] {'tc'}, dimensions={0} | all-to-all | bytes 1048576 | tf_op jit(solution)/shard_map/all_to_all | solution.py:300
  215.8 0.8 copy.166
  (74 shorter events, 2.6 us)
Async XLA Ops:
  0.0 177.2 %copy-start = (bf16[1024,256]{1,0:T(8,128)(2,1)S(1)}, bf16[1024,256]{1,0:T(8,128)(2,1)}, u32[]{:S(2)}) copy-start(bf16[1024,256]{1,0:T(8,128)(2,1)} %param.17) | copy-start | bytes 1572868
  0.0 4.6 %copy-start.4 = (bf16[256]{0:T(256)(128)(2,1)S(1)}, bf16[256]{0:T(256)(128)(2,1)}, u32[]{:S(2)}) copy-start(bf16[256]{0:T(256)(128)(2,1)} %param.13) | copy-start | bytes 1540
  0.0 4.7 %copy-start.2 = (bf16[32,8192]{1,0:T(8,128)(2,1)S(1)}, bf16[32,8192]{1,0:T(8,128)(2,1)}, u32[]{:S(2)}) copy-start(bf16[32,8192]{1,0:T(8,128)(2,1)} %param.12) | copy-start | bytes 1572868
  2.4 46.0 %collective-permute-start.1 = (bf16[256,640]{1,0:T(8,128)(2,1)S(1)}, bf16[256,640]{1,0:T(8,128)(2,1)S(1)}, u32[]{:S(2)}, u32[]{:S(2)}) collective-permute-start(bf16[256,640]{1,0:T(8,128)(2,1)S(1)} %get-tuple-element.24), channel_id=1, source_target_pairs={{0,64},{8,72},{16,80},{24,88},{32,96},{40,104},{48,112},{56,120},{... | collective-permute-start | bytes 983048 | tf_op jit(solution)/shard_map/ppermute | solution.py:147
  4.6 43.8 %collective-permute-start = (bf16[256]{0:T(256)(128)(2,1)S(1)}, bf16[256]{0:T(256)(128)(2,1)S(1)}, u32[]{:S(2)}, u32[]{:S(2)}) collective-permute-start(bf16[256]{0:T(256)(128)(2,1)S(1)} %copy-done.4), channel_id=1, source_target_pairs={{0,64},{8,72},{16,80},{24,88},{32,96},{40,104},{48,112},{56,120},{... | collective-permute-start | bytes 1544 | tf_op jit(solution)/shard_map/ppermute | solution.py:148
  6.0 12.4 %copy-start.3 = (s32[1024]{0:T(1024)S(1)}, s32[1024]{0:T(1024)}, u32[]{:S(2)}) copy-start(s32[1024]{0:T(1024)} %param.20) | copy-start | bytes 12292
  7.2 41.3 %all-to-all-start = ((bf16[32,32,512]{2,1,0:T(8,128)(2,1)}), bf16[32,32,512]{2,1,0:T(8,128)(2,1)S(1)}, u32[]{:S(2)}, u32[]{:S(2)}) async-start(bf16[32,32,512]{2,1,0:T(8,128)(2,1)} %bitcast.4), calls=%async_computation | async-start | bytes 2097152 | tf_op jit(solution)/shard_map/all_to_all | solution.py:167
  42.7 4.1 %copy-start.1 = (s32[1024]{0:T(1024)S(1)}, s32[1024]{0:T(1024)}, u32[]{:S(2)}) copy-start(s32[1024]{0:T(1024)} %param.19) | copy-start | bytes 12292
  50.6 40.2 %all-to-all-start.1 = ((bf16[32,32,640]{2,1,0:T(8,128)(2,1)}), bf16[32,32,640]{2,1,0:T(8,128)(2,1)S(1)}, u32[]{:S(2)}, u32[]{:S(2)}) async-start(bf16[32,32,640]{2,1,0:T(8,128)(2,1)} %bitcast.81), calls=%async_computation.1 | async-start | bytes 2621440 | tf_op jit(solution)/shard_map/all_to_all | solution.py:175
  93.6 16.9 %all-to-all-start.2 = ((bf16[32,2,10,128]{3,1,2,0:T(2,128)(2,1)}), bf16[32,2,10,128]{3,1,2,0:T(2,128)(2,1)S(1)}, u32[]{:S(2)}, u32[]{:S(2)}) async-start(bf16[32,2,10,128]{3,1,2,0:T(2,128)(2,1)} %copy.150), calls=%async_computation.2 | async-start | bytes 327680 | tf_op jit(solution)/shard_map/all_to_all | solution.py:236
  122.8 14.4 %all-to-all-start.3 = ((bf16[32,2,1024]{2,1,0:T(2,128)(2,1)}), bf16[32,2,1024]{2,1,0:T(2,128)(2,1)S(1)}, u32[]{:S(2)}, u32[]{:S(2)}) async-start(bf16[32,2,1024]{2,1,0:T(2,128)(2,1)} %broadcast_select_fusion.5), calls=%async_computation.3 | async-start | bytes 262144 | tf_op jit(solution)/shard_map/all_to_all | solution.py:268

commit v11 on v7

--- a/solution.py
+++ b/solution.py
@@ -9,7 +9,7 @@
 from jax.sharding import PartitionSpec as P
 
 HEAD_DIM = 128
-SLOTS_PER_STEP = 8
+SLOTS_PER_STEP = 16
 PLANE_Y = 4
 DP = ("dy", "dz")
 TP = ("tx", "tc")

time: 217 us -> 216 us (level)
  no operation moved by 1% of the time
where the time goes in v11:
time: 216 us; the launch traced here: 215 us
  blocking collectives  76.5 us (35%)
  waiting for transfers between devices  44.9 us (21%)
  local copies, waits for them, and re-layouts  37.1 us (17%)
  starting transfers between devices  34.9 us (16%)
  other arithmetic  9.61 us (4%)
  Pallas kernels  8.62 us (4%)
  matrix products  2.81 us (1%)
    all_to_all x1, waiting for transfers between devices, body(): lax.all_to_all(partial.astype(jnp.bfloat16).reshape(device_count, local_b...  27.3 us
    all_to_all x1, blocking collectives, body(): lax.all_to_all(jnp.broadcast_to(along_z[None], (y_count,) + along_z.shape...  23.4 us
    all_to_all x1, blocking collectives, body(): lax.all_to_all(jnp.broadcast_to(attention[None], (z_count,) + attention.s...  15.5 us
    unnamed x15, local copies, waits for them, and re-layouts  14.5 us
    all_to_all x1, blocking collectives, body(): lax.all_to_all(on_chip.reshape(ring_count, chunk_rows, out_width), 'tx',...  12.4 us
    all_to_all x1, starting transfers between devices, body(): lax.all_to_all(spread, DP, 0, 0, tiled=True)  10.9 us
    all_to_all x1, blocking collectives, body(): lax.all_to_all(partial_sum.reshape(core_count, total_rows // core_count,...  10.5 us
    slice x1, local copies, waits for them, and re-layouts, body(): values = key_value_cache[:, :, 1, 0, :]  10.1 us
  transfers between devices with their start and end apart: 6, of which 3 were waited for; matrix products, arithmetic and copies ran while one was open for 16% of the time, Pallas kernels for 0%

profile of v11, /device:TPU:1, one launch (start us, length us, event | category | flops | bytes accessed | tf_op | source)
XLA Modules:
  0.0 215.0 jit_solution(10410524526195333276)
XLA Ops:
  0.0 1.1 fusion.38
  1.2 1.0 fusion.39
  2.2 0.2 broadcast_select_fusion.1
  2.4 2.5 %collective-permute-start.1 = (bf16[256,640]{1,0:T(8,128)(2,1)S(1)}, bf16[256,640]{1,0:T(8,128)(2,1)S(1)}, u32[]{:S(2)}, u32[]{:S(2)}) collective-permute-start(bf16[256,640]{1,0:T(8,128)(2,1)S(1)} %get-tuple-element.24), channel_id=1, source_target_pairs={{0,8},{8,0},{16,24},{24,16},{32,40},{40,32},{48,56},{56,48},{64,72... | collective-permute-start | bytes 983048 | tf_op jit(solution)/shard_map/ppermute | solution.py:147
  5.0 0.1 collective-permute-start
  5.1 1.1 broadcast_in_dim.198
  6.2 10.9 %all-to-all-start = ((bf16[32,32,512]{2,1,0:T(8,128)(2,1)}), bf16[32,32,512]{2,1,0:T(8,128)(2,1)S(1)}, u32[]{:S(2)}, u32[]{:S(2)}) async-start(bf16[32,32,512]{2,1,0:T(8,128)(2,1)} %bitcast.3), calls=%async_computation | async-start | bytes 2097152 | tf_op jit(solution)/shard_map/all_to_all | solution.py:160
  17.3 0.8 convert_reduce_fusion.1
  18.2 0.1 fusion.11
  18.4 10.1 %fusion.37 = (bf16[32,256,1,1,128]{4,2,3,1,0:T(2,128)(2,1)}, bf16[32,256,1,1,128]{4,2,3,1,0:T(2,128)(2,1)}) fusion(bf16[32,256,2,1,128]{4,2,3,1,0:T(2,128)(2,1)} %param.18), kind=kLoop, calls=%fused_computation.140 | loop fusion | bytes 8388608 | tf_op jit(solution)/shard_map/slice | solution.py:191
  28.5 9.8 %copy.137 = bf16[32,256,1,1,128]{1,4,0,3,2:T(8,128)(2,1)} copy(bf16[32,256,1,1,128]{4,2,3,1,0:T(2,128)(2,1)} %get-tuple-element.22) | data formatting | bytes 4194304
  38.7 0.1 select_reduce_fusion
  39.0 0.6 convert_reduce_fusion.3
  39.6 0.1 fusion.12
  39.7 0.2 convert_reduce_fusion.2
  40.0 0.8 fusion.14
  40.8 0.6 iota_reduce_fusion
  41.4 3.9 %copy.143 = bf16[32,256,1,1,128]{4,1,0,3,2:T(8,128)(2,1)} copy(bf16[32,256,1,1,128]{4,2,3,1,0:T(2,128)(2,1)} %get-tuple-element.21) | data formatting | bytes 4194304
  45.3 0.1 broadcast_in_dim.196
  45.4 0.1 broadcast_in_dim.194
  45.5 0.7 gather_fusion.1
  46.2 0.7 gather_fusion
  47.0 0.1 sub.51
  47.2 2.1 convolution_convert_fusion
  49.3 9.2 %all-to-all-start.1 = ((bf16[32,32,640]{2,1,0:T(8,128)(2,1)}), bf16[32,32,640]{2,1,0:T(8,128)(2,1)S(1)}, u32[]{:S(2)}, u32[]{:S(2)}) async-start(bf16[32,32,640]{2,1,0:T(8,128)(2,1)} %bitcast.94), calls=%async_computation.1 | async-start | bytes 2621440 | tf_op jit(solution)/shard_map/all_to_all | solution.py:168
  58.6 0.1 select_reduce_fusion.1
  58.8 0.8 gather_fusion.6
  59.6 0.8 gather_fusion.7
  60.3 0.1 gt.42
  60.5 0.1 fusion.13
  60.6 0.2 multiply_reduce_fusion
  60.9 0.6 broadcast_select_fusion.6
  61.5 0.6 broadcast_select_fusion.7.parent_ref
  62.0 0.1 multiply_cosine_fusion.1
  62.2 27.3 %all-to-all-done.1 = bf16[32,32,640]{2,1,0:T(8,128)(2,1)S(1)} async-done(((bf16[32,32,640]{2,1,0:T(8,128)(2,1)}), bf16[32,32,640]{2,1,0:T(8,128)(2,1)S(1)}, u32[]{:S(2)}, u32[]{:S(2)}) %all-to-all-start.1) | async-done | bytes 1310752 | tf_op jit(solution)/shard_map/all_to_all | solution.py:168
  89.5 0.2 convert_reduce_fusion
  90.0 0.1 fusion.21
  90.3 0.1 subtract_convert_fusion
  90.5 0.6 gather_fusion.2
  91.2 0.3 broadcast_select_fusion.3
  91.5 0.8 copy.130
  92.3 7.6 %all-to-all-start.2 = ((bf16[32,2,10,128]{3,1,2,0:T(2,128)(2,1)}), bf16[32,2,10,128]{3,1,2,0:T(2,128)(2,1)S(1)}, u32[]{:S(2)}, u32[]{:S(2)}) async-start(bf16[32,2,10,128]{3,1,2,0:T(2,128)(2,1)} %copy.130), calls=%async_computation.2 | async-start | bytes 327680 | tf_op jit(solution)/shard_map/all_to_all | solution.py:226
  100.0 9.2 %all-to-all-done.2 = bf16[32,2,10,128]{3,1,2,0:T(2,128)(2,1)S(1)} async-done(((bf16[32,2,10,128]{3,1,2,0:T(2,128)(2,1)}), bf16[32,2,10,128]{3,1,2,0:T(2,128)(2,1)S(1)}, u32[]{:S(2)}, u32[]{:S(2)}) %all-to-all-start.2) | async-done | bytes 163872 | tf_op jit(solution)/shard_map/all_to_all | solution.py:226
  109.2 0.1 copy.131
  109.3 0.1 copy.135
  109.5 0.6 gather_fusion.3
  110.1 0.8 broadcast_select_fusion.4.packed_ref
  110.9 8.6 %shard_map.100 = bf16[64,8,128]{2,1,0:T(8,128)(2,1)} custom-call(s32[64]{0:T(128)} %broadcast_select_fusion.7.parent_ref, s32[64]{0:T(128)} %get-tuple-element.19.length_ref, bf16[64,10,128]{2,1,0:T(8,128)(2,1)} %broadcast_select_fusion.4.packed_ref, bf16[32,128,256]{2,1,0:T(8,128)(2,1)} %bitcast.55, bf16[32,128,256]{2,1,0:T(8,128)(2,1)} %bitcast.56, ...), custom_call_target="tpu_custom_call" | custom-call | tf_op jit(solution)/shard_map/pallas_call | solution.py:103
  119.6 1.5 gather_fusion.4
  121.1 0.9 broadcast_select_fusion.5
  122.0 4.5 %all-to-all-start.3 = ((bf16[32,2,1024]{2,1,0:T(2,128)(2,1)}), bf16[32,2,1024]{2,1,0:T(2,128)(2,1)S(1)}, u32[]{:S(2)}, u32[]{:S(2)}) async-start(bf16[32,2,1024]{2,1,0:T(2,128)(2,1)} %broadcast_select_fusion.5), calls=%async_computation.3 | async-start | bytes 262144 | tf_op jit(solution)/shard_map/all_to_all | solution.py:258
  126.5 0.8 dynamic-slice_compare_fusion
  127.3 8.4 %all-to-all-done.3 = bf16[32,2,1024]{2,1,0:T(2,128)(2,1)S(1)} async-done(((bf16[32,2,1024]{2,1,0:T(2,128)(2,1)}), bf16[32,2,1024]{2,1,0:T(2,128)(2,1)S(1)}, u32[]{:S(2)}, u32[]{:S(2)}) %all-to-all-start.3) | async-done | bytes 131104 | tf_op jit(solution)/shard_map/all_to_all | solution.py:258
  135.7 0.6 gather_fusion.5
  136.5 15.5 %all_to_all.50 = bf16[8,32,1024]{2,1,0:T(8,128)(2,1)S(1)} all-to-all(bf16[8,32,1024]{2,1,0:T(8,128)(2,1)S(1)} %broadcast_in_dim.209), channel_id=1, replica_groups=mesh['dy'=4,'dz'=8,'tx'=4,'tc'=2] {'dz'}, dimensions={0} | all-to-all | bytes 1048576 | tf_op jit(solution)/shard_map/all_to_all | solution.py:266
  151.9 0.3 broadcast_in_dim.211
  152.2 23.4 %all_to_all.51 = bf16[4,256,1024]{2,1,0:T(8,128)(2,1)S(1)} all-to-all(bf16[4,256,1024]{2,1,0:T(8,128)(2,1)S(1)} %broadcast_in_dim.211), channel_id=1, replica_groups=mesh['dy'=4,'dz'=8,'tx'=4,'tc'=2] {'dy'}, dimensions={0} | all-to-all | bytes 4194304 | tf_op jit(solution)/shard_map/all_to_all | solution.py:269
  175.6 0.7 fusion.9
  176.3 10.5 %all_to_all.52 = f32[2,512,256]{2,1,0:T(8,128)S(1)} all-to-all(f32[2,512,256]{2,1,0:T(8,128)S(1)} %fusion.9), channel_id=1, replica_groups=mesh['dy'=4,'dz'=8,'tx'=4,'tc'=2] {'tc'}, dimensions={0} | all-to-all | bytes 2097152 | tf_op jit(solution)/shard_map/all_to_all | solution.py:277
  186.9 0.1 reduce_sum.91
  187.0 12.4 %all_to_all.53 = f32[4,128,256]{2,1,0:T(8,128)S(1)} all-to-all(f32[4,128,256]{2,1,0:T(8,128)S(1)} %bitcast.92), channel_id=1, replica_groups=mesh['dy'=4,'dz'=8,'tx'=4,'tc'=2] {'tx'}, dimensions={0} | all-to-all | bytes 1048576 | tf_op jit(solution)/shard_map/all_to_all | solution.py:284
  199.5 7.9 %all_to_all.54 = bf16[4,128,256]{2,1,0:T(8,128)(2,1)S(1)} all-to-all(bf16[4,128,256]{2,1,0:T(8,128)(2,1)S(1)} %broadcast_in_dim.212), channel_id=1, replica_groups=mesh['dy'=4,'dz'=8,'tx'=4,'tc'=2] {'tx'}, dimensions={0} | all-to-all | bytes 524288 | tf_op jit(solution)/shard_map/all_to_all | solution.py:287
  207.4 6.7 %all_to_all.55 = bf16[2,512,256]{2,1,0:T(8,128)(2,1)S(1)} all-to-all(bf16[2,512,256]{2,1,0:T(8,128)(2,1)S(1)} %broadcast_in_dim.214), channel_id=1, replica_groups=mesh['dy'=4,'dz'=8,'tx'=4,'tc'=2] {'tc'}, dimensions={0} | all-to-all | bytes 1048576 | tf_op jit(solution)/shard_map/all_to_all | solution.py:290
  214.2 0.8 copy.146
  (71 shorter events, 2.2 us)
Async XLA Ops:
  0.0 175.6 %copy-start = (bf16[1024,256]{1,0:T(8,128)(2,1)S(1)}, bf16[1024,256]{1,0:T(8,128)(2,1)}, u32[]{:S(2)}) copy-start(bf16[1024,256]{1,0:T(8,128)(2,1)} %param.17) | copy-start | bytes 1572868
  0.0 4.9 %copy-start.4 = (bf16[256]{0:T(256)(128)(2,1)S(1)}, bf16[256]{0:T(256)(128)(2,1)}, u32[]{:S(2)}) copy-start(bf16[256]{0:T(256)(128)(2,1)} %param.13) | copy-start | bytes 1540
  0.0 5.1 %copy-start.2 = (bf16[32,8192]{1,0:T(8,128)(2,1)S(1)}, bf16[32,8192]{1,0:T(8,128)(2,1)}, u32[]{:S(2)}) copy-start(bf16[32,8192]{1,0:T(8,128)(2,1)} %param.12) | copy-start | bytes 1572868
  2.4 44.8 %collective-permute-start.1 = (bf16[256,640]{1,0:T(8,128)(2,1)S(1)}, bf16[256,640]{1,0:T(8,128)(2,1)S(1)}, u32[]{:S(2)}, u32[]{:S(2)}) collective-permute-start(bf16[256,640]{1,0:T(8,128)(2,1)S(1)} %get-tuple-element.24), channel_id=1, source_target_pairs={{0,8},{8,0},{16,24},{24,16},{32,40},{40,32},{48,56},{56,48},{64,72... | collective-permute-start | bytes 983048 | tf_op jit(solution)/shard_map/ppermute | solution.py:147
  5.0 42.2 %collective-permute-start = (bf16[256]{0:T(256)(128)(2,1)S(1)}, bf16[256]{0:T(256)(128)(2,1)S(1)}, u32[]{:S(2)}, u32[]{:S(2)}) collective-permute-start(bf16[256]{0:T(256)(128)(2,1)S(1)} %copy-done.4), channel_id=1, source_target_pairs={{0,8},{8,0},{16,24},{24,16},{32,40},{40,32},{48,56},{56,48},{64,72... | collective-permute-start | bytes 1544 | tf_op jit(solution)/shard_map/ppermute | solution.py:148
  5.1 12.1 %copy-start.3 = (s32[1024]{0:T(1024)S(1)}, s32[1024]{0:T(1024)}, u32[]{:S(2)}) copy-start(s32[1024]{0:T(1024)} %param.20) | copy-start | bytes 12292
  6.2 41.0 %all-to-all-start = ((bf16[32,32,512]{2,1,0:T(8,128)(2,1)}), bf16[32,32,512]{2,1,0:T(8,128)(2,1)S(1)}, u32[]{:S(2)}, u32[]{:S(2)}) async-start(bf16[32,32,512]{2,1,0:T(8,128)(2,1)} %bitcast.3), calls=%async_computation | async-start | bytes 2097152 | tf_op jit(solution)/shard_map/all_to_all | solution.py:160
  41.4 4.1 %copy-start.1 = (s32[1024]{0:T(1024)S(1)}, s32[1024]{0:T(1024)}, u32[]{:S(2)}) copy-start(s32[1024]{0:T(1024)} %param.19) | copy-start | bytes 12292
  49.3 40.2 %all-to-all-start.1 = ((bf16[32,32,640]{2,1,0:T(8,128)(2,1)}), bf16[32,32,640]{2,1,0:T(8,128)(2,1)S(1)}, u32[]{:S(2)}, u32[]{:S(2)}) async-start(bf16[32,32,640]{2,1,0:T(8,128)(2,1)} %bitcast.94), calls=%async_computation.1 | async-start | bytes 2621440 | tf_op jit(solution)/shard_map/all_to_all | solution.py:168
  92.3 16.9 %all-to-all-start.2 = ((bf16[32,2,10,128]{3,1,2,0:T(2,128)(2,1)}), bf16[32,2,10,128]{3,1,2,0:T(2,128)(2,1)S(1)}, u32[]{:S(2)}, u32[]{:S(2)}) async-start(bf16[32,2,10,128]{3,1,2,0:T(2,128)(2,1)} %copy.130), calls=%async_computation.2 | async-start | bytes 327680 | tf_op jit(solution)/shard_map/all_to_all | solution.py:226
  122.0 13.6 %all-to-all-start.3 = ((bf16[32,2,1024]{2,1,0:T(2,128)(2,1)}), bf16[32,2,1024]{2,1,0:T(2,128)(2,1)S(1)}, u32[]{:S(2)}, u32[]{:S(2)}) async-start(bf16[32,2,1024]{2,1,0:T(2,128)(2,1)} %broadcast_select_fusion.5), calls=%async_computation.3 | async-start | bytes 262144 | tf_op jit(solution)/shard_map/all_to_all | solution.py:258

commit v12 on v11

--- a/solution.py
+++ b/solution.py
@@ -9,7 +9,7 @@
 from jax.sharding import PartitionSpec as P
 
 HEAD_DIM = 128
-SLOTS_PER_STEP = 16
+SLOTS_PER_STEP = 32
 PLANE_Y = 4
 DP = ("dy", "dz")
 TP = ("tx", "tc")

time: 216 us -> 217 us (level)
  no operation moved by 1% of the time
where the time goes in v12:
time: 217 us; the launch traced here: 216 us
  blocking collectives  76.5 us (35%)
  waiting for transfers between devices  44.8 us (21%)
  local copies, waits for them, and re-layouts  37.1 us (17%)
  starting transfers between devices  36.3 us (17%)
  other arithmetic  9.61 us (4%)
  Pallas kernels  8.39 us (4%)
  matrix products  2.81 us (1%)
    all_to_all x1, waiting for transfers between devices, body(): lax.all_to_all(partial.astype(jnp.bfloat16).reshape(device_count, local_b...  27.3 us
    all_to_all x1, blocking collectives, body(): lax.all_to_all(jnp.broadcast_to(along_z[None], (y_count,) + along_z.shape...  23.4 us
    all_to_all x1, blocking collectives, body(): lax.all_to_all(jnp.broadcast_to(attention[None], (z_count,) + attention.s...  15.5 us
    unnamed x15, local copies, waits for them, and re-layouts  14.5 us
    all_to_all x1, blocking collectives, body(): lax.all_to_all(on_chip.reshape(ring_count, chunk_rows, out_width), 'tx',...  12.4 us
    all_to_all x1, starting transfers between devices, body(): lax.all_to_all(spread, DP, 0, 0, tiled=True)  10.9 us
    all_to_all x1, blocking collectives, body(): lax.all_to_all(partial_sum.reshape(core_count, total_rows // core_count,...  10.5 us
    slice x1, local copies, waits for them, and re-layouts, body(): values = key_value_cache[:, :, 1, 0, :]  10.1 us
  transfers between devices with their start and end apart: 6, of which 3 were waited for; matrix products, arithmetic and copies ran while one was open for 16% of the time, Pallas kernels for 0%

profile of v12, /device:TPU:1, one launch (start us, length us, event | category | flops | bytes accessed | tf_op | source)
XLA Modules:
  0.0 215.9 jit_solution(3842994635679031394)
XLA Ops:
  0.0 1.1 fusion.38
  1.2 1.0 fusion.39
  2.2 0.2 broadcast_select_fusion.1
  2.4 2.5 %collective-permute-start.1 = (bf16[256,640]{1,0:T(8,128)(2,1)S(1)}, bf16[256,640]{1,0:T(8,128)(2,1)S(1)}, u32[]{:S(2)}, u32[]{:S(2)}) collective-permute-start(bf16[256,640]{1,0:T(8,128)(2,1)S(1)} %get-tuple-element.24), channel_id=1, source_target_pairs={{0,8},{8,0},{16,24},{24,16},{32,40},{40,32},{48,56},{56,48},{64,72... | collective-permute-start | bytes 983048 | tf_op jit(solution)/shard_map/ppermute | solution.py:147
  5.0 0.1 collective-permute-start
  5.1 1.1 broadcast_in_dim.198
  6.2 10.9 %all-to-all-start = ((bf16[32,32,512]{2,1,0:T(8,128)(2,1)}), bf16[32,32,512]{2,1,0:T(8,128)(2,1)S(1)}, u32[]{:S(2)}, u32[]{:S(2)}) async-start(bf16[32,32,512]{2,1,0:T(8,128)(2,1)} %bitcast.3), calls=%async_computation | async-start | bytes 2097152 | tf_op jit(solution)/shard_map/all_to_all | solution.py:160
  17.3 0.8 convert_reduce_fusion.1
  18.2 0.1 fusion.11
  18.4 10.1 %fusion.37 = (bf16[32,256,1,1,128]{4,2,3,1,0:T(2,128)(2,1)}, bf16[32,256,1,1,128]{4,2,3,1,0:T(2,128)(2,1)}) fusion(bf16[32,256,2,1,128]{4,2,3,1,0:T(2,128)(2,1)} %param.18), kind=kLoop, calls=%fused_computation.140 | loop fusion | bytes 8388608 | tf_op jit(solution)/shard_map/slice | solution.py:191
  28.5 9.8 %copy.137 = bf16[32,256,1,1,128]{1,4,0,3,2:T(8,128)(2,1)} copy(bf16[32,256,1,1,128]{4,2,3,1,0:T(2,128)(2,1)} %get-tuple-element.22) | data formatting | bytes 4194304
  38.7 0.1 select_reduce_fusion
  39.0 0.6 convert_reduce_fusion.3
  39.6 0.1 fusion.12
  39.7 0.2 convert_reduce_fusion.2
  40.0 0.8 fusion.14
  40.8 0.6 iota_reduce_fusion
  41.4 3.9 %copy.143 = bf16[32,256,1,1,128]{4,1,0,3,2:T(8,128)(2,1)} copy(bf16[32,256,1,1,128]{4,2,3,1,0:T(2,128)(2,1)} %get-tuple-element.21) | data formatting | bytes 4194304
  45.3 0.1 broadcast_in_dim.196
  45.4 0.1 broadcast_in_dim.194
  45.5 0.7 gather_fusion.1
  46.2 0.7 gather_fusion
  47.0 0.1 sub.51
  47.2 2.1 convolution_convert_fusion
  49.3 9.2 %all-to-all-start.1 = ((bf16[32,32,640]{2,1,0:T(8,128)(2,1)}), bf16[32,32,640]{2,1,0:T(8,128)(2,1)S(1)}, u32[]{:S(2)}, u32[]{:S(2)}) async-start(bf16[32,32,640]{2,1,0:T(8,128)(2,1)} %bitcast.126), calls=%async_computation.1 | async-start | bytes 2621440 | tf_op jit(solution)/shard_map/all_to_all | solution.py:168
  58.6 0.1 select_reduce_fusion.1
  58.8 0.8 gather_fusion.6
  59.6 0.8 gather_fusion.7
  60.3 0.1 gt.42
  60.5 0.1 fusion.13
  60.6 0.2 multiply_reduce_fusion
  60.9 0.6 broadcast_select_fusion.6
  61.5 0.6 broadcast_select_fusion.7.parent_ref
  62.0 0.1 multiply_cosine_fusion.1
  62.2 27.3 %all-to-all-done.1 = bf16[32,32,640]{2,1,0:T(8,128)(2,1)S(1)} async-done(((bf16[32,32,640]{2,1,0:T(8,128)(2,1)}), bf16[32,32,640]{2,1,0:T(8,128)(2,1)S(1)}, u32[]{:S(2)}, u32[]{:S(2)}) %all-to-all-start.1) | async-done | bytes 1310752 | tf_op jit(solution)/shard_map/all_to_all | solution.py:168
  89.5 0.2 convert_reduce_fusion
  90.0 0.1 fusion.21
  90.3 0.1 subtract_convert_fusion
  90.5 0.6 gather_fusion.2
  91.2 0.3 broadcast_select_fusion.3
  91.5 0.8 copy.130
  92.3 7.8 %all-to-all-start.2 = ((bf16[32,2,10,128]{3,1,2,0:T(2,128)(2,1)}), bf16[32,2,10,128]{3,1,2,0:T(2,128)(2,1)S(1)}, u32[]{:S(2)}, u32[]{:S(2)}) async-start(bf16[32,2,10,128]{3,1,2,0:T(2,128)(2,1)} %copy.130), calls=%async_computation.2 | async-start | bytes 327680 | tf_op jit(solution)/shard_map/all_to_all | solution.py:226
  100.2 9.0 %all-to-all-done.2 = bf16[32,2,10,128]{3,1,2,0:T(2,128)(2,1)S(1)} async-done(((bf16[32,2,10,128]{3,1,2,0:T(2,128)(2,1)}), bf16[32,2,10,128]{3,1,2,0:T(2,128)(2,1)S(1)}, u32[]{:S(2)}, u32[]{:S(2)}) %all-to-all-start.2) | async-done | bytes 163872 | tf_op jit(solution)/shard_map/all_to_all | solution.py:226
  109.2 0.1 copy.131
  109.3 0.1 copy.135
  109.5 0.6 gather_fusion.3
  110.1 0.8 broadcast_select_fusion.4.packed_ref
  111.0 8.4 %shard_map.100 = bf16[64,8,128]{2,1,0:T(8,128)(2,1)} custom-call(s32[64]{0:T(128)} %broadcast_select_fusion.7.parent_ref, s32[64]{0:T(128)} %get-tuple-element.19.length_ref, bf16[64,10,128]{2,1,0:T(8,128)(2,1)} %broadcast_select_fusion.4.packed_ref, bf16[32,128,256]{2,1,0:T(8,128)(2,1)} %bitcast.70, bf16[32,128,256]{2,1,0:T(8,128)(2,1)} %bitcast.86, ...), custom_call_target="tpu_custom_call" | custom-call | tf_op jit(solution)/shard_map/pallas_call | solution.py:103
  119.3 1.5 gather_fusion.4
  120.9 0.9 broadcast_select_fusion.5
  121.8 5.7 %all-to-all-start.3 = ((bf16[32,2,1024]{2,1,0:T(2,128)(2,1)}), bf16[32,2,1024]{2,1,0:T(2,128)(2,1)S(1)}, u32[]{:S(2)}, u32[]{:S(2)}) async-start(bf16[32,2,1024]{2,1,0:T(2,128)(2,1)} %broadcast_select_fusion.5), calls=%async_computation.3 | async-start | bytes 262144 | tf_op jit(solution)/shard_map/all_to_all | solution.py:258
  127.5 0.8 dynamic-slice_compare_fusion
  128.2 8.4 %all-to-all-done.3 = bf16[32,2,1024]{2,1,0:T(2,128)(2,1)S(1)} async-done(((bf16[32,2,1024]{2,1,0:T(2,128)(2,1)}), bf16[32,2,1024]{2,1,0:T(2,128)(2,1)S(1)}, u32[]{:S(2)}, u32[]{:S(2)}) %all-to-all-start.3) | async-done | bytes 131104 | tf_op jit(solution)/shard_map/all_to_all | solution.py:258
  136.7 0.6 gather_fusion.5
  137.5 15.5 %all_to_all.50 = bf16[8,32,1024]{2,1,0:T(8,128)(2,1)S(1)} all-to-all(bf16[8,32,1024]{2,1,0:T(8,128)(2,1)S(1)} %broadcast_in_dim.209), channel_id=1, replica_groups=mesh['dy'=4,'dz'=8,'tx'=4,'tc'=2] {'dz'}, dimensions={0} | all-to-all | bytes 1048576 | tf_op jit(solution)/shard_map/all_to_all | solution.py:266
  152.9 0.3 broadcast_in_dim.211
  153.2 23.4 %all_to_all.51 = bf16[4,256,1024]{2,1,0:T(8,128)(2,1)S(1)} all-to-all(bf16[4,256,1024]{2,1,0:T(8,128)(2,1)S(1)} %broadcast_in_dim.211), channel_id=1, replica_groups=mesh['dy'=4,'dz'=8,'tx'=4,'tc'=2] {'dy'}, dimensions={0} | all-to-all | bytes 4194304 | tf_op jit(solution)/shard_map/all_to_all | solution.py:269
  176.6 0.7 fusion.9
  177.3 10.5 %all_to_all.52 = f32[2,512,256]{2,1,0:T(8,128)S(1)} all-to-all(f32[2,512,256]{2,1,0:T(8,128)S(1)} %fusion.9), channel_id=1, replica_groups=mesh['dy'=4,'dz'=8,'tx'=4,'tc'=2] {'tc'}, dimensions={0} | all-to-all | bytes 2097152 | tf_op jit(solution)/shard_map/all_to_all | solution.py:277
  187.8 0.1 reduce_sum.91
  188.0 12.4 %all_to_all.53 = f32[4,128,256]{2,1,0:T(8,128)S(1)} all-to-all(f32[4,128,256]{2,1,0:T(8,128)S(1)} %bitcast.124), channel_id=1, replica_groups=mesh['dy'=4,'dz'=8,'tx'=4,'tc'=2] {'tx'}, dimensions={0} | all-to-all | bytes 1048576 | tf_op jit(solution)/shard_map/all_to_all | solution.py:284
  200.5 7.9 %all_to_all.54 = bf16[4,128,256]{2,1,0:T(8,128)(2,1)S(1)} all-to-all(bf16[4,128,256]{2,1,0:T(8,128)(2,1)S(1)} %broadcast_in_dim.212), channel_id=1, replica_groups=mesh['dy'=4,'dz'=8,'tx'=4,'tc'=2] {'tx'}, dimensions={0} | all-to-all | bytes 524288 | tf_op jit(solution)/shard_map/all_to_all | solution.py:287
  208.4 6.7 %all_to_all.55 = bf16[2,512,256]{2,1,0:T(8,128)(2,1)S(1)} all-to-all(bf16[2,512,256]{2,1,0:T(8,128)(2,1)S(1)} %broadcast_in_dim.214), channel_id=1, replica_groups=mesh['dy'=4,'dz'=8,'tx'=4,'tc'=2] {'tc'}, dimensions={0} | all-to-all | bytes 1048576 | tf_op jit(solution)/shard_map/all_to_all | solution.py:290
  215.2 0.8 copy.146
  (71 shorter events, 2.2 us)
Async XLA Ops:
  0.0 176.6 %copy-start = (bf16[1024,256]{1,0:T(8,128)(2,1)S(1)}, bf16[1024,256]{1,0:T(8,128)(2,1)}, u32[]{:S(2)}) copy-start(bf16[1024,256]{1,0:T(8,128)(2,1)} %param.17) | copy-start | bytes 1572868
  0.0 4.9 %copy-start.4 = (bf16[256]{0:T(256)(128)(2,1)S(1)}, bf16[256]{0:T(256)(128)(2,1)}, u32[]{:S(2)}) copy-start(bf16[256]{0:T(256)(128)(2,1)} %param.13) | copy-start | bytes 1540
  0.0 5.1 %copy-start.2 = (bf16[32,8192]{1,0:T(8,128)(2,1)S(1)}, bf16[32,8192]{1,0:T(8,128)(2,1)}, u32[]{:S(2)}) copy-start(bf16[32,8192]{1,0:T(8,128)(2,1)} %param.12) | copy-start | bytes 1572868
  2.4 44.8 %collective-permute-start.1 = (bf16[256,640]{1,0:T(8,128)(2,1)S(1)}, bf16[256,640]{1,0:T(8,128)(2,1)S(1)}, u32[]{:S(2)}, u32[]{:S(2)}) collective-permute-start(bf16[256,640]{1,0:T(8,128)(2,1)S(1)} %get-tuple-element.24), channel_id=1, source_target_pairs={{0,8},{8,0},{16,24},{24,16},{32,40},{40,32},{48,56},{56,48},{64,72... | collective-permute-start | bytes 983048 | tf_op jit(solution)/shard_map/ppermute | solution.py:147
  5.0 42.2 %collective-permute-start = (bf16[256]{0:T(256)(128)(2,1)S(1)}, bf16[256]{0:T(256)(128)(2,1)S(1)}, u32[]{:S(2)}, u32[]{:S(2)}) collective-permute-start(bf16[256]{0:T(256)(128)(2,1)S(1)} %copy-done.4), channel_id=1, source_target_pairs={{0,8},{8,0},{16,24},{24,16},{32,40},{40,32},{48,56},{56,48},{64,72... | collective-permute-start | bytes 1544 | tf_op jit(solution)/shard_map/ppermute | solution.py:148
  5.1 12.1 %copy-start.3 = (s32[1024]{0:T(1024)S(1)}, s32[1024]{0:T(1024)}, u32[]{:S(2)}) copy-start(s32[1024]{0:T(1024)} %param.20) | copy-start | bytes 12292
  6.2 41.0 %all-to-all-start = ((bf16[32,32,512]{2,1,0:T(8,128)(2,1)}), bf16[32,32,512]{2,1,0:T(8,128)(2,1)S(1)}, u32[]{:S(2)}, u32[]{:S(2)}) async-start(bf16[32,32,512]{2,1,0:T(8,128)(2,1)} %bitcast.3), calls=%async_computation | async-start | bytes 2097152 | tf_op jit(solution)/shard_map/all_to_all | solution.py:160
  41.4 4.1 %copy-start.1 = (s32[1024]{0:T(1024)S(1)}, s32[1024]{0:T(1024)}, u32[]{:S(2)}) copy-start(s32[1024]{0:T(1024)} %param.19) | copy-start | bytes 12292
  49.3 40.2 %all-to-all-start.1 = ((bf16[32,32,640]{2,1,0:T(8,128)(2,1)}), bf16[32,32,640]{2,1,0:T(8,128)(2,1)S(1)}, u32[]{:S(2)}, u32[]{:S(2)}) async-start(bf16[32,32,640]{2,1,0:T(8,128)(2,1)} %bitcast.126), calls=%async_computation.1 | async-start | bytes 2621440 | tf_op jit(solution)/shard_map/all_to_all | solution.py:168
  92.3 16.9 %all-to-all-start.2 = ((bf16[32,2,10,128]{3,1,2,0:T(2,128)(2,1)}), bf16[32,2,10,128]{3,1,2,0:T(2,128)(2,1)S(1)}, u32[]{:S(2)}, u32[]{:S(2)}) async-start(bf16[32,2,10,128]{3,1,2,0:T(2,128)(2,1)} %copy.130), calls=%async_computation.2 | async-start | bytes 327680 | tf_op jit(solution)/shard_map/all_to_all | solution.py:226
  121.8 14.8 %all-to-all-start.3 = ((bf16[32,2,1024]{2,1,0:T(2,128)(2,1)}), bf16[32,2,1024]{2,1,0:T(2,128)(2,1)S(1)}, u32[]{:S(2)}, u32[]{:S(2)}) async-start(bf16[32,2,1024]{2,1,0:T(2,128)(2,1)} %broadcast_select_fusion.5), calls=%async_computation.3 | async-start | bytes 262144 | tf_op jit(solution)/shard_map/all_to_all | solution.py:258

commit v13 on v11

--- a/solution.py
+++ b/solution.py
@@ -284,11 +284,11 @@
         lax.all_to_all(on_chip.reshape(ring_count, chunk_rows, out_width), "tx", 0, 0, tiled=True),
         axis=0,
     ).astype(jnp.bfloat16)
-    ring_copies = lax.all_to_all(
-        jnp.broadcast_to(reduced[None], (ring_count,) + reduced.shape), "tx", 0, 0, tiled=True
-    ).reshape(ring_count * chunk_rows, out_width)
-    return lax.all_to_all(
-        jnp.broadcast_to(ring_copies[None], (core_count,) + ring_copies.shape), "tc", 0, 0, tiled=True
+    copies = lax.all_to_all(
+        jnp.broadcast_to(reduced[None], (ring_count * core_count,) + reduced.shape), TP, 0, 0, tiled=True
+    )
+    return jnp.swapaxes(
+        copies.reshape(ring_count, core_count, chunk_rows, out_width), 0, 1
     ).reshape(total_rows, out_width)
 
 def solution(mesh):

time: 216 us -> 215 us (level)
    all_to_all x2 -> x1, blocking collectives: 14.7 us -> 13.5 us  [body(): lax.all_to_all(jnp.broadcast_to(reduced[None], (ring_count * core_count,)...]
    unnamed x15 -> x14, local copies, waits for them, and re-layouts: 14.5 us -> 13.7 us
  transfers between devices with their start and end apart: 6 -> 6, of which waited for: 3 -> 3; matrix products, arithmetic and copies ran while one was open for 16% -> 17% of each run, Pallas kernels for 0% -> 0%
where the time goes in v13:
time: 215 us; the launch traced here: 213 us
  blocking collectives  75.4 us (35%)
  waiting for transfers between devices  45 us (21%)
  local copies, waits for them, and re-layouts  37.1 us (17%)
  starting transfers between devices  34.9 us (16%)
  other arithmetic  9.61 us (4%)
  Pallas kernels  7.98 us (4%)
  matrix products  2.81 us (1%)
    all_to_all x1, waiting for transfers between devices, body(): lax.all_to_all(partial.astype(jnp.bfloat16).reshape(device_count, local_b...  27.3 us
    all_to_all x1, blocking collectives, body(): lax.all_to_all(jnp.broadcast_to(along_z[None], (y_count,) + along_z.shape...  23.5 us
    all_to_all x1, blocking collectives, body(): lax.all_to_all(jnp.broadcast_to(attention[None], (z_count,) + attention.s...  15.5 us
    unnamed x14, local copies, waits for them, and re-layouts  13.7 us
    all_to_all x1, blocking collectives, body(): lax.all_to_all(jnp.broadcast_to(reduced[None], (ring_count * core_count,)...  13.5 us
    all_to_all x1, blocking collectives, body(): lax.all_to_all(on_chip.reshape(ring_count, chunk_rows, out_width), 'tx',...  12.4 us
    all_to_all x1, starting transfers between devices, body(): lax.all_to_all(spread, DP, 0, 0, tiled=True)  10.9 us
    all_to_all x1, blocking collectives, body(): lax.all_to_all(partial_sum.reshape(core_count, total_rows // core_count,...  10.4 us
  transfers between devices with their start and end apart: 6, of which 3 were waited for; matrix products, arithmetic and copies ran while one was open for 17% of the time, Pallas kernels for 0%

profile of v13, /device:TPU:1, one launch (start us, length us, event | category | flops | bytes accessed | tf_op | source)
XLA Modules:
  0.0 213.3 jit_solution(4148600145033985445)
XLA Ops:
  0.0 1.1 fusion.38
  1.2 1.0 fusion.39
  2.2 0.2 broadcast_select_fusion.1
  2.4 2.5 %collective-permute-start.1 = (bf16[256,640]{1,0:T(8,128)(2,1)S(1)}, bf16[256,640]{1,0:T(8,128)(2,1)S(1)}, u32[]{:S(2)}, u32[]{:S(2)}) collective-permute-start(bf16[256,640]{1,0:T(8,128)(2,1)S(1)} %get-tuple-element.24), channel_id=1, source_target_pairs={{0,8},{8,0},{16,24},{24,16},{32,40},{40,32},{48,56},{56,48},{64,72... | collective-permute-start | bytes 983048 | tf_op jit(solution)/shard_map/ppermute | solution.py:147
  5.0 0.1 collective-permute-start
  5.1 1.1 broadcast_in_dim.191
  6.2 10.9 %all-to-all-start = ((bf16[32,32,512]{2,1,0:T(8,128)(2,1)}), bf16[32,32,512]{2,1,0:T(8,128)(2,1)S(1)}, u32[]{:S(2)}, u32[]{:S(2)}) async-start(bf16[32,32,512]{2,1,0:T(8,128)(2,1)} %bitcast.3), calls=%async_computation | async-start | bytes 2097152 | tf_op jit(solution)/shard_map/all_to_all | solution.py:160
  17.3 0.8 convert_reduce_fusion.1
  18.2 0.1 fusion.11
  18.4 10.1 %fusion.37 = (bf16[32,256,1,1,128]{4,2,3,1,0:T(2,128)(2,1)}, bf16[32,256,1,1,128]{4,2,3,1,0:T(2,128)(2,1)}) fusion(bf16[32,256,2,1,128]{4,2,3,1,0:T(2,128)(2,1)} %param.18), kind=kLoop, calls=%fused_computation.140 | loop fusion | bytes 8388608 | tf_op jit(solution)/shard_map/slice | solution.py:191
  28.5 9.8 %copy.158 = bf16[32,256,1,1,128]{1,4,0,3,2:T(8,128)(2,1)} copy(bf16[32,256,1,1,128]{4,2,3,1,0:T(2,128)(2,1)} %get-tuple-element.22) | data formatting | bytes 4194304
  38.7 0.1 select_reduce_fusion
  38.8 0.1 copy.141
  39.0 0.6 convert_reduce_fusion.3
  39.6 0.1 fusion.12
  39.7 0.2 convert_reduce_fusion.2
  40.0 0.8 fusion.14
  40.8 0.6 iota_reduce_fusion
  41.4 3.9 %copy.164 = bf16[32,256,1,1,128]{4,1,0,3,2:T(8,128)(2,1)} copy(bf16[32,256,1,1,128]{4,2,3,1,0:T(2,128)(2,1)} %get-tuple-element.21) | data formatting | bytes 4194304
  45.3 0.1 broadcast_in_dim.189
  45.4 0.1 broadcast_in_dim.187
  45.5 0.7 gather_fusion.1
  46.2 0.7 gather_fusion
  47.0 0.1 sub.51
  47.2 2.1 convolution_convert_fusion
  49.3 9.2 %all-to-all-start.1 = ((bf16[32,32,640]{2,1,0:T(8,128)(2,1)}), bf16[32,32,640]{2,1,0:T(8,128)(2,1)S(1)}, u32[]{:S(2)}, u32[]{:S(2)}) async-start(bf16[32,32,640]{2,1,0:T(8,128)(2,1)} %bitcast.96), calls=%async_computation.1 | async-start | bytes 2621440 | tf_op jit(solution)/shard_map/all_to_all | solution.py:168
  58.6 0.1 select_reduce_fusion.1
  58.8 0.8 gather_fusion.6
  59.6 0.8 gather_fusion.7
  60.3 0.1 gt.42
  60.5 0.1 fusion.13
  60.6 0.2 multiply_reduce_fusion
  60.9 0.6 broadcast_select_fusion.6
  61.5 0.6 broadcast_select_fusion.7.parent_ref
  62.0 0.1 multiply_cosine_fusion.1
  62.2 27.3 %all-to-all-done.1 = bf16[32,32,640]{2,1,0:T(8,128)(2,1)S(1)} async-done(((bf16[32,32,640]{2,1,0:T(8,128)(2,1)}), bf16[32,32,640]{2,1,0:T(8,128)(2,1)S(1)}, u32[]{:S(2)}, u32[]{:S(2)}) %all-to-all-start.1) | async-done | bytes 1310752 | tf_op jit(solution)/shard_map/all_to_all | solution.py:168
  89.5 0.2 convert_reduce_fusion
  90.0 0.1 fusion.21
  90.3 0.1 subtract_convert_fusion
  90.5 0.6 gather_fusion.2
  91.2 0.3 broadcast_select_fusion.3
  91.5 0.8 copy.150
  92.3 7.6 %all-to-all-start.2 = ((bf16[32,2,10,128]{3,1,2,0:T(2,128)(2,1)}), bf16[32,2,10,128]{3,1,2,0:T(2,128)(2,1)S(1)}, u32[]{:S(2)}, u32[]{:S(2)}) async-start(bf16[32,2,10,128]{3,1,2,0:T(2,128)(2,1)} %copy.150), calls=%async_computation.2 | async-start | bytes 327680 | tf_op jit(solution)/shard_map/all_to_all | solution.py:226
  100.0 9.2 %all-to-all-done.2 = bf16[32,2,10,128]{3,1,2,0:T(2,128)(2,1)S(1)} async-done(((bf16[32,2,10,128]{3,1,2,0:T(2,128)(2,1)}), bf16[32,2,10,128]{3,1,2,0:T(2,128)(2,1)S(1)}, u32[]{:S(2)}, u32[]{:S(2)}) %all-to-all-start.2) | async-done | bytes 163872 | tf_op jit(solution)/shard_map/all_to_all | solution.py:226
  109.2 0.1 copy.151
  109.3 0.1 copy.155
  109.5 0.6 gather_fusion.3
  110.1 0.8 broadcast_select_fusion.4.packed_ref
  111.0 8.0 %shard_map.100 = bf16[64,8,128]{2,1,0:T(8,128)(2,1)} custom-call(s32[64]{0:T(128)} %broadcast_select_fusion.7.parent_ref, s32[64]{0:T(128)} %get-tuple-element.19.length_ref, bf16[64,10,128]{2,1,0:T(8,128)(2,1)} %broadcast_select_fusion.4.packed_ref, bf16[32,128,256]{2,1,0:T(8,128)(2,1)} %bitcast.57, bf16[32,128,256]{2,1,0:T(8,128)(2,1)} %bitcast.58, ...), custom_call_target="tpu_custom_call" | custom-call | tf_op jit(solution)/shard_map/pallas_call | solution.py:103
  118.9 1.5 gather_fusion.4
  120.5 0.9 broadcast_select_fusion.5
  121.4 4.5 %all-to-all-start.3 = ((bf16[32,2,1024]{2,1,0:T(2,128)(2,1)}), bf16[32,2,1024]{2,1,0:T(2,128)(2,1)S(1)}, u32[]{:S(2)}, u32[]{:S(2)}) async-start(bf16[32,2,1024]{2,1,0:T(2,128)(2,1)} %broadcast_select_fusion.5), calls=%async_computation.3 | async-start | bytes 262144 | tf_op jit(solution)/shard_map/all_to_all | solution.py:258
  125.9 0.8 dynamic-slice_compare_fusion
  126.6 8.4 %all-to-all-done.3 = bf16[32,2,1024]{2,1,0:T(2,128)(2,1)S(1)} async-done(((bf16[32,2,1024]{2,1,0:T(2,128)(2,1)}), bf16[32,2,1024]{2,1,0:T(2,128)(2,1)S(1)}, u32[]{:S(2)}, u32[]{:S(2)}) %all-to-all-start.3) | async-done | bytes 131104 | tf_op jit(solution)/shard_map/all_to_all | solution.py:258
  135.1 0.6 gather_fusion.5
  135.9 15.5 %all_to_all.45 = bf16[8,32,1024]{2,1,0:T(8,128)(2,1)S(1)} all-to-all(bf16[8,32,1024]{2,1,0:T(8,128)(2,1)S(1)} %broadcast_in_dim.202), channel_id=1, replica_groups=mesh['dy'=4,'dz'=8,'tx'=4,'tc'=2] {'dz'}, dimensions={0} | all-to-all | bytes 1048576 | tf_op jit(solution)/shard_map/all_to_all | solution.py:266
  151.4 0.3 broadcast_in_dim.204
  151.6 23.5 %all_to_all.46 = bf16[4,256,1024]{2,1,0:T(8,128)(2,1)S(1)} all-to-all(bf16[4,256,1024]{2,1,0:T(8,128)(2,1)S(1)} %broadcast_in_dim.204), channel_id=1, replica_groups=mesh['dy'=4,'dz'=8,'tx'=4,'tc'=2] {'dy'}, dimensions={0} | all-to-all | bytes 4194304 | tf_op jit(solution)/shard_map/all_to_all | solution.py:269
  175.2 0.7 fusion.9
  175.9 10.4 %all_to_all.47 = f32[2,512,256]{2,1,0:T(8,128)S(1)} all-to-all(f32[2,512,256]{2,1,0:T(8,128)S(1)} %fusion.9), channel_id=1, replica_groups=mesh['dy'=4,'dz'=8,'tx'=4,'tc'=2] {'tc'}, dimensions={0} | all-to-all | bytes 2097152 | tf_op jit(solution)/shard_map/all_to_all | solution.py:277
  186.3 0.1 reduce_sum.91
  186.4 12.4 %all_to_all.48 = f32[4,128,256]{2,1,0:T(8,128)S(1)} all-to-all(f32[4,128,256]{2,1,0:T(8,128)S(1)} %bitcast.94), channel_id=1, replica_groups=mesh['dy'=4,'dz'=8,'tx'=4,'tc'=2] {'tx'}, dimensions={0} | all-to-all | bytes 1048576 | tf_op jit(solution)/shard_map/all_to_all | solution.py:284
  198.9 13.5 %all_to_all.49 = bf16[8,128,256]{2,1,0:T(8,128)(2,1)S(1)} all-to-all(bf16[8,128,256]{2,1,0:T(8,128)(2,1)S(1)} %broadcast_in_dim.205), channel_id=1, replica_groups=mesh['dy'=4,'dz'=8,'tx'=4,'tc'=2] {'tx','tc'}, dimensions={0} | all-to-all | bytes 1048576 | tf_op jit(solution)/shard_map/all_to_all | solution.py:287
  212.5 0.8 copy.157
  (69 shorter events, 2.1 us)
Async XLA Ops:
  0.0 175.2 %copy-start = (bf16[1024,256]{1,0:T(8,128)(2,1)S(1)}, bf16[1024,256]{1,0:T(8,128)(2,1)}, u32[]{:S(2)}) copy-start(bf16[1024,256]{1,0:T(8,128)(2,1)} %param.17) | copy-start | bytes 1572868
  0.0 4.9 %copy-start.4 = (bf16[256]{0:T(256)(128)(2,1)S(1)}, bf16[256]{0:T(256)(128)(2,1)}, u32[]{:S(2)}) copy-start(bf16[256]{0:T(256)(128)(2,1)} %param.13) | copy-start | bytes 1540
  0.0 5.1 %copy-start.2 = (bf16[32,8192]{1,0:T(8,128)(2,1)S(1)}, bf16[32,8192]{1,0:T(8,128)(2,1)}, u32[]{:S(2)}) copy-start(bf16[32,8192]{1,0:T(8,128)(2,1)} %param.12) | copy-start | bytes 1572868
  2.4 44.8 %collective-permute-start.1 = (bf16[256,640]{1,0:T(8,128)(2,1)S(1)}, bf16[256,640]{1,0:T(8,128)(2,1)S(1)}, u32[]{:S(2)}, u32[]{:S(2)}) collective-permute-start(bf16[256,640]{1,0:T(8,128)(2,1)S(1)} %get-tuple-element.24), channel_id=1, source_target_pairs={{0,8},{8,0},{16,24},{24,16},{32,40},{40,32},{48,56},{56,48},{64,72... | collective-permute-start | bytes 983048 | tf_op jit(solution)/shard_map/ppermute | solution.py:147
  5.0 42.2 %collective-permute-start = (bf16[256]{0:T(256)(128)(2,1)S(1)}, bf16[256]{0:T(256)(128)(2,1)S(1)}, u32[]{:S(2)}, u32[]{:S(2)}) collective-permute-start(bf16[256]{0:T(256)(128)(2,1)S(1)} %copy-done.4), channel_id=1, source_target_pairs={{0,8},{8,0},{16,24},{24,16},{32,40},{40,32},{48,56},{56,48},{64,72... | collective-permute-start | bytes 1544 | tf_op jit(solution)/shard_map/ppermute | solution.py:148
  5.1 12.1 %copy-start.3 = (s32[1024]{0:T(1024)S(1)}, s32[1024]{0:T(1024)}, u32[]{:S(2)}) copy-start(s32[1024]{0:T(1024)} %param.20) | copy-start | bytes 12292
  6.2 41.0 %all-to-all-start = ((bf16[32,32,512]{2,1,0:T(8,128)(2,1)}), bf16[32,32,512]{2,1,0:T(8,128)(2,1)S(1)}, u32[]{:S(2)}, u32[]{:S(2)}) async-start(bf16[32,32,512]{2,1,0:T(8,128)(2,1)} %bitcast.3), calls=%async_computation | async-start | bytes 2097152 | tf_op jit(solution)/shard_map/all_to_all | solution.py:160
  41.4 4.1 %copy-start.1 = (s32[1024]{0:T(1024)S(1)}, s32[1024]{0:T(1024)}, u32[]{:S(2)}) copy-start(s32[1024]{0:T(1024)} %param.19) | copy-start | bytes 12292
  49.3 40.2 %all-to-all-start.1 = ((bf16[32,32,640]{2,1,0:T(8,128)(2,1)}), bf16[32,32,640]{2,1,0:T(8,128)(2,1)S(1)}, u32[]{:S(2)}, u32[]{:S(2)}) async-start(bf16[32,32,640]{2,1,0:T(8,128)(2,1)} %bitcast.96), calls=%async_computation.1 | async-start | bytes 2621440 | tf_op jit(solution)/shard_map/all_to_all | solution.py:168
  92.3 16.9 %all-to-all-start.2 = ((bf16[32,2,10,128]{3,1,2,0:T(2,128)(2,1)}), bf16[32,2,10,128]{3,1,2,0:T(2,128)(2,1)S(1)}, u32[]{:S(2)}, u32[]{:S(2)}) async-start(bf16[32,2,10,128]{3,1,2,0:T(2,128)(2,1)} %copy.150), calls=%async_computation.2 | async-start | bytes 327680 | tf_op jit(solution)/shard_map/all_to_all | solution.py:226
  121.4 13.7 %all-to-all-start.3 = ((bf16[32,2,1024]{2,1,0:T(2,128)(2,1)}), bf16[32,2,1024]{2,1,0:T(2,128)(2,1)S(1)}, u32[]{:S(2)}, u32[]{:S(2)}) async-start(bf16[32,2,1024]{2,1,0:T(2,128)(2,1)} %broadcast_select_fusion.5), calls=%async_computation.3 | async-start | bytes 262144 | tf_op jit(solution)/shard_map/all_to_all | solution.py:258

commit v14 on v11

--- a/solution.py
+++ b/solution.py
@@ -273,22 +273,14 @@
     total_rows, out_width = partial_sum.shape
     core_count = lax.axis_size("tc")
     ring_count = lax.axis_size("tx")
-    on_chip = jnp.sum(
-        lax.all_to_all(
-            partial_sum.reshape(core_count, total_rows // core_count, out_width), "tc", 0, 0, tiled=True
-        ),
-        axis=0,
-    )
-    chunk_rows = total_rows // (core_count * ring_count)
+    group_size = core_count * ring_count
+    chunk_rows = total_rows // group_size
     reduced = jnp.sum(
-        lax.all_to_all(on_chip.reshape(ring_count, chunk_rows, out_width), "tx", 0, 0, tiled=True),
+        lax.all_to_all(partial_sum.reshape(group_size, chunk_rows, out_width), TP, 0, 0, tiled=True),
         axis=0,
     ).astype(jnp.bfloat16)
-    ring_copies = lax.all_to_all(
-        jnp.broadcast_to(reduced[None], (ring_count,) + reduced.shape), "tx", 0, 0, tiled=True
-    ).reshape(ring_count * chunk_rows, out_width)
     return lax.all_to_all(
-        jnp.broadcast_to(ring_copies[None], (core_count,) + ring_copies.shape), "tc", 0, 0, tiled=True
+        jnp.broadcast_to(reduced[None], (group_size,) + reduced.shape), TP, 0, 0, tiled=True
     ).reshape(total_rows, out_width)
 
 def solution(mesh):

time: 216 us -> 216 us (level)
    all_to_all x4 -> x2, blocking collectives: 37.6 us -> 38.1 us  [the longest x1 25.3 us: body(): lax.all_to_all(partial_sum.reshape(group_size, chunk_rows, out_width), TP...]
where the time goes in v14:
time: 216 us; the launch traced here: 215 us
  blocking collectives  77 us (36%)
  waiting for transfers between devices  44.9 us (21%)
  local copies, waits for them, and re-layouts  37.1 us (17%)
  starting transfers between devices  35.1 us (16%)
  other arithmetic  9.54 us (4%)
  Pallas kernels  8.19 us (4%)
  matrix products  2.81 us (1%)
    all_to_all x1, waiting for transfers between devices, body(): lax.all_to_all(partial.astype(jnp.bfloat16).reshape(device_count, local_b...  27.3 us
    all_to_all x1, blocking collectives, body(): lax.all_to_all(partial_sum.reshape(group_size, chunk_rows, out_width), TP...  25.3 us
    all_to_all x1, blocking collectives, body(): lax.all_to_all(jnp.broadcast_to(along_z[None], (y_count,) + along_z.shape...  23.5 us
    all_to_all x1, blocking collectives, body(): lax.all_to_all(jnp.broadcast_to(attention[None], (z_count,) + attention.s...  15.4 us
    unnamed x15, local copies, waits for them, and re-layouts  14.5 us
    all_to_all x1, blocking collectives, body(): lax.all_to_all(jnp.broadcast_to(reduced[None], (group_size,) + reduced.sh...  12.8 us
    all_to_all x1, starting transfers between devices, body(): lax.all_to_all(spread, DP, 0, 0, tiled=True)  10.9 us
    slice x1, local copies, waits for them, and re-layouts, body(): values = key_value_cache[:, :, 1, 0, :]  10.1 us
  transfers between devices with their start and end apart: 6, of which 3 were waited for; matrix products, arithmetic and copies ran while one was open for 16% of the time, Pallas kernels for 0%

profile of v14, /device:TPU:1, one launch (start us, length us, event | category | flops | bytes accessed | tf_op | source)
XLA Modules:
  0.0 215.2 jit_solution(7475034618431883574)
XLA Ops:
  0.0 1.1 fusion.38
  1.2 1.0 fusion.39
  2.2 0.2 broadcast_select_fusion.1
  2.4 2.5 %collective-permute-start.1 = (bf16[256,640]{1,0:T(8,128)(2,1)S(1)}, bf16[256,640]{1,0:T(8,128)(2,1)S(1)}, u32[]{:S(2)}, u32[]{:S(2)}) collective-permute-start(bf16[256,640]{1,0:T(8,128)(2,1)S(1)} %get-tuple-element.24), channel_id=1, source_target_pairs={{0,8},{8,0},{16,24},{24,16},{32,40},{40,32},{48,56},{56,48},{64,72... | collective-permute-start | bytes 983048 | tf_op jit(solution)/shard_map/ppermute | solution.py:147
  5.0 0.1 collective-permute-start
  5.1 1.1 broadcast_in_dim.191
  6.2 10.9 %all-to-all-start = ((bf16[32,32,512]{2,1,0:T(8,128)(2,1)}), bf16[32,32,512]{2,1,0:T(8,128)(2,1)S(1)}, u32[]{:S(2)}, u32[]{:S(2)}) async-start(bf16[32,32,512]{2,1,0:T(8,128)(2,1)} %bitcast.3), calls=%async_computation | async-start | bytes 2097152 | tf_op jit(solution)/shard_map/all_to_all | solution.py:160
  17.3 0.8 convert_reduce_fusion.1
  18.2 0.1 fusion.11
  18.4 10.1 %fusion.37 = (bf16[32,256,1,1,128]{4,2,3,1,0:T(2,128)(2,1)}, bf16[32,256,1,1,128]{4,2,3,1,0:T(2,128)(2,1)}) fusion(bf16[32,256,2,1,128]{4,2,3,1,0:T(2,128)(2,1)} %param.18), kind=kLoop, calls=%fused_computation.140 | loop fusion | bytes 8388608 | tf_op jit(solution)/shard_map/slice | solution.py:191
  28.5 9.8 %copy.137 = bf16[32,256,1,1,128]{1,4,0,3,2:T(8,128)(2,1)} copy(bf16[32,256,1,1,128]{4,2,3,1,0:T(2,128)(2,1)} %get-tuple-element.22) | data formatting | bytes 4194304
  38.7 0.1 select_reduce_fusion
  38.8 0.1 copy.121
  39.0 0.6 convert_reduce_fusion.3
  39.6 0.1 fusion.12
  39.7 0.2 convert_reduce_fusion.2
  40.0 0.8 fusion.14
  40.8 0.6 iota_reduce_fusion
  41.4 3.9 %copy.143 = bf16[32,256,1,1,128]{4,1,0,3,2:T(8,128)(2,1)} copy(bf16[32,256,1,1,128]{4,2,3,1,0:T(2,128)(2,1)} %get-tuple-element.21) | data formatting | bytes 4194304
  45.3 0.1 broadcast_in_dim.189
  45.4 0.1 broadcast_in_dim.187
  45.5 0.7 gather_fusion.1
  46.2 0.7 gather_fusion
  46.9 0.1 sub.48
  47.0 0.1 sub.51
  47.2 2.1 convolution_convert_fusion
  49.3 9.2 %all-to-all-start.1 = ((bf16[32,32,640]{2,1,0:T(8,128)(2,1)}), bf16[32,32,640]{2,1,0:T(8,128)(2,1)S(1)}, u32[]{:S(2)}, u32[]{:S(2)}) async-start(bf16[32,32,640]{2,1,0:T(8,128)(2,1)} %bitcast.91), calls=%async_computation.1 | async-start | bytes 2621440 | tf_op jit(solution)/shard_map/all_to_all | solution.py:168
  58.6 0.1 select_reduce_fusion.1
  58.7 0.1 copy.132
  58.8 0.8 gather_fusion.6
  59.6 0.8 gather_fusion.7
  60.3 0.1 gt.42
  60.5 0.1 fusion.13
  60.6 0.2 multiply_reduce_fusion
  60.9 0.6 broadcast_select_fusion.6
  61.5 0.6 broadcast_select_fusion.7.parent_ref
  62.0 0.1 multiply_cosine_fusion.1
  62.2 27.3 %all-to-all-done.1 = bf16[32,32,640]{2,1,0:T(8,128)(2,1)S(1)} async-done(((bf16[32,32,640]{2,1,0:T(8,128)(2,1)}), bf16[32,32,640]{2,1,0:T(8,128)(2,1)S(1)}, u32[]{:S(2)}, u32[]{:S(2)}) %all-to-all-start.1) | async-done | bytes 1310752 | tf_op jit(solution)/shard_map/all_to_all | solution.py:168
  89.5 0.2 convert_reduce_fusion
  90.0 0.1 fusion.21
  90.3 0.1 subtract_convert_fusion
  90.5 0.6 gather_fusion.2
  91.2 0.3 broadcast_select_fusion.3
  91.5 0.8 copy.130
  92.3 7.6 %all-to-all-start.2 = ((bf16[32,2,10,128]{3,1,2,0:T(2,128)(2,1)}), bf16[32,2,10,128]{3,1,2,0:T(2,128)(2,1)S(1)}, u32[]{:S(2)}, u32[]{:S(2)}) async-start(bf16[32,2,10,128]{3,1,2,0:T(2,128)(2,1)} %copy.130), calls=%async_computation.2 | async-start | bytes 327680 | tf_op jit(solution)/shard_map/all_to_all | solution.py:226
  100.0 9.2 %all-to-all-done.2 = bf16[32,2,10,128]{3,1,2,0:T(2,128)(2,1)S(1)} async-done(((bf16[32,2,10,128]{3,1,2,0:T(2,128)(2,1)}), bf16[32,2,10,128]{3,1,2,0:T(2,128)(2,1)S(1)}, u32[]{:S(2)}, u32[]{:S(2)}) %all-to-all-start.2) | async-done | bytes 163872 | tf_op jit(solution)/shard_map/all_to_all | solution.py:226
  109.2 0.1 copy.131
  109.3 0.1 copy.135
  109.5 0.6 gather_fusion.3
  110.1 0.8 broadcast_select_fusion.4.packed_ref
  111.0 8.2 %shard_map.100 = bf16[64,8,128]{2,1,0:T(8,128)(2,1)} custom-call(s32[64]{0:T(128)} %broadcast_select_fusion.7.parent_ref, s32[64]{0:T(128)} %get-tuple-element.19.length_ref, bf16[64,10,128]{2,1,0:T(8,128)(2,1)} %broadcast_select_fusion.4.packed_ref, bf16[32,128,256]{2,1,0:T(8,128)(2,1)} %bitcast.53, bf16[32,128,256]{2,1,0:T(8,128)(2,1)} %bitcast.54, ...), custom_call_target="tpu_custom_call" | custom-call | tf_op jit(solution)/shard_map/pallas_call | solution.py:103
  119.1 1.5 gather_fusion.4
  120.7 0.9 broadcast_select_fusion.5
  121.6 4.7 %all-to-all-start.3 = ((bf16[32,2,1024]{2,1,0:T(2,128)(2,1)}), bf16[32,2,1024]{2,1,0:T(2,128)(2,1)S(1)}, u32[]{:S(2)}, u32[]{:S(2)}) async-start(bf16[32,2,1024]{2,1,0:T(2,128)(2,1)} %broadcast_select_fusion.5), calls=%async_computation.3 | async-start | bytes 262144 | tf_op jit(solution)/shard_map/all_to_all | solution.py:258
  126.3 0.8 dynamic-slice_compare_fusion
  127.1 8.4 %all-to-all-done.3 = bf16[32,2,1024]{2,1,0:T(2,128)(2,1)S(1)} async-done(((bf16[32,2,1024]{2,1,0:T(2,128)(2,1)}), bf16[32,2,1024]{2,1,0:T(2,128)(2,1)S(1)}, u32[]{:S(2)}, u32[]{:S(2)}) %all-to-all-start.3) | async-done | bytes 131104 | tf_op jit(solution)/shard_map/all_to_all | solution.py:258
  135.5 0.6 gather_fusion.5
  136.3 15.4 %all_to_all.40 = bf16[8,32,1024]{2,1,0:T(8,128)(2,1)S(1)} all-to-all(bf16[8,32,1024]{2,1,0:T(8,128)(2,1)S(1)} %broadcast_in_dim.202), channel_id=1, replica_groups=mesh['dy'=4,'dz'=8,'tx'=4,'tc'=2] {'dz'}, dimensions={0} | all-to-all | bytes 1048576 | tf_op jit(solution)/shard_map/all_to_all | solution.py:266
  151.7 0.3 broadcast_in_dim.204
  152.0 23.5 %all_to_all.41 = bf16[4,256,1024]{2,1,0:T(8,128)(2,1)S(1)} all-to-all(bf16[4,256,1024]{2,1,0:T(8,128)(2,1)S(1)} %broadcast_in_dim.204), channel_id=1, replica_groups=mesh['dy'=4,'dz'=8,'tx'=4,'tc'=2] {'dy'}, dimensions={0} | all-to-all | bytes 4194304 | tf_op jit(solution)/shard_map/all_to_all | solution.py:269
  175.4 0.7 fusion.9
  176.2 25.3 %all_to_all.42 = f32[8,128,256]{2,1,0:T(8,128)S(1)} all-to-all(f32[8,128,256]{2,1,0:T(8,128)S(1)} %fusion.9), channel_id=1, replica_groups=mesh['dy'=4,'dz'=8,'tx'=4,'tc'=2] {'tx','tc'}, dimensions={0} | all-to-all | bytes 2097152 | tf_op jit(solution)/shard_map/all_to_all | solution.py:279
  201.6 12.8 %all_to_all.43 = bf16[8,128,256]{2,1,0:T(8,128)(2,1)S(1)} all-to-all(bf16[8,128,256]{2,1,0:T(8,128)(2,1)S(1)} %broadcast_in_dim.205), channel_id=1, replica_groups=mesh['dy'=4,'dz'=8,'tx'=4,'tc'=2] {'tx','tc'}, dimensions={0} | all-to-all | bytes 1048576 | tf_op jit(solution)/shard_map/all_to_all | solution.py:282
  214.4 0.8 copy.146
  (67 shorter events, 1.9 us)
Async XLA Ops:
  0.0 175.4 %copy-start = (bf16[1024,256]{1,0:T(8,128)(2,1)S(1)}, bf16[1024,256]{1,0:T(8,128)(2,1)}, u32[]{:S(2)}) copy-start(bf16[1024,256]{1,0:T(8,128)(2,1)} %param.17) | copy-start | bytes 1572868
  0.0 4.9 %copy-start.4 = (bf16[256]{0:T(256)(128)(2,1)S(1)}, bf16[256]{0:T(256)(128)(2,1)}, u32[]{:S(2)}) copy-start(bf16[256]{0:T(256)(128)(2,1)} %param.13) | copy-start | bytes 1540
  0.0 5.1 %copy-start.2 = (bf16[32,8192]{1,0:T(8,128)(2,1)S(1)}, bf16[32,8192]{1,0:T(8,128)(2,1)}, u32[]{:S(2)}) copy-start(bf16[32,8192]{1,0:T(8,128)(2,1)} %param.12) | copy-start | bytes 1572868
  2.4 44.8 %collective-permute-start.1 = (bf16[256,640]{1,0:T(8,128)(2,1)S(1)}, bf16[256,640]{1,0:T(8,128)(2,1)S(1)}, u32[]{:S(2)}, u32[]{:S(2)}) collective-permute-start(bf16[256,640]{1,0:T(8,128)(2,1)S(1)} %get-tuple-element.24), channel_id=1, source_target_pairs={{0,8},{8,0},{16,24},{24,16},{32,40},{40,32},{48,56},{56,48},{64,72... | collective-permute-start | bytes 983048 | tf_op jit(solution)/shard_map/ppermute | solution.py:147
  5.0 42.2 %collective-permute-start = (bf16[256]{0:T(256)(128)(2,1)S(1)}, bf16[256]{0:T(256)(128)(2,1)S(1)}, u32[]{:S(2)}, u32[]{:S(2)}) collective-permute-start(bf16[256]{0:T(256)(128)(2,1)S(1)} %copy-done.4), channel_id=1, source_target_pairs={{0,8},{8,0},{16,24},{24,16},{32,40},{40,32},{48,56},{56,48},{64,72... | collective-permute-start | bytes 1544 | tf_op jit(solution)/shard_map/ppermute | solution.py:148
  5.1 12.1 %copy-start.3 = (s32[1024]{0:T(1024)S(1)}, s32[1024]{0:T(1024)}, u32[]{:S(2)}) copy-start(s32[1024]{0:T(1024)} %param.20) | copy-start | bytes 12292
  6.2 41.0 %all-to-all-start = ((bf16[32,32,512]{2,1,0:T(8,128)(2,1)}), bf16[32,32,512]{2,1,0:T(8,128)(2,1)S(1)}, u32[]{:S(2)}, u32[]{:S(2)}) async-start(bf16[32,32,512]{2,1,0:T(8,128)(2,1)} %bitcast.3), calls=%async_computation | async-start | bytes 2097152 | tf_op jit(solution)/shard_map/all_to_all | solution.py:160
  41.4 4.1 %copy-start.1 = (s32[1024]{0:T(1024)S(1)}, s32[1024]{0:T(1024)}, u32[]{:S(2)}) copy-start(s32[1024]{0:T(1024)} %param.19) | copy-start | bytes 12292
  49.3 40.2 %all-to-all-start.1 = ((bf16[32,32,640]{2,1,0:T(8,128)(2,1)}), bf16[32,32,640]{2,1,0:T(8,128)(2,1)S(1)}, u32[]{:S(2)}, u32[]{:S(2)}) async-start(bf16[32,32,640]{2,1,0:T(8,128)(2,1)} %bitcast.91), calls=%async_computation.1 | async-start | bytes 2621440 | tf_op jit(solution)/shard_map/all_to_all | solution.py:168
  92.3 16.9 %all-to-all-start.2 = ((bf16[32,2,10,128]{3,1,2,0:T(2,128)(2,1)}), bf16[32,2,10,128]{3,1,2,0:T(2,128)(2,1)S(1)}, u32[]{:S(2)}, u32[]{:S(2)}) async-start(bf16[32,2,10,128]{3,1,2,0:T(2,128)(2,1)} %copy.130), calls=%async_computation.2 | async-start | bytes 327680 | tf_op jit(solution)/shard_map/all_to_all | solution.py:226
  121.6 13.9 %all-to-all-start.3 = ((bf16[32,2,1024]{2,1,0:T(2,128)(2,1)}), bf16[32,2,1024]{2,1,0:T(2,128)(2,1)S(1)}, u32[]{:S(2)}, u32[]{:S(2)}) async-start(bf16[32,2,1024]{2,1,0:T(2,128)(2,1)} %broadcast_select_fusion.5), calls=%async_computation.3 | async-start | bytes 262144 | tf_op jit(solution)/shard_map/all_to_all | solution.py:258
